TPU v7x, 32 devices: a whole 2x2x4 slice. The times are simulated.
32 devices in a mesh: user: 8 (over z, y), item: 4 (over x, core).
Axes of the slice: x: 2, y: 2, z: 4, core: 2. Of those that a mesh axis runs over, the one named last changes fastest.
Arguments:
- theta_shape: float32 [16384, 1024], P('user', 'item'), may hold values from 0.3 to 3
- theta_rate: float32 [16384, 1024], P('user', 'item'), may hold values from 100 to 1000
- xi_rate: float32 [16384], P('user'), may hold values from 1 to 10
- beta_shape: float32 [4096, 1024], P('item', 'user'), may hold values from 0.3 to 3
- beta_rate: float32 [4096, 1024], P('item', 'user'), may hold values from 50 to 500
- eta_rate: float32 [4096], P('item'), may hold values from 1 to 10
- tile_slots: int32 [8, 4, 32], P('user', 'item'), may hold values from 0 to 31, as said below
- tile_counts: bfloat16 [8, 4, 32, 256, 256], P('user', 'item'), may hold values from 0 to 5, as said below
- live_tiles: int32 [8, 4], P('user', 'item'), may hold values from 1 to 32, as said below
Outputs:
- theta_shape_new: float32 [16384, 1024], P('user', 'item')
- theta_log_rate: float32 [16384, 1024], P('user', 'item')
- xi_rate_new: float32 [16384], P('user')
- beta_shape_new: float32 [4096, 1024], P('item', 'user')
- beta_log_rate: float32 [4096, 1024], P('item', 'user')
- eta_rate_new: float32 [4096], P('item')
Inputs may be any that keep to these rules, and one draw needn't show every extreme that they name: `tile_slots`: within one device's 32 slots the positions are distinct. `tile_counts`: whole numbers. `live_tiles`: some device uses all 32 slots.
All inputs are finite; a program needn't handle non-finite values.
Results may differ from a plain program's by a relative error of at most 0.0029.
Values may be sent and summed in bfloat16 or wider, within the bound.
No kernel may reach another device: no remote copies, remote signals or barrier semaphores. Data moves between devices by JAX's collectives and lax.ppermute only.
A program may use at most 128 MiB of HBM per device.

v0:
```python
import math

import jax
import jax.numpy as jnp
from jax import lax
from jax.sharding import PartitionSpec as P

BLK = 256
UB = 8
IB = 4
TMAX = 32


prior_a = 0.3
prior_a2 = 0.3
prior_b2 = 1.0
prior_c = 0.3
prior_c2 = 0.3
prior_d2 = 1.0


def exp_mean_log(shape_param, rate_param):
    return jnp.exp(lax.digamma(shape_param) - jnp.log(rate_param)).astype(jnp.bfloat16)


def on_device(
    theta_shape,
    theta_rate,
    xi_rate,
    beta_shape,
    beta_rate,
    eta_rate,
    tile_slots,
    tile_counts,
    live_tiles,
):
    user_width = lax.axis_size("user")
    item_width = lax.axis_size("item")
    user_index = lax.axis_index("user")
    item_index = lax.axis_index("item")
    theta_part = exp_mean_log(theta_shape, theta_rate)
    beta_part = exp_mean_log(beta_shape, beta_rate)
    theta_full = lax.all_gather(theta_part, "item", axis=1, tiled=True)
    beta_full = lax.all_gather(beta_part, "user", axis=1, tiled=True)
    factors = theta_full.shape[1]
    user_rows = theta_full.shape[0]
    item_rows = beta_full.shape[0]
    theta_blocks = theta_full.reshape(UB, BLK, factors)
    beta_blocks = beta_full.reshape(IB, BLK, factors)
    slot_list = tile_slots.reshape(TMAX)
    count_tiles = tile_counts.reshape(TMAX, BLK, BLK)
    used_slots = live_tiles.reshape(())
    user_blocks = slot_list // IB
    item_blocks = slot_list % IB
    group_size = math.gcd(TMAX, 8)

    def group_step(group_index, carried):
        user_acc, item_acc = carried
        first_slot = group_index * group_size
        rows_user = lax.dynamic_slice_in_dim(user_blocks, first_slot, group_size, 0)
        rows_item = lax.dynamic_slice_in_dim(item_blocks, first_slot, group_size, 0)
        counts = lax.dynamic_slice_in_dim(count_tiles, first_slot, group_size, 0).astype(
            jnp.float32
        )
        slot_mask = (first_slot + jnp.arange(group_size) < used_slots).astype(jnp.float32)
        counts = counts * slot_mask[:, None, None]
        users = jnp.take(theta_blocks, rows_user, axis=0)
        items = jnp.take(beta_blocks, rows_item, axis=0)
        denominator = jnp.einsum("tuk,tik->tui", users, items, preferred_element_type=jnp.float32)
        ratio_tile = (counts / denominator).astype(jnp.bfloat16)
        user_terms = jnp.einsum(
            "tui,tik->tuk", ratio_tile, items, preferred_element_type=jnp.float32
        )
        item_terms = jnp.einsum(
            "tui,tuk->tik", ratio_tile, users, preferred_element_type=jnp.float32
        )
        user_acc = user_acc.at[rows_user].add(user_terms)
        item_acc = item_acc.at[rows_item].add(item_terms)
        return (user_acc, item_acc)

    start_acc = (
        jnp.zeros((UB, BLK, factors), jnp.float32),
        jnp.zeros((IB, BLK, factors), jnp.float32),
    )
    group_count = TMAX // group_size
    user_acc, item_acc = lax.fori_loop(0, group_count, group_step, start_acc)
    user_acc = user_acc.reshape(user_rows, factors)
    item_acc = item_acc.reshape(item_rows, factors)
    beta_columns = factors // user_width
    theta_columns = factors // item_width
    beta_local = jnp.sum(beta_shape / beta_rate, axis=0)
    theta_local = jnp.sum(theta_shape / theta_rate, axis=0)
    beta_placed = lax.dynamic_update_slice_in_dim(
        jnp.zeros((factors,), jnp.float32), beta_local, user_index * beta_columns, 0
    )
    theta_placed = lax.dynamic_update_slice_in_dim(
        jnp.zeros((factors,), jnp.float32), theta_local, item_index * theta_columns, 0
    )
    beta_total, theta_total = lax.psum((beta_placed, theta_placed), ("user", "item"))
    xi_mean = (prior_a2 + factors * prior_a) / xi_rate
    user_summed = lax.psum(user_acc, "item")
    shape_whole = prior_a + theta_full.astype(jnp.float32) * user_summed
    rate_whole = xi_mean[:, None] + beta_total[None, :]
    xi_rate_new = prior_a2 / prior_b2 + jnp.sum(shape_whole / rate_whole, axis=1)
    theta_shape_new = lax.dynamic_slice_in_dim(
        shape_whole, item_index * theta_columns, theta_columns, 1
    )
    theta_rate_new = lax.dynamic_slice_in_dim(
        rate_whole, item_index * theta_columns, theta_columns, 1
    )
    item_share = lax.psum_scatter(item_acc, "user", scatter_dimension=1, tiled=True)
    beta_shape_new = prior_c + beta_part.astype(jnp.float32) * item_share
    eta_mean = (prior_c2 + factors * prior_c) / eta_rate
    theta_slice = lax.dynamic_slice_in_dim(theta_total, user_index * beta_columns, beta_columns, 0)
    beta_rate_new = eta_mean[:, None] + theta_slice[None, :]
    item_part = jnp.sum(beta_shape_new / beta_rate_new, axis=1)
    eta_rate_new = prior_c2 / prior_d2 + lax.psum(item_part, "user")
    return (
        theta_shape_new,
        jnp.log(theta_rate_new),
        xi_rate_new,
        beta_shape_new,
        jnp.log(beta_rate_new),
        eta_rate_new,
    )


def solution(mesh):
    in_specs = (
        P("user", "item"),
        P("user", "item"),
        P("user"),
        P("item", "user"),
        P("item", "user"),
        P("item"),
        P("user", "item", None),
        P("user", "item", None, None, None),
        P("user", "item"),
    )
    out_specs = (
        P("user", "item"),
        P("user", "item"),
        P("user"),
        P("item", "user"),
        P("item", "user"),
        P("item"),
    )
    return jax.shard_map(
        on_device, mesh=mesh, in_specs=in_specs, out_specs=out_specs, check_vma=False
    )
```

profile of v0, /device:TPU:0, one launch (start us, length us, event | category | flops | bytes accessed | tf_op | source)
XLA Modules:
  0.0 631.7 jit_solution(3128361467981943288)
XLA Ops:
  7.2 0.0 all-gather.5.cloned.1.call-start
  7.2 6.0 fusion.22
  13.2 0.0 all-gather.5.cloned.1.call-update
  13.2 0.0 all-gather.3.cloned.1.call-start
  13.3 17.6 %fusion.16 = (bf16[2048,256]{1,0:T(8,128)(2,1)}, f32[256]{0:T(256)}) fusion(f32[2048,256]{1,0:T(8,128)} %param.12, f32[2048,256]{1,0:T(8,128)} %param.11), kind=kLoop, calls=%fused_computation.36 | loop fusion | flops 41418496 | bytes 5243904 | tf_op jit(solution)/shard_map/convert_element_type | solution.py:23
  30.8 0.0 all-gather.3.cloned.1.call-update
  30.9 0.0 all-reduce.3.cloned.1.call-start
  30.9 35.5 %all-gather.5.cloned.1.call-done = bf16[1024,1024]{1,0:T(8,128)(2,1)} async-done(((bf16[1024,128]{1,0:T(8,128)(2,1)}), bf16[1024,1024]{1,0:T(8,128)(2,1)}) %all-gather.5.cloned.1.call-update) | async-done | bytes 2097168 | tf_op jit(solution)/shard_map/all_gather | solution.py:44
  66.4 35.3 %all-gather.3.cloned.1.call-done = bf16[2048,1024]{1,0:T(8,128)(2,1)} async-done(((bf16[2048,256]{1,0:T(8,128)(2,1)}), bf16[2048,1024]{1,0:T(8,128)(2,1)}) %all-gather.3.cloned.1.call-update) | async-done | bytes 4194320 | tf_op jit(solution)/shard_map/all_gather | solution.py:43
  101.7 4.3 broadcast_in_dim.57
  106.0 2.5 broadcast_in_dim.58
  108.5 246.8 %while.15 = (s32[]{:T(128)}, f32[8,256,1024]{2,1,0:T(8,128)}, f32[4,256,1024]{2,1,0:T(8,128)}, s32[32]{0:T(128)S(1)}, bf16[32,256,256]{2,1,0:T(8,128)(2,1)}, /*i...) while((s32[]{:T(128)}, f32[8,256,1024]{2,1,0:T(8,128)}, ...), condition=%wide.region_3.4_spmd, body=%wide.region_0.3_spmd.sunk | while | flops 3238004736 | bytes 134226640 | solution.py:86
  108.5 0.1 compare_and_fusion.3
  108.6 5.0 gather_fusion
  113.6 2.8 gather_fusion.1
  116.4 5.0 fusion.28
  121.4 0.7 compare_convert_fusion.2
  122.1 6.0 fusion.30
  128.1 17.3 %scatter_fusion.1 = f32[4,256,1024]{2,1,0:T(8,128)} fusion(f32[4,256,1024]{2,1,0:T(8,128)} %get-tuple-element.281, s32[8]{0:T(128)S(1)} %get-tuple-element.264, f32[8,256,1024]{2,1,0:T(8,128)} %fusion.30), kind=kCustom, calls=%fused_computation.3.clone.1 | custom fusion | flops 2097152 | bytes 25165856 | tf_op jit(solution)/shard_map/while/body/eval_jaxpr/scatter-add | solution.py:78
  145.4 7.7 %fusion.29 = f32[8,256,1024]{2,1,0:T(8,128)} fusion(f32[8,256,256]{2,1,0:T(8,128)} %copy-done.8, bf16[8,256,1024]{2,1,0:T(8,128)(2,1)} %gather_fusion.1, pred[8]{0:T(512)(128)(4,1)S(1)} %get-tuple-element.265, f32[8]{0:T(128)S(1)} %compare_convert_fusion.2, bf16[32,256,256]{2,1,0:T(8,128)(2,1)} %get-tuple-element.296, s32[]{:T(128)S(6)} %select_n.90), kind=kOutput, calls=%fused_computation.8.clone.1 | convolution fusion | flops 1077936128 | bytes 15728684 | tf_op jit(solution)/shard_map/while/body/eval_jaxpr/tui,tik->tuk/dot_general | solution.py:71
  153.1 17.1 %scatter_fusion = f32[8,256,1024]{2,1,0:T(8,128)} fusion(f32[8,256,1024]{2,1,0:T(8,128)} %get-tuple-element.280, s32[8]{0:T(128)S(1)} %get-tuple-element.262, f32[8,256,1024]{2,1,0:T(8,128)} %fusion.29), kind=kCustom, calls=%fused_computation.2.clone.1 | custom fusion | flops 2097152 | bytes 25165856 | tf_op jit(solution)/shard_map/while/body/eval_jaxpr/scatter-add | solution.py:77
  170.2 0.1 compare_and_fusion.3
  170.3 5.0 gather_fusion
  175.2 2.8 gather_fusion.1
  178.0 5.0 fusion.28
  183.1 0.7 compare_convert_fusion.2
  183.8 6.0 fusion.30
  189.8 17.5 %scatter_fusion.1 = f32[4,256,1024]{2,1,0:T(8,128)} fusion(f32[4,256,1024]{2,1,0:T(8,128)} %get-tuple-element.281, s32[8]{0:T(128)S(1)} %get-tuple-element.264, f32[8,256,1024]{2,1,0:T(8,128)} %fusion.30), kind=kCustom, calls=%fused_computation.3.clone.1 | custom fusion | flops 2097152 | bytes 25165856 | tf_op jit(solution)/shard_map/while/body/eval_jaxpr/scatter-add | solution.py:78
  207.3 7.7 %fusion.29 = f32[8,256,1024]{2,1,0:T(8,128)} fusion(f32[8,256,256]{2,1,0:T(8,128)} %copy-done.8, bf16[8,256,1024]{2,1,0:T(8,128)(2,1)} %gather_fusion.1, pred[8]{0:T(512)(128)(4,1)S(1)} %get-tuple-element.265, f32[8]{0:T(128)S(1)} %compare_convert_fusion.2, bf16[32,256,256]{2,1,0:T(8,128)(2,1)} %get-tuple-element.296, s32[]{:T(128)S(6)} %select_n.90), kind=kOutput, calls=%fused_computation.8.clone.1 | convolution fusion | flops 1077936128 | bytes 15728684 | tf_op jit(solution)/shard_map/while/body/eval_jaxpr/tui,tik->tuk/dot_general | solution.py:71
  215.0 17.4 %scatter_fusion = f32[8,256,1024]{2,1,0:T(8,128)} fusion(f32[8,256,1024]{2,1,0:T(8,128)} %get-tuple-element.280, s32[8]{0:T(128)S(1)} %get-tuple-element.262, f32[8,256,1024]{2,1,0:T(8,128)} %fusion.29), kind=kCustom, calls=%fused_computation.2.clone.1 | custom fusion | flops 2097152 | bytes 25165856 | tf_op jit(solution)/shard_map/while/body/eval_jaxpr/scatter-add | solution.py:77
  232.4 0.1 compare_and_fusion.3
  232.5 5.0 gather_fusion
  237.5 2.8 gather_fusion.1
  240.2 5.0 fusion.28
  245.3 0.7 compare_convert_fusion.2
  246.0 6.0 fusion.30
  252.0 17.1 %scatter_fusion.1 = f32[4,256,1024]{2,1,0:T(8,128)} fusion(f32[4,256,1024]{2,1,0:T(8,128)} %get-tuple-element.281, s32[8]{0:T(128)S(1)} %get-tuple-element.264, f32[8,256,1024]{2,1,0:T(8,128)} %fusion.30), kind=kCustom, calls=%fused_computation.3.clone.1 | custom fusion | flops 2097152 | bytes 25165856 | tf_op jit(solution)/shard_map/while/body/eval_jaxpr/scatter-add | solution.py:78
  269.1 7.7 %fusion.29 = f32[8,256,1024]{2,1,0:T(8,128)} fusion(f32[8,256,256]{2,1,0:T(8,128)} %copy-done.8, bf16[8,256,1024]{2,1,0:T(8,128)(2,1)} %gather_fusion.1, pred[8]{0:T(512)(128)(4,1)S(1)} %get-tuple-element.265, f32[8]{0:T(128)S(1)} %compare_convert_fusion.2, bf16[32,256,256]{2,1,0:T(8,128)(2,1)} %get-tuple-element.296, s32[]{:T(128)S(6)} %select_n.90), kind=kOutput, calls=%fused_computation.8.clone.1 | convolution fusion | flops 1077936128 | bytes 15728684 | tf_op jit(solution)/shard_map/while/body/eval_jaxpr/tui,tik->tuk/dot_general | solution.py:71
  276.8 17.1 %scatter_fusion = f32[8,256,1024]{2,1,0:T(8,128)} fusion(f32[8,256,1024]{2,1,0:T(8,128)} %get-tuple-element.280, s32[8]{0:T(128)S(1)} %get-tuple-element.262, f32[8,256,1024]{2,1,0:T(8,128)} %fusion.29), kind=kCustom, calls=%fused_computation.2.clone.1 | custom fusion | flops 2097152 | bytes 25165856 | tf_op jit(solution)/shard_map/while/body/eval_jaxpr/scatter-add | solution.py:77
  293.9 0.1 compare_and_fusion.3
  294.0 5.0 gather_fusion
  299.0 2.8 gather_fusion.1
  301.7 5.0 fusion.28
  306.8 0.7 compare_convert_fusion.2
  307.5 6.0 fusion.30
  313.5 16.8 %scatter_fusion.1 = f32[4,256,1024]{2,1,0:T(8,128)} fusion(f32[4,256,1024]{2,1,0:T(8,128)} %get-tuple-element.281, s32[8]{0:T(128)S(1)} %get-tuple-element.264, f32[8,256,1024]{2,1,0:T(8,128)} %fusion.30), kind=kCustom, calls=%fused_computation.3.clone.1 | custom fusion | flops 2097152 | bytes 25165856 | tf_op jit(solution)/shard_map/while/body/eval_jaxpr/scatter-add | solution.py:78
  330.2 7.7 %fusion.29 = f32[8,256,1024]{2,1,0:T(8,128)} fusion(f32[8,256,256]{2,1,0:T(8,128)} %copy-done.8, bf16[8,256,1024]{2,1,0:T(8,128)(2,1)} %gather_fusion.1, pred[8]{0:T(512)(128)(4,1)S(1)} %get-tuple-element.265, f32[8]{0:T(128)S(1)} %compare_convert_fusion.2, bf16[32,256,256]{2,1,0:T(8,128)(2,1)} %get-tuple-element.296, s32[]{:T(128)S(6)} %select_n.90), kind=kOutput, calls=%fused_computation.8.clone.1 | convolution fusion | flops 1077936128 | bytes 15728684 | tf_op jit(solution)/shard_map/while/body/eval_jaxpr/tui,tik->tuk/dot_general | solution.py:71
  337.9 17.4 %scatter_fusion = f32[8,256,1024]{2,1,0:T(8,128)} fusion(f32[8,256,1024]{2,1,0:T(8,128)} %get-tuple-element.280, s32[8]{0:T(128)S(1)} %get-tuple-element.262, f32[8,256,1024]{2,1,0:T(8,128)} %fusion.29), kind=kCustom, calls=%fused_computation.2.clone.1 | custom fusion | flops 2097152 | bytes 25165856 | tf_op jit(solution)/shard_map/while/body/eval_jaxpr/scatter-add | solution.py:77
  355.3 0.0 all-reduce.3.cloned.1.call-update
  355.3 0.0 reduce-scatter.2.cloned.1.call-start
  355.4 0.5 reduce-scatter.2.cloned.1.call-update
  355.9 0.1 copy-done.5
  356.1 0.2 dynamic_update_slice.7
  356.3 0.2 dynamic_update_slice.6
  356.5 40.8 %all-reduce = (f32[1024]{0:T(1024)S(1)}, f32[1024]{0:T(1024)S(1)}) all-reduce(f32[1024]{0:T(1024)S(1)} %dynamic_update_slice.6, f32[1024]{0:T(1024)S(1)} %dynamic_update_slice.7), channel_id=1, replica_groups=mesh['user'=8,'item'=4] {'user','item'}, use_global_device_ids=true, to_apply=%region_6.7 | all-reduce | flops 2048 | bytes 16384 | tf_op jit(solution)/shard_map/psum | solution.py:99
  397.3 0.1 dynamic_slice.32
  397.4 112.6 %all-reduce.3.cloned.1.call-done = f32[2048,1024]{1,0:T(8,128)} async-done(((f32[2048,1024]{1,0:T(8,128)}), f32[2048,1024]{1,0:T(8,128)}) %all-reduce.3.cloned.1.call-update) | async-done | bytes 8388624 | tf_op jit(solution)/shard_map/psum | solution.py:101
  510.0 6.0 divide_reduce_fusion
  516.0 0.6 broadcast_add_fusion.1
  516.6 2.5 dynamic-slice_log_fusion
  519.1 83.2 %reduce-scatter.2.cloned.1.call-done = f32[1024,128]{1,0:T(8,128)} async-done(((f32[1024,1024]{1,0:T(8,128)}), f32[1024,128]{1,0:T(8,128)}) %reduce-scatter.2.cloned.1.call-update) | async-done | bytes 524304 | tf_op jit(solution)/shard_map/reduce_scatter | solution.py:111
  602.3 2.2 fusion.23
  604.5 20.1 %psum.31 = f32[1024]{0:T(1024)S(1)} all-reduce(f32[1024]{0:T(1024)S(1)} %get-tuple-element.187), channel_id=1, replica_groups=mesh['user'=8,'item'=4] {'user'}, use_global_device_ids=true, to_apply=%region_12.13 | all-reduce | flops 1024 | bytes 8192 | tf_op jit(solution)/shard_map/psum | solution.py:117
  624.6 0.6 broadcast_add_fusion.2
  (42 shorter events, 0.1 us)
Async XLA Ops:
  7.2 59.2 %all-gather.5.cloned.1.call-start = ((), (), s32[]{:S(2)}) async-start(), calls=%async_computation.2 | async-start | bytes 2359296 | tf_op jit(solution)/shard_map/all_gather | solution.py:44
  13.2 17.7 %copy-start.7 = (s32[1,1,32]{2,1,0:T(1,128)S(1)}, s32[1,1,32]{2,1,0:T(1,128)}, u32[]{:S(2)}) copy-start(s32[1,1,32]{2,1,0:T(1,128)} %param.17) | copy-start | bytes 388
  13.2 88.5 %all-gather.3.cloned.1.call-start = ((), (), s32[]{:S(2)}) async-start(), calls=%async_computation.1 | async-start | bytes 5242880 | tf_op jit(solution)/shard_map/all_gather | solution.py:43
  30.9 479.1 %all-reduce.3.cloned.1.call-start = ((), (), s32[]{:S(2)}) async-start(), calls=%async_computation.3 | async-start | bytes 16777216 | tf_op jit(solution)/shard_map/psum | solution.py:101
  106.0 2.5 copy-start
  116.4 5.8 copy-start.1
  121.4 6.7 %copy-start.8 = (f32[8,256,256]{2,1,0:T(8,128)}, f32[8,256,256]{2,1,0:T(8,128)S(1)}, u32[]{:S(2)}) copy-start(f32[8,256,256]{2,1,0:T(8,128)S(1)} %fusion.28) | copy-start | bytes 6291460 | tf_op jit(solution)/shard_map/while
  178.0 5.8 copy-start.1
  183.1 6.7 %copy-start.8 = (f32[8,256,256]{2,1,0:T(8,128)}, f32[8,256,256]{2,1,0:T(8,128)S(1)}, u32[]{:S(2)}) copy-start(f32[8,256,256]{2,1,0:T(8,128)S(1)} %fusion.28) | copy-start | bytes 6291460 | tf_op jit(solution)/shard_map/while
  240.2 5.7 copy-start.1
  245.3 6.7 %copy-start.8 = (f32[8,256,256]{2,1,0:T(8,128)}, f32[8,256,256]{2,1,0:T(8,128)S(1)}, u32[]{:S(2)}) copy-start(f32[8,256,256]{2,1,0:T(8,128)S(1)} %fusion.28) | copy-start | bytes 6291460 | tf_op jit(solution)/shard_map/while
  301.7 5.8 copy-start.1
  306.8 6.7 %copy-start.8 = (f32[8,256,256]{2,1,0:T(8,128)}, f32[8,256,256]{2,1,0:T(8,128)S(1)}, u32[]{:S(2)}) copy-start(f32[8,256,256]{2,1,0:T(8,128)S(1)} %fusion.28) | copy-start | bytes 6291460 | tf_op jit(solution)/shard_map/while
  355.3 247.0 %reduce-scatter.2.cloned.1.call-start = ((), (), s32[]{:S(2)}) async-start(), calls=%async_computation.4 | async-start | bytes 4718592 | tf_op jit(solution)/shard_map/reduce_scatter | solution.py:111
  355.4 0.7 copy-start.5
  355.4 0.8 copy-start.6
  355.4 41.9 %copy-start.4 = (f32[1024]{0:T(1024)S(1)}, f32[1024]{0:T(1024)}, u32[]{:S(2)}) copy-start(f32[1024]{0:T(1024)} %param.16) | copy-start | bytes 12292
  355.4 41.9 %copy-start.3 = (f32[2048]{0:T(1024)S(1)}, f32[2048]{0:T(1024)}, u32[]{:S(2)}) copy-start(f32[2048]{0:T(1024)} %param.13) | copy-start | bytes 24580
  516.6 85.7 %copy-start.2 = (bf16[1024,128]{1,0:T(8,128)(2,1)S(1)}, bf16[1024,128]{1,0:T(8,128)(2,1)}, u32[]{:S(2)}) copy-start(bf16[1024,128]{1,0:T(8,128)(2,1)} %get-tuple-element.195) | copy-start | bytes 786436
Sparse Core Ops, SparseCore 0:
  13.3 53.0 all-gather.4
  68.5 33.1 all-gather.2
  355.5 154.4 all-reduce.2
  513.5 88.8 reduce-scatter.1
where the time goes:
time: 633 us; the launch traced here: 632 us
  waiting for transfers between devices  267 us (42%)
  other arithmetic  174 us (27%)
  matrix products  74.9 us (12%)
  blocking collectives  60.9 us (10%)
  local copies, waits for them, and re-layouts  41 us (6%)
  between operations  13.9 us (2%)
    psum x1, waiting for transfers between devices, on_device(): user_summed = lax.psum(user_acc, 'item')  113 us
    reduce_scatter x1, waiting for transfers between devices, on_device(): lax.psum_scatter(item_acc, 'user', scatter_dimension=1, tiled=True)  83.2 us
    scatter-add x4, other arithmetic, group_step(): user_acc = user_acc.at[rows_user].add(user_terms)  68.9 us
    scatter-add x4, other arithmetic, group_step(): item_acc = item_acc.at[rows_item].add(item_terms)  68.7 us
    psum x1, blocking collectives, on_device(): lax.psum((beta_placed, theta_placed), ('user', 'item'))  40.8 us
    all_gather x1, waiting for transfers between devices, on_device(): beta_full = lax.all_gather(beta_part, 'user', axis=1, tiled=True)  35.5 us
    all_gather x1, waiting for transfers between devices, on_device(): theta_full = lax.all_gather(theta_part, 'item', axis=1, tiled=True)  35.3 us
    dot_general x4, matrix products, group_step(): jnp.einsum('tui,tik->tuk', ratio_tile, items, preferred_element_type=jnp....  30.8 us
  transfers between devices with their start and end apart: 4, of which 4 were waited for; matrix products, arithmetic and copies ran while one was open for 4% of the time, Pallas kernels for 0%

commit v1 on v0

v1 whole, which is shorter than its diff:
```python
import jax
import jax.numpy as jnp
from jax import lax
from jax.sharding import PartitionSpec as P

BLK = 256
UB = 8
IB = 4
TMAX = 32


prior_a = 0.3
prior_a2 = 0.3
prior_b2 = 1.0
prior_c = 0.3
prior_c2 = 0.3
prior_d2 = 1.0


def exp_mean_log(shape_param, rate_param):
    return jnp.exp(lax.digamma(shape_param) - jnp.log(rate_param)).astype(jnp.bfloat16)


def dense_counts(tile_slots, tile_counts, live_tiles):
    slot_list = tile_slots.reshape(TMAX)
    used_slots = live_tiles.reshape(())
    positions = jnp.arange(UB * IB, dtype=jnp.int32)
    live = jnp.arange(TMAX, dtype=jnp.int32) < used_slots
    match = (slot_list[None, :] == positions[:, None]) & live[None, :]
    present = jnp.any(match, axis=1)
    source = jnp.argmax(match, axis=1)
    count_tiles = tile_counts.reshape(TMAX, BLK, BLK)
    grid = jnp.take(count_tiles, source, axis=0)
    grid = jnp.where(present[:, None, None], grid, jnp.zeros_like(grid))
    return grid.reshape(UB, IB, BLK, BLK)


def on_device(
    theta_shape,
    theta_rate,
    xi_rate,
    beta_shape,
    beta_rate,
    eta_rate,
    tile_slots,
    tile_counts,
    live_tiles,
):
    user_width = lax.axis_size("user")
    item_width = lax.axis_size("item")
    user_index = lax.axis_index("user")
    item_index = lax.axis_index("item")
    theta_part = exp_mean_log(theta_shape, theta_rate)
    beta_part = exp_mean_log(beta_shape, beta_rate)
    theta_full = lax.all_gather(theta_part, "item", axis=1, tiled=True)
    beta_full = lax.all_gather(beta_part, "user", axis=1, tiled=True)
    factors = theta_full.shape[1]
    user_rows = theta_full.shape[0]
    item_rows = beta_full.shape[0]
    theta_blocks = theta_full.reshape(UB, BLK, factors)
    beta_blocks = beta_full.reshape(IB, BLK, factors)
    counts = dense_counts(tile_slots, tile_counts, live_tiles).astype(jnp.float32)
    denominator = jnp.einsum(
        "buk,jik->bjui", theta_blocks, beta_blocks, preferred_element_type=jnp.float32
    )
    ratio = (counts / denominator).astype(jnp.bfloat16)
    user_acc = jnp.einsum("bjui,jik->buk", ratio, beta_blocks, preferred_element_type=jnp.float32)
    item_acc = jnp.einsum("bjui,buk->jik", ratio, theta_blocks, preferred_element_type=jnp.float32)
    user_acc = user_acc.reshape(user_rows, factors)
    item_acc = item_acc.reshape(item_rows, factors)
    beta_columns = factors // user_width
    theta_columns = factors // item_width
    beta_local = jnp.sum(beta_shape / beta_rate, axis=0)
    theta_local = jnp.sum(theta_shape / theta_rate, axis=0)
    beta_placed = lax.dynamic_update_slice_in_dim(
        jnp.zeros((factors,), jnp.float32), beta_local, user_index * beta_columns, 0
    )
    theta_placed = lax.dynamic_update_slice_in_dim(
        jnp.zeros((factors,), jnp.float32), theta_local, item_index * theta_columns, 0
    )
    beta_total, theta_total = lax.psum((beta_placed, theta_placed), ("user", "item"))
    xi_mean = (prior_a2 + factors * prior_a) / xi_rate
    user_share = lax.psum_scatter(user_acc, "item", scatter_dimension=1, tiled=True)
    theta_shape_new = prior_a + theta_part.astype(jnp.float32) * user_share
    beta_slice = lax.dynamic_slice_in_dim(beta_total, item_index * theta_columns, theta_columns, 0)
    theta_rate_new = xi_mean[:, None] + beta_slice[None, :]
    user_part = jnp.sum(theta_shape_new / theta_rate_new, axis=1)
    xi_rate_new = prior_a2 / prior_b2 + lax.psum(user_part, "item")
    item_share = lax.psum_scatter(item_acc, "user", scatter_dimension=1, tiled=True)
    beta_shape_new = prior_c + beta_part.astype(jnp.float32) * item_share
    eta_mean = (prior_c2 + factors * prior_c) / eta_rate
    theta_slice = lax.dynamic_slice_in_dim(theta_total, user_index * beta_columns, beta_columns, 0)
    beta_rate_new = eta_mean[:, None] + theta_slice[None, :]
    item_part = jnp.sum(beta_shape_new / beta_rate_new, axis=1)
    eta_rate_new = prior_c2 / prior_d2 + lax.psum(item_part, "user")
    return (
        theta_shape_new,
        jnp.log(theta_rate_new),
        xi_rate_new,
        beta_shape_new,
        jnp.log(beta_rate_new),
        eta_rate_new,
    )


def solution(mesh):
    in_specs = (
        P("user", "item"),
        P("user", "item"),
        P("user"),
        P("item", "user"),
        P("item", "user"),
        P("item"),
        P("user", "item", None),
        P("user", "item", None, None, None),
        P("user", "item"),
    )
    out_specs = (
        P("user", "item"),
        P("user", "item"),
        P("user"),
        P("item", "user"),
        P("item", "user"),
        P("item"),
    )
    return jax.shard_map(
        on_device, mesh=mesh, in_specs=in_specs, out_specs=out_specs, check_vma=False
    )
```

time: 633 us -> 301 us (0.48)
  other arithmetic: 174 us -> 30.9 us
  waiting for transfers between devices: 267 us -> 142 us
  matrix products: 74.9 us -> 24.1 us
  local copies, waits for them, and re-layouts: 41 us -> 22.3 us
    scatter-add x8 -> x0, other arithmetic: 138 us -> none  [the longest x4 68.9 us: group_step(): user_acc = user_acc.at[rows_user].add(user_terms)]
    psum x1 -> x0, waiting for transfers between devices: 113 us -> none  [on_device(): user_summed = lax.psum(user_acc, 'item')]
    dot_general x12 -> x3, matrix products: 74.9 us -> 24.1 us  [the longest x1 9.23 us: on_device(): jnp.einsum('bjui,jik->buk', ratio, beta_blocks, preferred_element_type=jn...]
    reduce_scatter x1, waiting for transfers between devices: 83.2 us -> 32.6 us  [on_device(): lax.psum_scatter(item_acc, 'user', scatter_dimension=1, tiled=True)]
    reduce_scatter x0 -> x1, waiting for transfers between devices: none -> 50.5 us  [on_device(): lax.psum_scatter(user_acc, 'item', scatter_dimension=1, tiled=True)]
    gather x8 -> x2, local copies, waits for them, and re-layouts: 31 us -> 11.2 us  [dense_counts(): grid = jnp.take(count_tiles, source, axis=0)]
    all_gather x1, waiting for transfers between devices: 35.5 us -> 23 us  [on_device(): beta_full = lax.all_gather(beta_part, 'user', axis=1, tiled=True)]
    dot_general x0 -> x2, local copies, waits for them, and re-layouts: none -> 8.84 us  [the longest x1 6.37 us: on_device(): jnp.einsum('bjui,jik->buk', ratio, beta_blocks, preferred_element_type=jn...]
  transfers between devices with their start and end apart: 4 -> 4, of which waited for: 4 -> 4; matrix products, arithmetic and copies ran while one was open for 4% -> 16% of each run, Pallas kernels for 0% -> 0%
where the time goes in v1:
time: 301 us
  waiting for transfers between devices  142 us (47%)
  blocking collectives  66.9 us (22%)
  other arithmetic  30.9 us (10%)
  matrix products  24.1 us (8%)
  local copies, waits for them, and re-layouts  22.3 us (7%)
  between operations  14.5 us (5%)
    reduce_scatter x1, waiting for transfers between devices, on_device(): lax.psum_scatter(user_acc, 'item', scatter_dimension=1, tiled=True)  50.5 us
    psum x1, blocking collectives, on_device(): lax.psum((beta_placed, theta_placed), ('user', 'item'))  41 us
    all_gather x1, waiting for transfers between devices, on_device(): theta_full = lax.all_gather(theta_part, 'item', axis=1, tiled=True)  35.3 us
    reduce_scatter x1, waiting for transfers between devices, on_device(): lax.psum_scatter(item_acc, 'user', scatter_dimension=1, tiled=True)  32.6 us
    all_gather x1, waiting for transfers between devices, on_device(): beta_full = lax.all_gather(beta_part, 'user', axis=1, tiled=True)  23 us
    convert_element_type x2, other arithmetic, exp_mean_log(): jnp.exp(lax.digamma(shape_param) - jnp.log(rate_param)).astype(jnp.bfloat16)  22.5 us
    psum x1, blocking collectives, on_device(): eta_rate_new = prior_c2 / prior_d2 + lax.psum(item_part, 'user')  20 us
    gather x2, local copies, waits for them, and re-layouts, dense_counts(): grid = jnp.take(count_tiles, source, axis=0)  11.2 us
  transfers between devices with their start and end apart: 4, of which 4 were waited for; matrix products, arithmetic and copies ran while one was open for 16% of the time, Pallas kernels for 0%

profile of v1, /device:TPU:0, one launch (start us, length us, event | category | flops | bytes accessed | tf_op | source)
XLA Modules:
  0.0 300.6 jit_solution(4408127229234385359)
XLA Ops:
  7.2 0.0 all-gather.3.cloned.1.call-start
  7.2 5.4 %fusion.17 = (bf16[1024,128]{1,0:T(8,128)(2,1)}, f32[128]{0:T(128)S(1)}) fusion(f32[1024,128]{1,0:T(8,128)} %param.13, f32[1024,128]{1,0:T(8,128)} %param.12), kind=kLoop, calls=%fused_computation.28 | loop fusion | flops 10354560 | bytes 1311232 | tf_op jit(solution)/shard_map/convert_element_type | solution.py:21
  12.7 0.0 all-gather.3.cloned.1.call-update
  12.7 0.0 copy-start.5
  12.7 0.0 all-gather.5.cloned.1.call-start
  12.7 17.0 %fusion.10 = (bf16[2048,256]{1,0:T(8,128)(2,1)}, f32[256]{0:T(256)S(1)}) fusion(f32[2048,256]{1,0:T(8,128)} %param.10, f32[2048,256]{1,0:T(8,128)} %param.9), kind=kLoop, calls=%fused_computation.15 | loop fusion | flops 41418496 | bytes 5243904 | tf_op jit(solution)/shard_map/convert_element_type | solution.py:21
  29.8 0.0 all-gather.5.cloned.1.call-update
  29.8 0.0 reduce-scatter.5.cloned.1.call-start
  30.5 0.0 copy-done.5
  30.5 0.6 iota_reduce_fusion
  31.2 5.0 %gather_fusion = bf16[32,256,256]{2,1,0:T(8,128)(2,1)} fusion(bf16[32,256,256]{2,1,0:T(8,128)(2,1)} %bitcast.33, s32[1024]{0:T(1024)S(1)} %pad_clamp_fusion), kind=kCustom, calls=%fused_computation | custom fusion | bytes 8388736 | tf_op jit(solution)/shard_map/jit(_take)/gather | solution.py:33
  36.2 6.2 %copy.25 = bf16[8,4,256,256]{2,3,0,1:T(8,128)(2,1)} copy(bf16[8,4,256,256]{3,2,1,0:T(8,128)(2,1)} %bitcast.32) | data formatting | bytes 8388608 | tf_op jit(solution)/shard_map/jit(_take)/gather | solution.py:33
  42.4 0.1 broadcast_in_dim.36
  42.5 0.1 copy.24
  42.6 0.1 fusion.21
  42.7 0.1 broadcast_in_dim.34
  42.8 0.1 copy.23
  42.9 23.0 %all-gather.3.cloned.1.call-done = bf16[1024,1024]{1,0:T(8,128)(2,1)} async-done(((bf16[1024,128]{1,0:T(8,128)(2,1)}), bf16[1024,1024]{1,0:T(8,128)(2,1)}) %all-gather.3.cloned.1.call-update) | async-done | bytes 2097168 | tf_op jit(solution)/shard_map/all_gather | solution.py:56
  65.9 35.3 %all-gather.5.cloned.1.call-done = bf16[2048,1024]{1,0:T(8,128)(2,1)} async-done(((bf16[2048,256]{1,0:T(8,128)(2,1)}), bf16[2048,1024]{1,0:T(8,128)(2,1)}) %all-gather.5.cloned.1.call-update) | async-done | bytes 4194320 | tf_op jit(solution)/shard_map/all_gather | solution.py:55
  101.2 8.7 %fusion = bf16[8,4,256,256]{2,3,0,1:T(8,128)(2,1)S(1)} fusion(bf16[8,4,256,256]{2,3,0,1:T(8,128)(2,1)} %copy.25, pred[8,4]{0,1:T(4,128)(4,1)S(1)} %copy.24, pred[8,4]{0,1:T(4,128)(4,1)S(1)} %copy.23, bf16[4,256,1024,1]{2,1,3,0:T(8,128)(2,1)} %bitcast.40, bf16[8,256,1024,1]{2,1,0,3:T(8,128)(2,1)} %bitcast.38), kind=kOutput, calls=%fused_computation.2 | convolution fusion | flops 4305453056 | bytes 14680128 | tf_op jit(solution)/shard_map/buk,jik->bjui/dot_general | solution.py:63
  110.0 0.0 copy-start
  110.0 0.0 copy-start.6
  110.0 2.5 copy.27
  112.4 0.0 copy-done
  112.4 1.2 copy-done.6
  113.7 6.2 %fusion.3 = f32[1024,1024]{1,0:T(8,128)} fusion(bf16[8,256,1024]{2,1,0:T(8,128)(2,1)S(1)} %bitcast.39, bf16[1024,8,256]{2,1,0:T(8,128)(2,1)S(1)} %bitcast.35), kind=kOutput, calls=%fused_computation.10 | convolution fusion | flops 4294967296 | bytes 12582912 | tf_op jit(solution)/shard_map/bjui,buk->jik/dot_general | solution.py:68
  119.8 0.0 reduce-scatter.5.cloned.1.call-update
  119.8 0.2 reduce-scatter.3.cloned.1.call-start
  120.1 0.0 copy-start.7
  120.1 6.4 %copy.26 = bf16[8,256,256,4]{2,1,0,3:T(8,128)(2,1)} copy(bf16[8,256,256,4]{1,2,0,3:T(8,128)(2,1)} %bitcast.31) | data formatting | bytes 8388608 | tf_op jit(solution)/shard_map/bjui,jik->buk/dot_general | solution.py:67
  126.5 0.0 copy-done.7
  126.5 9.2 %convolution_bitcast_fusion = f32[2048,1024]{1,0:T(8,128)} fusion(bf16[2048,256,4]{1,0,2:T(8,128)(2,1)} %bitcast.34, bf16[4,256,1024]{2,1,0:T(8,128)(2,1)S(1)} %bitcast.41), kind=kOutput, calls=%fused_computation.3 | convolution fusion | flops 4294967296 | bytes 14680064 | tf_op jit(solution)/shard_map/bjui,jik->buk/dot_general | solution.py:67
  135.7 0.0 copy-start.4
  135.7 0.0 copy-start.3
  135.7 0.0 copy-start.2
  135.7 0.0 reduce-scatter.3.cloned.1.call-update
  135.7 0.0 copy-start.1
  135.7 0.3 dynamic_update_slice.7
  136.0 0.2 dynamic_update_slice.6
  136.2 41.0 %all-reduce = (f32[1024]{0:T(1024)S(1)}, f32[1024]{0:T(1024)S(1)}) all-reduce(f32[1024]{0:T(1024)S(1)} %dynamic_update_slice.6, f32[1024]{0:T(1024)S(1)} %dynamic_update_slice.7), channel_id=1, replica_groups=mesh['user'=8,'item'=4] {'user','item'}, use_global_device_ids=true, to_apply=%region_4.5 | all-reduce | flops 2048 | bytes 16384 | tf_op jit(solution)/shard_map/psum | solution.py:81
  177.2 0.1 dynamic_slice.6
  177.3 0.1 dynamic_slice.7
  177.4 0.0 copy-done.4
  177.4 0.0 copy-done.3
  177.4 32.6 %reduce-scatter.5.cloned.1.call-done = f32[1024,128]{1,0:T(8,128)} async-done(((f32[1024,1024]{1,0:T(8,128)}), f32[1024,128]{1,0:T(8,128)}) %reduce-scatter.5.cloned.1.call-update) | async-done | bytes 524304 | tf_op jit(solution)/shard_map/reduce_scatter | solution.py:89
  210.0 0.0 copy-done.2
  210.0 2.2 fusion.18
  212.2 20.0 %psum.31 = f32[1024]{0:T(1024)S(1)} all-reduce(f32[1024]{0:T(1024)S(1)} %get-tuple-element.10), channel_id=1, replica_groups=mesh['user'=8,'item'=4] {'user'}, use_global_device_ids=true, to_apply=%region_11.12 | all-reduce | flops 1024 | bytes 8192 | tf_op jit(solution)/shard_map/psum | solution.py:95
  232.2 0.6 broadcast_add_fusion.1
  232.8 50.5 %reduce-scatter.3.cloned.1.call-done = f32[2048,256]{1,0:T(8,128)} async-done(((f32[2048,1024]{1,0:T(8,128)}), f32[2048,256]{1,0:T(8,128)}) %reduce-scatter.3.cloned.1.call-update) | async-done | bytes 2097168 | tf_op jit(solution)/shard_map/reduce_scatter | solution.py:83
  283.3 0.0 copy-done.1
  283.3 4.3 %fusion.11 = (f32[2048]{0:T(1024)S(1)}, f32[2048,256]{1,0:T(8,128)}, f32[2048,256]{1,0:T(8,128)}) fusion(f32[256]{0:T(256)S(1)} %dynamic_slice.6, f32[2048]{0:T(1024)S(1)} %broadcast_divide_fusion, f32[2048,256]{1,0:T(8,128)} %reduce-scatter.3.cloned.1.call-done, bf16[2048,256]{1,0:T(8,128)(2,1)S(1)} %copy-done.1), kind=kLoop, calls=%fused_computation.18 | loop fusion | flops 3143680 | bytes 7357440 | tf_op jit(solution)/shard_map/reduce_sum | solution.py:87
  287.7 5.8 %psum.29 = f32[2048]{0:T(1024)S(1)} all-reduce(f32[2048]{0:T(1024)S(1)} %get-tuple-element.12), channel_id=1, replica_groups=mesh['user'=8,'item'=4] {'item'}, use_global_device_ids=true, to_apply=%region_6.7 | all-reduce | flops 2048 | bytes 16384 | tf_op jit(solution)/shard_map/psum | solution.py:88
  293.5 0.6 broadcast_add_fusion
  (8 shorter events, 0.0 us)
Async XLA Ops:
  7.2 58.7 %all-gather.3.cloned.1.call-start = ((), (), s32[]{:S(2)}) async-start(), calls=%async_computation.2 | async-start | bytes 2359296 | tf_op jit(solution)/shard_map/all_gather | solution.py:56
  12.7 17.8 %copy-start.5 = (s32[1,1,32]{2,1,0:T(1,128)S(1)}, s32[1,1,32]{2,1,0:T(1,128)}, u32[]{:S(2)}) copy-start(s32[1,1,32]{2,1,0:T(1,128)} %param.15) | copy-start | bytes 388
  12.7 88.5 %all-gather.5.cloned.1.call-start = ((), (), s32[]{:S(2)}) async-start(), calls=%async_computation.3 | async-start | bytes 5242880 | tf_op jit(solution)/shard_map/all_gather | solution.py:55
  29.8 180.2 %reduce-scatter.5.cloned.1.call-start = ((), (), s32[]{:S(2)}) async-start(), calls=%async_computation.5 | async-start | bytes 4718592 | tf_op jit(solution)/shard_map/reduce_scatter | solution.py:89
  110.0 2.5 copy-start
  110.0 3.7 %copy-start.6 = (bf16[2048,1024]{1,0:T(8,128)(2,1)S(1)}, bf16[2048,1024]{1,0:T(8,128)(2,1)}, u32[]{:S(2)}) copy-start(bf16[2048,1024]{1,0:T(8,128)(2,1)} %all-gather.5.cloned.1.call-done) | copy-start | bytes 12582916
  119.8 163.5 %reduce-scatter.3.cloned.1.call-start = ((), (), s32[]{:S(2)}) async-start(), calls=%async_computation.4 | async-start | bytes 10485760 | tf_op jit(solution)/shard_map/reduce_scatter | solution.py:83
  120.1 6.4 %copy-start.7 = (bf16[1024,1024]{1,0:T(8,128)(2,1)S(1)}, bf16[1024,1024]{1,0:T(8,128)(2,1)}, u32[]{:S(2)}) copy-start(bf16[1024,1024]{1,0:T(8,128)(2,1)} %all-gather.3.cloned.1.call-done) | copy-start | bytes 6291460
  135.7 41.7 %copy-start.4 = (f32[1024]{0:T(1024)S(1)}, f32[1024]{0:T(1024)}, u32[]{:S(2)}) copy-start(f32[1024]{0:T(1024)} %param.14) | copy-start | bytes 12292
  135.7 41.7 %copy-start.3 = (f32[2048]{0:T(1024)S(1)}, f32[2048]{0:T(1024)}, u32[]{:S(2)}) copy-start(f32[2048]{0:T(1024)} %param.11) | copy-start | bytes 24580
  135.7 74.3 %copy-start.2 = (bf16[1024,128]{1,0:T(8,128)(2,1)S(1)}, bf16[1024,128]{1,0:T(8,128)(2,1)}, u32[]{:S(2)}) copy-start(bf16[1024,128]{1,0:T(8,128)(2,1)} %get-tuple-element.16) | copy-start | bytes 786436
  135.7 147.6 %copy-start.1 = (bf16[2048,256]{1,0:T(8,128)(2,1)S(1)}, bf16[2048,256]{1,0:T(8,128)(2,1)}, u32[]{:S(2)}) copy-start(bf16[2048,256]{1,0:T(8,128)(2,1)} %get-tuple-element.14) | copy-start | bytes 3145732
Sparse Core Ops, SparseCore 0:
  12.8 53.0 all-gather.2
  68.0 33.1 all-gather.4
  120.0 90.0 reduce-scatter.4
  212.4 70.8 reduce-scatter.2

commit v2 on v1

--- a/solution.py
+++ b/solution.py
@@ -50,11 +50,28 @@
     item_width = lax.axis_size("item")
     user_index = lax.axis_index("user")
     item_index = lax.axis_index("item")
+    factors = theta_shape.shape[1] * item_width
+    beta_columns = factors // user_width
+    theta_columns = factors // item_width
     theta_part = exp_mean_log(theta_shape, theta_rate)
     beta_part = exp_mean_log(beta_shape, beta_rate)
+    beta_local = jnp.sum(beta_shape / beta_rate, axis=0)
+    theta_local = jnp.sum(theta_shape / theta_rate, axis=0)
+    beta_placed = lax.dynamic_update_slice_in_dim(
+        jnp.zeros((factors,), jnp.float32), beta_local, user_index * beta_columns, 0
+    )
+    theta_placed = lax.dynamic_update_slice_in_dim(
+        jnp.zeros((factors,), jnp.float32), theta_local, item_index * theta_columns, 0
+    )
     theta_full = lax.all_gather(theta_part, "item", axis=1, tiled=True)
     beta_full = lax.all_gather(beta_part, "user", axis=1, tiled=True)
-    factors = theta_full.shape[1]
+    theta_part, beta_placed, theta_placed = lax.optimization_barrier(
+        (theta_part, beta_placed, theta_placed)
+    )
+    beta_total, theta_total = lax.psum((beta_placed, theta_placed), ("user", "item"))
+    tile_counts, beta_total, theta_total = lax.optimization_barrier(
+        (tile_counts, beta_total, theta_total)
+    )
     user_rows = theta_full.shape[0]
     item_rows = beta_full.shape[0]
     theta_blocks = theta_full.reshape(UB, BLK, factors)
@@ -68,17 +85,6 @@
     item_acc = jnp.einsum("bjui,buk->jik", ratio, theta_blocks, preferred_element_type=jnp.float32)
     user_acc = user_acc.reshape(user_rows, factors)
     item_acc = item_acc.reshape(item_rows, factors)
-    beta_columns = factors // user_width
-    theta_columns = factors // item_width
-    beta_local = jnp.sum(beta_shape / beta_rate, axis=0)
-    theta_local = jnp.sum(theta_shape / theta_rate, axis=0)
-    beta_placed = lax.dynamic_update_slice_in_dim(
-        jnp.zeros((factors,), jnp.float32), beta_local, user_index * beta_columns, 0
-    )
-    theta_placed = lax.dynamic_update_slice_in_dim(
-        jnp.zeros((factors,), jnp.float32), theta_local, item_index * theta_columns, 0
-    )
-    beta_total, theta_total = lax.psum((beta_placed, theta_placed), ("user", "item"))
     xi_mean = (prior_a2 + factors * prior_a) / xi_rate
     user_share = lax.psum_scatter(user_acc, "item", scatter_dimension=1, tiled=True)
     theta_shape_new = prior_a + theta_part.astype(jnp.float32) * user_share

time: 301 us -> 301 us (level)
  waiting for transfers between devices: 142 us -> 136 us
  blocking collectives: 66.9 us -> 71.4 us
    reduce_scatter x1, waiting for transfers between devices: 32.6 us -> 72.3 us  [on_device(): lax.psum_scatter(item_acc, 'user', scatter_dimension=1, tiled=True)]
    all_gather x1, waiting for transfers between devices: 23 us -> 0.01 us  [on_device(): beta_full = lax.all_gather(beta_part, 'user', axis=1, tiled=True)]
    all_gather x1, waiting for transfers between devices: 35.3 us -> 12.8 us  [on_device(): theta_full = lax.all_gather(theta_part, 'item', axis=1, tiled=True)]
    reduce_sum x0 -> x1, other arithmetic: none -> 17 us  [on_device(): theta_local = jnp.sum(theta_shape / theta_rate, axis=0)]
    convert_element_type x2 -> x1, other arithmetic: 22.5 us -> 5.45 us  [exp_mean_log(): jnp.exp(lax.digamma(shape_param) - jnp.log(rate_param)).astype(jnp.bfloat16)]
    psum x1, blocking collectives: 41 us -> 45.5 us  [on_device(): lax.psum((beta_placed, theta_placed), ('user', 'item'))]
  transfers between devices with their start and end apart: 4 -> 4, of which waited for: 4 -> 3; matrix products, arithmetic and copies ran while one was open for 16% -> 16% of each run, Pallas kernels for 0% -> 0%
where the time goes in v2:
time: 301 us; the launch traced here: 300 us
  waiting for transfers between devices  136 us (45%)
  blocking collectives  71.4 us (24%)
  other arithmetic  30.9 us (10%)
  matrix products  24.1 us (8%)
  local copies, waits for them, and re-layouts  22.9 us (8%)
  between operations  14.5 us (5%)
    reduce_scatter x1, waiting for transfers between devices, on_device(): lax.psum_scatter(item_acc, 'user', scatter_dimension=1, tiled=True)  72.3 us
    reduce_scatter x1, waiting for transfers between devices, on_device(): lax.psum_scatter(user_acc, 'item', scatter_dimension=1, tiled=True)  50.5 us
    psum x1, blocking collectives, on_device(): lax.psum((beta_placed, theta_placed), ('user', 'item'))  45.5 us
    psum x1, blocking collectives, on_device(): eta_rate_new = prior_c2 / prior_d2 + lax.psum(item_part, 'user')  20.1 us
    reduce_sum x1, other arithmetic, on_device(): theta_local = jnp.sum(theta_shape / theta_rate, axis=0)  17 us
    all_gather x1, waiting for transfers between devices, on_device(): theta_full = lax.all_gather(theta_part, 'item', axis=1, tiled=True)  12.8 us
    gather x2, local copies, waits for them, and re-layouts, dense_counts(): grid = jnp.take(count_tiles, source, axis=0)  11.3 us
    dot_general x1, matrix products, on_device(): jnp.einsum('bjui,jik->buk', ratio, beta_blocks, preferred_element_type=jn...  9.2 us
  transfers between devices with their start and end apart: 4, of which 3 were waited for; matrix products, arithmetic and copies ran while one was open for 16% of the time, Pallas kernels for 0%

profile of v2, /device:TPU:0, one launch (start us, length us, event | category | flops | bytes accessed | tf_op | source)
XLA Modules:
  0.0 299.8 jit_solution(15192449991630237248)
XLA Ops:
  7.2 0.0 all-gather.3.cloned.1.call-start
  7.2 5.4 %fusion.17 = (bf16[1024,128]{1,0:T(8,128)(2,1)}, f32[128]{0:T(128)S(1)}) fusion(f32[1024,128]{1,0:T(8,128)} %param.13, f32[1024,128]{1,0:T(8,128)} %param.12), kind=kLoop, calls=%fused_computation.28 | loop fusion | flops 10354560 | bytes 1311232 | tf_op jit(solution)/shard_map/convert_element_type | solution.py:21
  12.7 0.0 all-gather.3.cloned.1.call-update
  12.7 0.0 copy-start.5
  12.7 0.0 all-gather.5.cloned.1.call-start
  12.7 17.0 %divide_reduce_fusion = (f32[256]{0:T(256)S(1)}, bf16[2048,256]{1,0:T(8,128)(2,1)}) fusion(f32[2048,256]{1,0:T(8,128)} %param.9, f32[2048,256]{1,0:T(8,128)} %param.10), kind=kLoop, calls=%fused_computation.17 | loop fusion | flops 41418496 | bytes 5243904 | tf_op jit(solution)/shard_map/reduce_sum | solution.py:59
  29.8 0.0 all-gather.5.cloned.1.call-update
  29.8 0.0 reduce-scatter.5.cloned.1.call-start
  29.9 0.3 dynamic_update_slice.7
  30.1 0.2 dynamic_update_slice.6
  30.4 45.5 %all-reduce = (f32[1024]{0:T(1024)S(1)}, f32[1024]{0:T(1024)S(1)}) all-reduce(f32[1024]{0:T(1024)S(1)} %dynamic_update_slice.6, f32[1024]{0:T(1024)S(1)} %dynamic_update_slice.7), channel_id=1, replica_groups=mesh['user'=8,'item'=4] {'user','item'}, use_global_device_ids=true, to_apply=%region_4.0 | all-reduce | flops 2048 | bytes 16384 | tf_op jit(solution)/shard_map/psum | solution.py:71
  76.5 0.0 copy-done.5
  76.5 0.6 iota_reduce_fusion
  77.2 5.1 %gather_fusion = bf16[32,256,256]{2,1,0:T(8,128)(2,1)} fusion(bf16[32,256,256]{2,1,0:T(8,128)(2,1)} %bitcast.33, s32[1024]{0:T(1024)S(1)} %pad_clamp_fusion), kind=kCustom, calls=%fused_computation | custom fusion | bytes 8388736 | tf_op jit(solution)/shard_map/jit(_take)/gather | solution.py:33
  82.2 6.2 %copy.25 = bf16[8,4,256,256]{2,3,0,1:T(8,128)(2,1)} copy(bf16[8,4,256,256]{3,2,1,0:T(8,128)(2,1)} %bitcast.32) | data formatting | bytes 8388608 | tf_op jit(solution)/shard_map/jit(_take)/gather | solution.py:33
  88.4 0.1 broadcast_in_dim.36
  88.5 0.1 copy.24
  88.6 0.1 fusion.21
  88.7 0.1 broadcast_in_dim.34
  88.8 0.1 copy.23
  88.9 0.0 all-gather.3.cloned.1.call-done
  88.9 12.8 %all-gather.5.cloned.1.call-done = bf16[2048,1024]{1,0:T(8,128)(2,1)} async-done(((bf16[2048,256]{1,0:T(8,128)(2,1)}), bf16[2048,1024]{1,0:T(8,128)(2,1)}) %all-gather.5.cloned.1.call-update) | async-done | bytes 4194320 | tf_op jit(solution)/shard_map/all_gather | solution.py:66
  101.7 8.7 %fusion = bf16[8,4,256,256]{2,3,0,1:T(8,128)(2,1)S(1)} fusion(bf16[8,4,256,256]{2,3,0,1:T(8,128)(2,1)} %copy.25, pred[8,4]{0,1:T(4,128)(4,1)S(1)} %copy.24, pred[8,4]{0,1:T(4,128)(4,1)S(1)} %copy.23, bf16[4,256,1024,1]{2,1,3,0:T(8,128)(2,1)} %bitcast.40, bf16[8,256,1024,1]{2,1,0,3:T(8,128)(2,1)} %bitcast.38), kind=kOutput, calls=%fused_computation.2 | convolution fusion | flops 4305453056 | bytes 14680128 | tf_op jit(solution)/shard_map/buk,jik->bjui/dot_general | solution.py:80
  110.4 0.0 copy-start
  110.4 0.0 copy-start.6
  110.4 2.5 copy.27
  112.9 0.0 copy-done
  112.9 1.2 copy-done.6
  114.1 6.2 %fusion.3 = f32[1024,1024]{1,0:T(8,128)} fusion(bf16[8,256,1024]{2,1,0:T(8,128)(2,1)S(1)} %bitcast.39, bf16[1024,8,256]{2,1,0:T(8,128)(2,1)S(1)} %bitcast.35), kind=kOutput, calls=%fused_computation.10 | convolution fusion | flops 4294967296 | bytes 12582912 | tf_op jit(solution)/shard_map/bjui,buk->jik/dot_general | solution.py:85
  120.3 0.0 reduce-scatter.5.cloned.1.call-update
  120.3 0.3 reduce-scatter.3.cloned.1.call-start
  120.6 0.0 copy-start.7
  120.6 6.4 %copy.26 = bf16[8,256,256,4]{2,1,0,3:T(8,128)(2,1)} copy(bf16[8,256,256,4]{1,2,0,3:T(8,128)(2,1)} %bitcast.31) | data formatting | bytes 8388608 | tf_op jit(solution)/shard_map/bjui,jik->buk/dot_general | solution.py:84
  127.0 0.0 copy-done.7
  127.0 9.2 %convolution_bitcast_fusion = f32[2048,1024]{1,0:T(8,128)} fusion(bf16[2048,256,4]{1,0,2:T(8,128)(2,1)} %bitcast.34, bf16[4,256,1024]{2,1,0:T(8,128)(2,1)S(1)} %bitcast.41), kind=kOutput, calls=%fused_computation.3 | convolution fusion | flops 4294967296 | bytes 14680064 | tf_op jit(solution)/shard_map/bjui,jik->buk/dot_general | solution.py:84
  136.2 0.0 copy-start.4
  136.2 0.0 copy-start.3
  136.2 0.0 copy-start.2
  136.2 0.0 reduce-scatter.3.cloned.1.call-update
  136.2 0.0 copy-start.1
  136.2 0.1 dynamic_slice.6
  136.3 0.1 dynamic_slice.7
  136.4 0.5 copy-done.4
  136.8 0.0 copy-done.3
  136.9 72.3 %reduce-scatter.5.cloned.1.call-done = f32[1024,128]{1,0:T(8,128)} async-done(((f32[1024,1024]{1,0:T(8,128)}), f32[1024,128]{1,0:T(8,128)}) %reduce-scatter.5.cloned.1.call-update) | async-done | bytes 524304 | tf_op jit(solution)/shard_map/reduce_scatter | solution.py:95
  209.2 0.0 copy-done.2
  209.2 2.2 fusion.18
  211.4 20.1 %psum.31 = f32[1024]{0:T(1024)S(1)} all-reduce(f32[1024]{0:T(1024)S(1)} %get-tuple-element.22), channel_id=1, replica_groups=mesh['user'=8,'item'=4] {'user'}, use_global_device_ids=true, to_apply=%region_11.12 | all-reduce | flops 1024 | bytes 8192 | tf_op jit(solution)/shard_map/psum | solution.py:101
  231.4 0.6 broadcast_add_fusion.1
  232.0 50.5 %reduce-scatter.3.cloned.1.call-done = f32[2048,256]{1,0:T(8,128)} async-done(((f32[2048,1024]{1,0:T(8,128)}), f32[2048,256]{1,0:T(8,128)}) %reduce-scatter.3.cloned.1.call-update) | async-done | bytes 2097168 | tf_op jit(solution)/shard_map/reduce_scatter | solution.py:89
  282.5 0.0 copy-done.1
  282.5 4.3 %fusion.11 = (f32[2048]{0:T(1024)S(1)}, f32[2048,256]{1,0:T(8,128)}, f32[2048,256]{1,0:T(8,128)}) fusion(f32[256]{0:T(256)S(1)} %dynamic_slice.6, f32[2048]{0:T(1024)S(1)} %broadcast_divide_fusion, f32[2048,256]{1,0:T(8,128)} %reduce-scatter.3.cloned.1.call-done, bf16[2048,256]{1,0:T(8,128)(2,1)S(1)} %copy-done.1), kind=kLoop, calls=%fused_computation.18 | loop fusion | flops 3143680 | bytes 7357440 | tf_op jit(solution)/shard_map/reduce_sum | solution.py:93
  286.8 5.8 %psum.30 = f32[2048]{0:T(1024)S(1)} all-reduce(f32[2048]{0:T(1024)S(1)} %get-tuple-element.24), channel_id=1, replica_groups=mesh['user'=8,'item'=4] {'item'}, use_global_device_ids=true, to_apply=%region_8.9 | all-reduce | flops 2048 | bytes 16384 | tf_op jit(solution)/shard_map/psum | solution.py:94
  292.7 0.6 broadcast_add_fusion
  (8 shorter events, 0.0 us)
Async XLA Ops:
  7.2 81.8 %all-gather.3.cloned.1.call-start = ((), (), s32[]{:S(2)}) async-start(), calls=%async_computation.2 | async-start | bytes 2359296 | tf_op jit(solution)/shard_map/all_gather | solution.py:67
  12.7 63.8 %copy-start.5 = (s32[1,1,32]{2,1,0:T(1,128)S(1)}, s32[1,1,32]{2,1,0:T(1,128)}, u32[]{:S(2)}) copy-start(s32[1,1,32]{2,1,0:T(1,128)} %param.15) | copy-start | bytes 388
  12.7 89.0 %all-gather.5.cloned.1.call-start = ((), (), s32[]{:S(2)}) async-start(), calls=%async_computation.3 | async-start | bytes 5242880 | tf_op jit(solution)/shard_map/all_gather | solution.py:66
  29.8 179.4 %reduce-scatter.5.cloned.1.call-start = ((), (), s32[]{:S(2)}) async-start(), calls=%async_computation.5 | async-start | bytes 4718592 | tf_op jit(solution)/shard_map/reduce_scatter | solution.py:95
  110.4 2.5 copy-start
  110.4 3.7 %copy-start.6 = (bf16[2048,1024]{1,0:T(8,128)(2,1)S(1)}, bf16[2048,1024]{1,0:T(8,128)(2,1)}, u32[]{:S(2)}) copy-start(bf16[2048,1024]{1,0:T(8,128)(2,1)} %all-gather.5.cloned.1.call-done) | copy-start | bytes 12582916
  120.3 162.2 %reduce-scatter.3.cloned.1.call-start = ((), (), s32[]{:S(2)}) async-start(), calls=%async_computation.4 | async-start | bytes 10485760 | tf_op jit(solution)/shard_map/reduce_scatter | solution.py:89
  120.6 6.4 %copy-start.7 = (bf16[1024,1024]{1,0:T(8,128)(2,1)S(1)}, bf16[1024,1024]{1,0:T(8,128)(2,1)}, u32[]{:S(2)}) copy-start(bf16[1024,1024]{1,0:T(8,128)(2,1)} %all-gather.3.cloned.1.call-done) | copy-start | bytes 6291460
  136.2 0.7 copy-start.4
  136.2 0.7 copy-start.3
  136.2 73.1 %copy-start.2 = (bf16[1024,128]{1,0:T(8,128)(2,1)S(1)}, bf16[1024,128]{1,0:T(8,128)(2,1)}, u32[]{:S(2)}) copy-start(bf16[1024,128]{1,0:T(8,128)(2,1)} %get-tuple-element.28) | copy-start | bytes 786436
  136.2 146.3 %copy-start.1 = (bf16[2048,256]{1,0:T(8,128)(2,1)S(1)}, bf16[2048,256]{1,0:T(8,128)(2,1)}, u32[]{:S(2)}) copy-start(bf16[2048,256]{1,0:T(8,128)(2,1)} %get-tuple-element.13) | copy-start | bytes 3145732
Sparse Core Ops, SparseCore 0:
  12.8 53.4 all-gather.2
  68.4 33.2 all-gather.4
  120.4 88.7 reduce-scatter.4
  211.6 70.8 reduce-scatter.2

commit v3 on v2

--- a/solution.py
+++ b/solution.py
@@ -33,6 +33,24 @@
     grid = jnp.take(count_tiles, source, axis=0)
     grid = jnp.where(present[:, None, None], grid, jnp.zeros_like(grid))
     return grid.reshape(UB, IB, BLK, BLK)
+
+
+def halving_reduce_scatter(partial, axis_name, width, index):
+    rows, columns = partial.shape
+    block = columns // width
+    held = partial.reshape(rows, width, block)
+    bit = 0
+    while (1 << bit) < width:
+        groups = held.shape[1] // 2
+        pairs = held.reshape(rows, groups, 2, block)
+        own_bit = (index >> bit) & 1
+        keep = lax.dynamic_index_in_dim(pairs, own_bit, axis=2, keepdims=False)
+        send = lax.dynamic_index_in_dim(pairs, 1 - own_bit, axis=2, keepdims=False)
+        step = 1 << bit
+        perm = [(i, i ^ step) for i in range(width)]
+        held = keep + lax.ppermute(send, axis_name, perm)
+        bit += 1
+    return held.reshape(rows, block)
 
 
 def on_device(
@@ -86,7 +104,7 @@
     user_acc = user_acc.reshape(user_rows, factors)
     item_acc = item_acc.reshape(item_rows, factors)
     xi_mean = (prior_a2 + factors * prior_a) / xi_rate
-    user_share = lax.psum_scatter(user_acc, "item", scatter_dimension=1, tiled=True)
+    user_share = halving_reduce_scatter(user_acc, "item", item_width, item_index)
     theta_shape_new = prior_a + theta_part.astype(jnp.float32) * user_share
     beta_slice = lax.dynamic_slice_in_dim(beta_total, item_index * theta_columns, theta_columns, 0)
     theta_rate_new = xi_mean[:, None] + beta_slice[None, :]

time: 301 us -> 250 us (0.83)
  waiting for transfers between devices: 136 us -> 57.3 us
  local copies, waits for them, and re-layouts: 22.9 us -> 46.7 us
  other arithmetic: 30.9 us -> 35.2 us
    reduce_scatter x1, waiting for transfers between devices: 72.3 us -> 0.01 us  [on_device(): lax.psum_scatter(item_acc, 'user', scatter_dimension=1, tiled=True)]
    reduce_scatter x1 -> x0, waiting for transfers between devices: 50.5 us -> none  [on_device(): lax.psum_scatter(user_acc, 'item', scatter_dimension=1, tiled=True)]
    ppermute x0 -> x2, waiting for transfers between devices: none -> 49.1 us  [halving_reduce_scatter(): held = keep + lax.ppermute(send, axis_name, perm)]
    dynamic_slice x0 -> x3, local copies, waits for them, and re-layouts: none -> 14.7 us  [the longest x2 9.27 us: halving_reduce_scatter(): keep = lax.dynamic_index_in_dim(pairs, own_bit, axis=2, keepdims=False)]
    all_gather x1, waiting for transfers between devices: 12.8 us -> 8.07 us  [on_device(): theta_full = lax.all_gather(theta_part, 'item', axis=1, tiled=True)]
    dot_general x1 -> x2, local copies, waits for them, and re-layouts: 6.37 us -> 10.9 us  [on_device(): jnp.einsum('bjui,jik->buk', ratio, beta_blocks, preferred_element_type=jn...]
    add x0 -> x1, other arithmetic: none -> 4.23 us  [halving_reduce_scatter(): held = keep + lax.ppermute(send, axis_name, perm)]
  transfers between devices with their start and end apart: 4 -> 5, of which waited for: 3 -> 3; matrix products, arithmetic and copies ran while one was open for 16% -> 27% of each run, Pallas kernels for 0% -> 0%
where the time goes in v3:
time: 250 us; the launch traced here: 249 us
  blocking collectives  72.9 us (29%)
  waiting for transfers between devices  57.3 us (23%)
  local copies, waits for them, and re-layouts  46.7 us (19%)
  other arithmetic  35.2 us (14%)
  matrix products  21.7 us (9%)
  between operations  14.5 us (6%)
    ppermute x2, waiting for transfers between devices, halving_reduce_scatter(): held = keep + lax.ppermute(send, axis_name, perm)  49.1 us
    psum x1, blocking collectives, on_device(): lax.psum((beta_placed, theta_placed), ('user', 'item'))  45.5 us
    psum x1, blocking collectives, on_device(): eta_rate_new = prior_c2 / prior_d2 + lax.psum(item_part, 'user')  21.2 us
    reduce_sum x1, other arithmetic, on_device(): theta_local = jnp.sum(theta_shape / theta_rate, axis=0)  17 us
    gather x2, local copies, waits for them, and re-layouts, dense_counts(): grid = jnp.take(count_tiles, source, axis=0)  11.3 us
    dot_general x2, local copies, waits for them, and re-layouts, on_device(): jnp.einsum('bjui,jik->buk', ratio, beta_blocks, preferred_element_type=jn...  10.9 us
    dynamic_slice x2, local copies, waits for them, and re-layouts, halving_reduce_scatter(): keep = lax.dynamic_index_in_dim(pairs, own_bit, axis=2, keepdims=False)  9.27 us
    dot_general x1, matrix products, on_device(): jnp.einsum('buk,jik->bjui', theta_blocks, beta_blocks, preferred_element_...  8.98 us
  transfers between devices with their start and end apart: 5, of which 3 were waited for; matrix products, arithmetic and copies ran while one was open for 27% of the time, Pallas kernels for 0%

profile of v3, /device:TPU:0, one launch (start us, length us, event | category | flops | bytes accessed | tf_op | source)
XLA Modules:
  0.0 249.1 jit_solution(7248290899947394698)
XLA Ops:
  7.2 0.0 all-gather.3.cloned.1.call-start
  7.2 5.4 %fusion.19 = (bf16[1024,128]{1,0:T(8,128)(2,1)}, f32[128]{0:T(128)S(1)}) fusion(f32[1024,128]{1,0:T(8,128)} %param.13, f32[1024,128]{1,0:T(8,128)} %param.12), kind=kLoop, calls=%fused_computation.31 | loop fusion | flops 10354560 | bytes 1311232 | tf_op jit(solution)/shard_map/convert_element_type | solution.py:21
  12.7 0.0 all-gather.3.cloned.1.call-update
  12.7 0.0 copy-start.7
  12.7 0.0 all-gather.5.cloned.1.call-start
  12.7 17.0 %divide_reduce_fusion = (f32[256]{0:T(256)S(1)}, bf16[2048,256]{1,0:T(8,128)(2,1)}) fusion(f32[2048,256]{1,0:T(8,128)} %param.9, f32[2048,256]{1,0:T(8,128)} %param.10), kind=kLoop, calls=%fused_computation.20 | loop fusion | flops 41418496 | bytes 5243904 | tf_op jit(solution)/shard_map/reduce_sum | solution.py:77
  29.8 0.0 all-gather.5.cloned.1.call-update
  29.8 0.0 reduce-scatter.2.cloned.1.call-start
  29.9 0.3 dynamic_update_slice.7
  30.1 0.2 dynamic_update_slice.6
  30.4 45.5 %all-reduce = (f32[1024]{0:T(1024)S(1)}, f32[1024]{0:T(1024)S(1)}) all-reduce(f32[1024]{0:T(1024)S(1)} %dynamic_update_slice.6, f32[1024]{0:T(1024)S(1)} %dynamic_update_slice.7), channel_id=1, replica_groups=mesh['user'=8,'item'=4] {'user','item'}, use_global_device_ids=true, to_apply=%region_4.0 | all-reduce | flops 2048 | bytes 16384 | tf_op jit(solution)/shard_map/psum | solution.py:89
  76.5 0.0 copy-done.7
  76.5 0.6 iota_reduce_fusion
  77.2 5.1 %gather_fusion = bf16[32,256,256]{2,1,0:T(8,128)(2,1)} fusion(bf16[32,256,256]{2,1,0:T(8,128)(2,1)} %bitcast.49, s32[1024]{0:T(1024)S(1)} %pad_clamp_fusion), kind=kCustom, calls=%fused_computation | custom fusion | bytes 8388736 | tf_op jit(solution)/shard_map/jit(_take)/gather | solution.py:33
  82.2 6.2 %copy.29 = bf16[8,4,256,256]{2,3,0,1:T(8,128)(2,1)} copy(bf16[8,4,256,256]{3,2,1,0:T(8,128)(2,1)} %bitcast.48) | data formatting | bytes 8388608 | tf_op jit(solution)/shard_map/jit(_take)/gather | solution.py:33
  88.4 0.1 broadcast_in_dim.36
  88.5 0.1 copy.28
  88.6 0.1 fusion.23
  88.7 0.1 broadcast_in_dim.34
  88.8 0.1 copy.27
  88.9 0.0 all-gather.3.cloned.1.call-done
  88.9 0.0 copy-start.3
  88.9 4.7 %dot_general.25 = bf16[2,2,256,256,4]{2,1,0,3,4:T(2,128)(2,1)} reshape(bf16[1024,256,4]{0,1,2:T(8,128)(2,1)} %bitcast.53) | data formatting | bytes 4194304 | tf_op jit(solution)/shard_map/bjui,jik->buk/dot_general | solution.py:102
  93.6 8.1 %all-gather.5.cloned.1.call-done = bf16[2048,1024]{1,0:T(8,128)(2,1)} async-done(((bf16[2048,256]{1,0:T(8,128)(2,1)}), bf16[2048,1024]{1,0:T(8,128)(2,1)}) %all-gather.5.cloned.1.call-update) | async-done | bytes 4194320 | tf_op jit(solution)/shard_map/all_gather | solution.py:84
  101.7 0.0 copy-done.3
  101.7 9.0 %fusion = bf16[8,4,256,256]{2,3,0,1:T(8,128)(2,1)} fusion(bf16[8,4,256,256]{2,3,0,1:T(8,128)(2,1)} %copy.29, pred[8,4]{0,1:T(4,128)(4,1)S(1)} %copy.28, pred[8,4]{0,1:T(4,128)(4,1)S(1)} %copy.27, bf16[4,256,1024,1]{2,1,3,0:T(8,128)(2,1)S(1)} %bitcast.54, bf16[8,256,1024,1]{2,1,0,3:T(8,128)(2,1)} %bitcast.57), kind=kOutput, calls=%fused_computation.2 | convolution fusion | flops 4305453056 | bytes 14680128 | tf_op jit(solution)/shard_map/buk,jik->bjui/dot_general | solution.py:98
  110.7 6.2 %copy.30 = bf16[8,256,256,4]{2,1,0,3:T(8,128)(2,1)} copy(bf16[8,256,256,4]{1,2,0,3:T(8,128)(2,1)} %bitcast.46) | data formatting | bytes 8388608 | tf_op jit(solution)/shard_map/bjui,jik->buk/dot_general | solution.py:102
  116.9 0.0 copy-start.8
  116.9 4.7 %copy.34 = bf16[4,256,8,256]{3,2,1,0:T(8,128)(2,1)S(1)} copy(bf16[4,256,8,256]{3,1,2,0:T(8,128)(2,1)} %bitcast.47) | data formatting | bytes 8388608 | tf_op jit(solution)/shard_map/bjui,buk->jik/dot_general | solution.py:103
  121.6 0.0 copy-done.8
  121.6 6.2 %fusion.3 = f32[1024,1024]{1,0:T(8,128)} fusion(bf16[8,256,1024]{2,1,0:T(8,128)(2,1)S(1)} %bitcast.58, bf16[1024,8,256]{2,1,0:T(8,128)(2,1)S(1)} %bitcast.52), kind=kOutput, calls=%fused_computation.11 | convolution fusion | flops 4294967296 | bytes 12582912 | tf_op jit(solution)/shard_map/bjui,buk->jik/dot_general | solution.py:103
  127.8 0.0 copy-start.4
  127.8 0.0 reduce-scatter.2.cloned.1.call-update
  127.8 1.6 copy-done.4
  129.4 6.6 %convolution_bitcast_fusion = f32[2048,2,2,256]{0,3,2,1:T(8,128)S(1)} fusion(bf16[2048,256,4,1,1]{1,0,2,4,3:T(8,128)(2,1)} %bitcast.51, bf16[2,2,256,256,4]{2,1,0,3,4:T(2,128)(2,1)S(1)} %copy-done.4), kind=kOutput, calls=%fused_computation.3 | convolution fusion | flops 4294967296 | bytes 14680064 | tf_op jit(solution)/shard_map/bjui,jik->buk/dot_general | solution.py:102
  136.0 3.8 %constant_dynamic-slice_fusion.2 = (f32[2048,2,1,256]{0,3,2,1:T(8,128)}, f32[2048,2,1,256]{0,3,2,1:T(8,128)}) fusion(f32[2048,2,2,256]{0,3,2,1:T(8,128)S(1)} %convolution_bitcast_fusion, s32[]{:T(128)S(6)} %select_n.46, s32[]{:T(128)S(6)} %select_n.47), kind=kLoop, calls=%fused_computation.49 | loop fusion | bytes 16777224 | tf_op jit(solution)/shard_map/jit(dynamic_index_in_dim)/dynamic_slice | solution.py:47
  139.8 5.4 %copy.33 = f32[2048,2,1,256]{3,0,2,1:T(8,128)} copy(f32[2048,2,1,256]{0,3,2,1:T(8,128)} %get-tuple-element.27) | data formatting | bytes 8388608 | tf_op jit(solution)/shard_map/jit(dynamic_index_in_dim)/dynamic_slice | solution.py:48
  145.2 0.2 collective-permute-start
  145.4 5.5 %copy.32 = f32[2048,2,1,256]{3,0,2,1:T(8,128)} copy(f32[2048,2,1,256]{0,3,2,1:T(8,128)} %get-tuple-element.26) | data formatting | bytes 8388608 | tf_op jit(solution)/shard_map/jit(dynamic_index_in_dim)/dynamic_slice | solution.py:47
  150.9 1.8 collective-permute-done
  152.7 4.2 %bitcast_add_fusion = f32[2048,2,256]{2,0,1:T(8,128)S(1)} fusion(f32[2048,2,256]{2,0,1:T(8,128)} %collective-permute-done, f32[2048,2,1,256]{3,0,2,1:T(8,128)} %copy.32), kind=kLoop, calls=%fused_computation.4 | loop fusion | flops 1048576 | bytes 12582912 | tf_op jit(solution)/shard_map/add | solution.py:51
  156.9 0.0 copy-start
  156.9 0.0 copy-start.6
  156.9 0.0 copy-start.5
  157.0 0.0 copy-start.1
  157.0 1.5 constant_dynamic-slice_fusion
  158.4 1.1 copy-done
  159.5 0.5 collective-permute-start.1
  160.0 0.1 dynamic_slice.18
  160.1 0.1 dynamic_slice.19
  160.2 0.0 copy-done.6
  160.2 0.0 copy-done.5
  160.2 0.0 copy-start.2
  160.2 47.3 %collective-permute-done.1 = f32[2048,1,256]{2,0,1:T(8,128)S(1)} collective-permute-done((f32[2048,1,256]{2,0,1:T(8,128)}, f32[2048,1,256]{2,0,1:T(8,128)S(1)}, u32[]{:S(2)}, u32[]{:S(2)}) %collective-permute-start.1) | collective-permute-done | bytes 2097184 | tf_op jit(solution)/shard_map/ppermute | solution.py:51
  207.5 0.0 copy-done.1
  207.5 4.3 %fusion.13 = (f32[2048]{0:T(1024)S(1)}, f32[2048,256]{1,0:T(8,128)}, f32[2048,256]{1,0:T(8,128)}) fusion(f32[256]{0:T(256)S(1)} %dynamic_slice.18, f32[2048]{0:T(1024)S(1)} %broadcast_divide_fusion, f32[2048,1,256]{2,0,1:T(8,128)S(1)} %collective-permute-done.1, f32[2048,2,256]{2,0,1:T(8,128)} %copy-done, s32[]{:T(128)S(6)} %select_n.48, ...), kind=kLoop, calls=%fused_computation.21 | loop fusion | flops 3667968 | bytes 9454596 | tf_op jit(solution)/shard_map/reduce_sum | solution.py:111
  211.8 6.2 %psum.30 = f32[2048]{0:T(1024)S(1)} all-reduce(f32[2048]{0:T(1024)S(1)} %get-tuple-element.24), channel_id=1, replica_groups=mesh['user'=8,'item'=4] {'item'}, use_global_device_ids=true, to_apply=%region_7.8 | all-reduce | flops 2048 | bytes 16384 | tf_op jit(solution)/shard_map/psum | solution.py:112
  218.0 0.6 broadcast_add_fusion
  218.6 0.0 reduce-scatter.2.cloned.1.call-done
  218.6 0.0 copy-done.2
  218.6 2.2 fusion.20
  220.8 21.2 %psum.31 = f32[1024]{0:T(1024)S(1)} all-reduce(f32[1024]{0:T(1024)S(1)} %get-tuple-element.22), channel_id=1, replica_groups=mesh['user'=8,'item'=4] {'user'}, use_global_device_ids=true, to_apply=%region_10.11 | all-reduce | flops 1024 | bytes 8192 | tf_op jit(solution)/shard_map/psum | solution.py:119
  242.0 0.6 broadcast_add_fusion.1
  (8 shorter events, 0.0 us)
Async XLA Ops:
  7.2 81.8 %all-gather.3.cloned.1.call-start = ((), (), s32[]{:S(2)}) async-start(), calls=%async_computation.1 | async-start | bytes 2359296 | tf_op jit(solution)/shard_map/all_gather | solution.py:85
  12.7 63.8 %copy-start.7 = (s32[1,1,32]{2,1,0:T(1,128)S(1)}, s32[1,1,32]{2,1,0:T(1,128)}, u32[]{:S(2)}) copy-start(s32[1,1,32]{2,1,0:T(1,128)} %param.15) | copy-start | bytes 388
  12.7 89.0 %all-gather.5.cloned.1.call-start = ((), (), s32[]{:S(2)}) async-start(), calls=%async_computation.2 | async-start | bytes 5242880 | tf_op jit(solution)/shard_map/all_gather | solution.py:84
  29.8 188.8 %reduce-scatter.2.cloned.1.call-start = ((), (), s32[]{:S(2)}) async-start(), calls=%async_computation.3 | async-start | bytes 4718592 | tf_op jit(solution)/shard_map/reduce_scatter | solution.py:113
  88.9 12.8 %copy-start.3 = (bf16[1024,1024]{1,0:T(8,128)(2,1)S(1)}, bf16[1024,1024]{1,0:T(8,128)(2,1)}, u32[]{:S(2)}) copy-start(bf16[1024,1024]{1,0:T(8,128)(2,1)} %all-gather.3.cloned.1.call-done) | copy-start | bytes 6291460
  116.9 4.7 %copy-start.8 = (bf16[2048,1024]{1,0:T(8,128)(2,1)S(1)}, bf16[2048,1024]{1,0:T(8,128)(2,1)}, u32[]{:S(2)}) copy-start(bf16[2048,1024]{1,0:T(8,128)(2,1)} %all-gather.5.cloned.1.call-done) | copy-start | bytes 12582916
  127.8 1.6 copy-start.4
  145.2 7.5 %collective-permute-start = (f32[2048,2,256]{2,0,1:T(8,128)}, f32[2048,2,256]{2,0,1:T(8,128)}, u32[]{:S(2)}, u32[]{:S(2)}) collective-permute-start(f32[2048,2,256]{2,0,1:T(8,128)} %bitcast.50), channel_id=1, source_target_pairs={{0,1},{1,0},{2,3},{3,2},{4,5},{5,4},{6,7},{7,6},{8,9},{9,8},{10,11... | collective-permute-start | bytes 12582920 | tf_op jit(solution)/shard_map/ppermute | solution.py:51
  156.9 2.6 %copy-start = (f32[2048,2,256]{2,0,1:T(8,128)}, f32[2048,2,256]{2,0,1:T(8,128)S(1)}, u32[]{:S(2)}) copy-start(f32[2048,2,256]{2,0,1:T(8,128)S(1)} %bitcast_add_fusion) | copy-start | bytes 12582916
  156.9 3.2 %copy-start.6 = (f32[1024]{0:T(1024)S(1)}, f32[1024]{0:T(1024)}, u32[]{:S(2)}) copy-start(f32[1024]{0:T(1024)} %param.14) | copy-start | bytes 12292
  156.9 3.2 %copy-start.5 = (f32[2048]{0:T(1024)S(1)}, f32[2048]{0:T(1024)}, u32[]{:S(2)}) copy-start(f32[2048]{0:T(1024)} %param.11) | copy-start | bytes 24580
  157.0 50.6 %copy-start.1 = (bf16[2048,256]{1,0:T(8,128)(2,1)S(1)}, bf16[2048,256]{1,0:T(8,128)(2,1)}, u32[]{:S(2)}) copy-start(bf16[2048,256]{1,0:T(8,128)(2,1)} %get-tuple-element.13) | copy-start | bytes 3145732
  159.5 48.0 %collective-permute-start.1 = (f32[2048,1,256]{2,0,1:T(8,128)}, f32[2048,1,256]{2,0,1:T(8,128)S(1)}, u32[]{:S(2)}, u32[]{:S(2)}) collective-permute-start(f32[2048,1,256]{2,0,1:T(8,128)} %constant_dynamic-slice_fusion), channel_id=1, source_target_pairs={{0,2},{1,3},{2,0},{3,1},{4,6},{5,7},{6,4},{7,5},{8,10},{9,11},{10,... | collective-permute-start | bytes 6291464 | tf_op jit(solution)/shard_map/ppermute | solution.py:51
  160.2 58.4 %copy-start.2 = (bf16[1024,128]{1,0:T(8,128)(2,1)S(1)}, bf16[1024,128]{1,0:T(8,128)(2,1)}, u32[]{:S(2)}) copy-start(bf16[1024,128]{1,0:T(8,128)(2,1)} %get-tuple-element.30) | copy-start | bytes 786436
Sparse Core Ops, SparseCore 0:
  12.8 53.4 all-gather.2
  68.4 33.2 all-gather.4
  128.0 88.7 reduce-scatter.1

commit v4 on v2

--- a/solution.py
+++ b/solution.py
@@ -33,6 +33,44 @@
     grid = jnp.take(count_tiles, source, axis=0)
     grid = jnp.where(present[:, None, None], grid, jnp.zeros_like(grid))
     return grid.reshape(UB, IB, BLK, BLK)
+
+
+def halving_order(width):
+    order = [0]
+    step = width
+    while step > 1:
+        step //= 2
+        order = [c ^ step for c in order] + order
+    return order
+
+
+def halving_user_sums(ratio, beta_full, width, index, axis_name):
+    items, factors = beta_full.shape
+    block = factors // width
+    order = jnp.asarray(halving_order(width), jnp.int32) ^ index
+    beta_ordered = jnp.take(beta_full.reshape(items, width, block), order, axis=1)
+    sizes = []
+    size = width
+    while size > 1:
+        size //= 2
+        sizes.append(size)
+    sizes.append(1)
+    terms = []
+    first = 0
+    for size in sizes:
+        piece = beta_ordered[:, first : first + size].reshape(items, size * block)
+        terms.append(jnp.dot(ratio, piece, preferred_element_type=jnp.float32))
+        first += size
+    for step_index in range(len(sizes) - 1):
+        partner = 1 << step_index
+        perm = [(i, i ^ partner) for i in range(width)]
+        received = lax.ppermute(terms[step_index], axis_name, perm)
+        offset = 0
+        for later in range(step_index + 1, len(sizes)):
+            span = terms[later].shape[1]
+            terms[later] = terms[later] + received[:, offset : offset + span]
+            offset += span
+    return terms[-1]
 
 
 def on_device(
@@ -74,19 +112,17 @@
     )
     user_rows = theta_full.shape[0]
     item_rows = beta_full.shape[0]
-    theta_blocks = theta_full.reshape(UB, BLK, factors)
-    beta_blocks = beta_full.reshape(IB, BLK, factors)
-    counts = dense_counts(tile_slots, tile_counts, live_tiles).astype(jnp.float32)
-    denominator = jnp.einsum(
-        "buk,jik->bjui", theta_blocks, beta_blocks, preferred_element_type=jnp.float32
+    grid = dense_counts(tile_slots, tile_counts, live_tiles)
+    counts = grid.transpose(0, 2, 1, 3).reshape(user_rows, item_rows).astype(jnp.float32)
+    denominator = lax.dot_general(
+        theta_full, beta_full, (((1,), (1,)), ((), ())), preferred_element_type=jnp.float32
     )
     ratio = (counts / denominator).astype(jnp.bfloat16)
-    user_acc = jnp.einsum("bjui,jik->buk", ratio, beta_blocks, preferred_element_type=jnp.float32)
-    item_acc = jnp.einsum("bjui,buk->jik", ratio, theta_blocks, preferred_element_type=jnp.float32)
-    user_acc = user_acc.reshape(user_rows, factors)
-    item_acc = item_acc.reshape(item_rows, factors)
+    item_acc = lax.dot_general(
+        ratio, theta_full, (((0,), (0,)), ((), ())), preferred_element_type=jnp.float32
+    )
     xi_mean = (prior_a2 + factors * prior_a) / xi_rate
-    user_share = lax.psum_scatter(user_acc, "item", scatter_dimension=1, tiled=True)
+    user_share = halving_user_sums(ratio, beta_full, item_width, item_index, "item")
     theta_shape_new = prior_a + theta_part.astype(jnp.float32) * user_share
     beta_slice = lax.dynamic_slice_in_dim(beta_total, item_index * theta_columns, theta_columns, 0)
     theta_rate_new = xi_mean[:, None] + beta_slice[None, :]

time: 301 us -> 240 us (0.80)
  waiting for transfers between devices: 136 us -> 62.2 us
  local copies, waits for them, and re-layouts: 22.9 us -> 29.8 us
  other arithmetic: 30.9 us -> 36.5 us
    reduce_scatter x1, waiting for transfers between devices: 72.3 us -> 10.6 us  [on_device(): lax.psum_scatter(item_acc, 'user', scatter_dimension=1, tiled=True)]
    ppermute x0 -> x2, waiting for transfers between devices: none -> 51.6 us  [halving_user_sums(): received = lax.ppermute(terms[step_index], axis_name, perm)]
    reduce_scatter x1 -> x0, waiting for transfers between devices: 50.5 us -> none  [on_device(): lax.psum_scatter(user_acc, 'item', scatter_dimension=1, tiled=True)]
    convert_element_type x1 -> x2, other arithmetic: 5.45 us -> 22.3 us  [exp_mean_log(): jnp.exp(lax.digamma(shape_param) - jnp.log(rate_param)).astype(jnp.bfloat16)]
    unnamed x16 -> x31, local copies, waits for them, and re-layouts: 1.76 us -> 18.1 us
    reduce_sum x1, other arithmetic: 17 us -> 1.96 us  [on_device(): theta_local = jnp.sum(theta_shape / theta_rate, axis=0)]
    all_gather x1, waiting for transfers between devices: 12.8 us -> 0.02 us  [on_device(): theta_full = lax.all_gather(theta_part, 'item', axis=1, tiled=True)]
    dot_general x2 -> x0, local copies, waits for them, and re-layouts: 8.84 us -> none  [the longest x1 6.37 us: on_device(): jnp.einsum('bjui,jik->buk', ratio, beta_blocks, preferred_element_type=jn...]
  transfers between devices with their start and end apart: 4 -> 5, of which waited for: 3 -> 3; matrix products, arithmetic and copies ran while one was open for 16% -> 26% of each run, Pallas kernels for 0% -> 0%
where the time goes in v4:
time: 240 us; the launch traced here: 239 us
  blocking collectives  69.7 us (29%)
  waiting for transfers between devices  62.2 us (26%)
  other arithmetic  36.5 us (15%)
  local copies, waits for them, and re-layouts  29.8 us (12%)
  matrix products  23.8 us (10%)
  between operations  14.7 us (6%)
  starting transfers between devices  2.72 us (1%)
    ppermute x2, waiting for transfers between devices, halving_user_sums(): received = lax.ppermute(terms[step_index], axis_name, perm)  51.6 us
    psum x1, blocking collectives, on_device(): lax.psum((beta_placed, theta_placed), ('user', 'item'))  42.9 us
    convert_element_type x2, other arithmetic, exp_mean_log(): jnp.exp(lax.digamma(shape_param) - jnp.log(rate_param)).astype(jnp.bfloat16)  22.3 us
    psum x1, blocking collectives, on_device(): eta_rate_new = prior_c2 / prior_d2 + lax.psum(item_part, 'user')  20 us
    unnamed x31, local copies, waits for them, and re-layouts  18.1 us
    reduce_scatter x1, waiting for transfers between devices, on_device(): lax.psum_scatter(item_acc, 'user', scatter_dimension=1, tiled=True)  10.6 us
    dot_general x1, matrix products, on_device(): lax.dot_general(theta_full, beta_full, (((1,), (1,)), ((), ())), preferre...  10.3 us
    dot_general x3, matrix products, halving_user_sums(): terms.append(jnp.dot(ratio, piece, preferred_element_type=jnp.float32))  7.35 us
  transfers between devices with their start and end apart: 5, of which 3 were waited for; matrix products, arithmetic and copies ran while one was open for 26% of the time, Pallas kernels for 0%

profile of v4, /device:TPU:0, one launch (start us, length us, event | category | flops | bytes accessed | tf_op | source)
XLA Modules:
  0.0 239.4 jit_solution(16811132625226433610)
XLA Ops:
  7.2 0.0 all-gather.5.cloned.1.call-start
  7.2 5.4 %fusion.16 = (bf16[1024,128]{1,0:T(8,128)(2,1)}, f32[128]{0:T(128)S(1)}) fusion(f32[1024,128]{1,0:T(8,128)} %param.14, f32[1024,128]{1,0:T(8,128)} %param.13), kind=kLoop, calls=%fused_computation.33 | loop fusion | flops 10354560 | bytes 1311232 | tf_op jit(solution)/shard_map/convert_element_type | solution.py:21
  12.7 0.0 all-gather.5.cloned.1.call-update
  12.7 0.0 copy-start.4
  12.7 0.0 all-gather.3.cloned.1.call-start
  12.7 3.0 %copy.64 = f32[2048,256]{0,1:T(8,128)} copy(f32[2048,256]{1,0:T(8,128)} %param.10) | data formatting | bytes 4194304 | tf_op args[0]
  15.8 0.0 copy-done.4
  15.8 1.8 copy.73
  17.6 16.8 %fusion.6 = bf16[2048,256]{0,1:T(8,128)(2,1)} fusion(f32[2048,256]{0,1:T(8,128)} %copy.73, f32[2048,256]{0,1:T(8,128)} %copy.64), kind=kLoop, calls=%fused_computation.14 | loop fusion | flops 40370176 | bytes 5242880 | tf_op jit(solution)/shard_map/convert_element_type | solution.py:21
  34.4 0.0 all-gather.3.cloned.1.call-update
  34.4 0.0 reduce-scatter.2.cloned.1.call-start
  34.5 0.0 copy-done.3
  34.5 0.0 copy-start.10
  34.5 2.0 divide_reduce_fusion
  36.5 0.2 dynamic_update_slice.7
  36.7 0.2 dynamic_update_slice.6
  36.9 42.9 %all-reduce = (f32[1024]{0:T(1024)S(1)}, f32[1024]{0:T(1024)S(1)}) all-reduce(f32[1024]{0:T(1024)S(1)} %dynamic_update_slice.6, f32[1024]{0:T(1024)S(1)} %dynamic_update_slice.7), channel_id=1, replica_groups=mesh['user'=8,'item'=4] {'user','item'}, use_global_device_ids=true, to_apply=%region_4.0 | all-reduce | flops 2048 | bytes 16384 | tf_op jit(solution)/shard_map/psum | solution.py:109
  80.5 0.0 copy-done.10
  80.5 0.8 iota_reduce_fusion
  81.3 0.1 broadcast_in_dim.48
  81.4 0.1 fusion.22
  81.5 0.1 broadcast_in_dim.46
  81.7 4.9 %gather_fusion = bf16[32,256,256]{2,1,0:T(8,128)(2,1)} fusion(bf16[32,256,256]{2,1,0:T(8,128)(2,1)} %bitcast.36, s32[1024]{0:T(1024)S(1)} %pad_clamp_fusion.1), kind=kCustom, calls=%fused_computation | custom fusion | bytes 8388736 | tf_op jit(solution)/shard_map/jit(_take)/gather | solution.py:33
  86.6 5.4 %fusion.1 = f32[8,4,256,256]{3,1,2,0:T(4,128)S(1)} fusion(bf16[8,4,256,256]{3,2,1,0:T(8,128)(2,1)} %bitcast.33, pred[8,4]{1,0:T(8,128)(4,1)S(1)} %broadcast_in_dim.48, pred[8,4]{1,0:T(8,128)(4,1)S(1)} %broadcast_in_dim.46), kind=kLoop, calls=%fused_computation.5 | loop fusion | flops 6291456 | bytes 12582976 | tf_op jit(solution)/shard_map/convert_element_type | solution.py:116
  92.0 0.0 copy-start.11
  92.0 5.3 %copy.84 = f32[256,8,4,256]{3,1,2,0:T(8,128)} copy(f32[256,8,4,256]{3,2,1,0:T(4,128)S(1)} %bitcast.32) | data formatting | bytes 16777216
  97.3 0.0 copy-done.11
  97.4 0.0 all-gather.5.cloned.1.call-done
  97.4 3.1 %copy.91 = bf16[128,4,8,256]{3,2,0,1:T(8,128)(2,1)} copy(bf16[128,4,8,256]{3,2,1,0:T(8,128)(2,1)} %bitcast.37) | data formatting | bytes 4194304 | tf_op jit(solution)/shard_map/reshape | solution.py:51
  100.5 2.3 gather_fusion.1
  102.8 0.0 all-gather.3.cloned.1.call-done
  102.8 0.0 copy-start.12
  102.8 10.3 %divide_convert_fusion = bf16[2048,1024]{1,0:T(8,128)(2,1)S(1)} fusion(f32[2048,1024]{1,0:T(8,128)} %bitcast.34, bf16[2048,1024]{0,1:T(8,128)(2,1)} %all-gather.3.cloned.1.call-done, bf16[1024,1024]{1,0:T(8,128)(2,1)} %all-gather.5.cloned.1.call-done), kind=kOutput, calls=%fused_computation.2 | convolution fusion | flops 4299161600 | bytes 18874368 | tf_op jit(solution)/shard_map/dot_general | solution.py:117
  113.2 1.9 copy-done
  115.1 6.1 %fusion.25 = f32[1024,1024]{1,0:T(8,128)} fusion(bf16[2048,1024]{1,0:T(8,128)(2,1)S(1)} %divide_convert_fusion, bf16[2048,1024]{0,1:T(8,128)(2,1)S(1)} %copy-done.12), kind=kOutput, calls=%fused_computation.58 | convolution fusion | flops 4294967296 | bytes 12582912 | tf_op jit(solution)/shard_map/dot_general | solution.py:121
  121.2 0.0 reduce-scatter.2.cloned.1.call-update
  121.2 0.3 select_bitcast_fusion
  121.5 0.0 copy-start.5
  121.5 1.3 copy-done.5
  122.8 0.1 slice.25
  122.9 0.5 copy.76
  123.4 0.0 copy-start.6
  123.5 4.7 %fusion.24 = f32[2048,512]{0,1:T(8,128)S(1)} fusion(bf16[2048,1024]{1,0:T(8,128)(2,1)} %copy-done, bf16[1024,512]{0,1:T(8,128)(2,1)S(1)} %bitcast.38), kind=kOutput, calls=%fused_computation.57 | convolution fusion | flops 2147483648 | bytes 9437184 | tf_op jit(solution)/shard_map/dot_general | solution.py:62
  128.2 0.0 copy-start.9
  128.2 0.0 copy-start.8
  128.2 0.1 collective-permute-start
  128.3 7.1 %collective-permute-done = f32[2048,512]{0,1:T(8,128)S(1)} collective-permute-done((f32[2048,512]{0,1:T(8,128)S(1)}, f32[2048,512]{0,1:T(8,128)S(1)}, u32[]{:S(2)}, u32[]{:S(2)}) %collective-permute-start) | collective-permute-done | bytes 4194336 | tf_op jit(solution)/shard_map/ppermute | solution.py:67
  135.4 1.3 slice_add_fusion
  136.8 2.5 %collective-permute-start.1 = (f32[2048,256]{0,1:T(8,128)S(1)}, f32[2048,256]{0,1:T(8,128)S(1)}, u32[]{:S(2)}, u32[]{:S(2)}) collective-permute-start(f32[2048,256]{0,1:T(8,128)S(1)} %slice_add_fusion), channel_id=1, source_target_pairs={{0,2},{1,3},{2,0},{3,1},{4,6},{5,7},{6,4},{7,5},{8,10},{9,11},{10,... | collective-permute-start | bytes 6291464 | tf_op jit(solution)/shard_map/ppermute | solution.py:67
  139.3 0.1 dynamic_slice.6
  139.4 0.1 dynamic_slice.7
  139.4 0.0 copy-done.9
  139.5 1.3 fusion.18
  140.8 44.4 %collective-permute-done.1 = f32[2048,256]{0,1:T(8,128)S(1)} collective-permute-done((f32[2048,256]{0,1:T(8,128)S(1)}, f32[2048,256]{0,1:T(8,128)S(1)}, u32[]{:S(2)}, u32[]{:S(2)}) %collective-permute-start.1) | collective-permute-done | bytes 2097184 | tf_op jit(solution)/shard_map/ppermute | solution.py:67
  185.2 2.2 fusion.10
  187.5 2.9 %copy.79 = f32[2048,256]{1,0:T(8,128)} copy(f32[2048,256]{0,1:T(8,128)} %get-tuple-element.49) | data formatting | bytes 4194304
  190.3 1.8 copy.80
  192.1 6.8 %psum.30 = f32[2048]{0:T(1024)S(1)} all-reduce(f32[2048]{0:T(1024)S(1)} %get-tuple-element.48), channel_id=1, replica_groups=mesh['user'=8,'item'=4] {'item'}, use_global_device_ids=true, to_apply=%region_7.8 | all-reduce | flops 2048 | bytes 16384 | tf_op jit(solution)/shard_map/psum | solution.py:130
  198.9 0.6 broadcast_add_fusion
  199.5 10.6 %reduce-scatter.2.cloned.1.call-done = f32[1024,128]{1,0:T(8,128)} async-done(((f32[1024,1024]{1,0:T(8,128)}), f32[1024,128]{1,0:T(8,128)}) %reduce-scatter.2.cloned.1.call-update) | async-done | bytes 524304 | tf_op jit(solution)/shard_map/reduce_scatter | solution.py:131
  210.1 0.0 copy-done.7
  210.1 2.2 fusion.19
  212.2 20.0 %psum.31 = f32[1024]{0:T(1024)S(1)} all-reduce(f32[1024]{0:T(1024)S(1)} %get-tuple-element.46), channel_id=1, replica_groups=mesh['user'=8,'item'=4] {'user'}, use_global_device_ids=true, to_apply=%region_10.11 | all-reduce | flops 1024 | bytes 8192 | tf_op jit(solution)/shard_map/psum | solution.py:137
  232.3 0.6 broadcast_add_fusion.1
  (20 shorter events, 0.1 us)
Async XLA Ops:
  7.2 90.2 %all-gather.5.cloned.1.call-start = ((), (), s32[]{:S(2)}) async-start(), calls=%async_computation.2 | async-start | bytes 2359296 | tf_op jit(solution)/shard_map/all_gather | solution.py:105
  12.7 3.1 %copy-start.4 = (f32[2048,256]{1,0:T(8,128)S(1)}, f32[2048,256]{1,0:T(8,128)}, u32[]{:S(2)}) copy-start(f32[2048,256]{1,0:T(8,128)} %param.11) | copy-start | bytes 6291460
  12.7 90.1 %all-gather.3.cloned.1.call-start = ((), (), s32[]{:S(2)}) async-start(), calls=%async_computation.1 | async-start | bytes 5242880 | tf_op jit(solution)/shard_map/all_gather | solution.py:104
  17.6 16.9 %copy-start.3 = (f32[2048,256]{1,0:T(8,128)S(1)}, f32[2048,256]{1,0:T(8,128)}, u32[]{:S(2)}) copy-start(f32[2048,256]{1,0:T(8,128)} %param.10) | copy-start | bytes 6291460
  34.4 175.7 %reduce-scatter.2.cloned.1.call-start = ((), (), s32[]{:S(2)}) async-start(), calls=%async_computation.3 | async-start | bytes 4718592 | tf_op jit(solution)/shard_map/reduce_scatter | solution.py:131
  34.5 46.0 %copy-start.10 = (s32[1,1,32]{2,1,0:T(1,128)S(1)}, s32[1,1,32]{2,1,0:T(1,128)}, u32[]{:S(2)}) copy-start(s32[1,1,32]{2,1,0:T(1,128)} %param.16) | copy-start | bytes 388
  92.0 5.3 %copy-start.11 = (s32[4]{0:T(128)S(1)}, s32[4]{0:T(128)}, u32[]{:S(2)}) copy-start(s32[4]{0:T(128)} %constant.83.clone) | copy-start | bytes 52
  102.8 12.3 %copy-start.12 = (bf16[2048,1024]{0,1:T(8,128)(2,1)S(1)}, bf16[2048,1024]{0,1:T(8,128)(2,1)}, u32[]{:S(2)}) copy-start(bf16[2048,1024]{0,1:T(8,128)(2,1)} %all-gather.3.cloned.1.call-done) | copy-start | bytes 12582916
  113.1 1.9 copy-start
  121.5 1.3 copy-start.5
  123.4 12.0 %copy-start.1 = (bf16[2048,1024]{1,0:T(8,128)(2,1)S(1)}, bf16[2048,1024]{1,0:T(8,128)(2,1)}, u32[]{:S(2)}) copy-start(bf16[2048,1024]{1,0:T(8,128)(2,1)} %copy-done) | copy-start | bytes 12582916
  123.4 12.0 %copy-start.6 = (bf16[1024,4,256]{2,0,1:T(8,128)(2,1)S(1)}, bf16[1024,4,256]{2,0,1:T(8,128)(2,1)}, u32[]{:S(2)}) copy-start(bf16[1024,4,256]{2,0,1:T(8,128)(2,1)} %copy-done.5) | copy-start | bytes 6291460
  128.2 11.3 %copy-start.9 = (f32[1024]{0:T(1024)S(1)}, f32[1024]{0:T(1024)}, u32[]{:S(2)}) copy-start(f32[1024]{0:T(1024)} %param.15) | copy-start | bytes 12292
  128.2 11.3 %copy-start.8 = (f32[2048]{0:T(1024)S(1)}, f32[2048]{0:T(1024)}, u32[]{:S(2)}) copy-start(f32[2048]{0:T(1024)} %param.12) | copy-start | bytes 24580
  128.2 7.2 %collective-permute-start = (f32[2048,512]{0,1:T(8,128)S(1)}, f32[2048,512]{0,1:T(8,128)S(1)}, u32[]{:S(2)}, u32[]{:S(2)}) collective-permute-start(f32[2048,512]{0,1:T(8,128)S(1)} %fusion.24), channel_id=1, source_target_pairs={{0,1},{1,0},{2,3},{3,2},{4,5},{5,4},{6,7},{7,6},{8,9},{9,8},{10,11... | collective-permute-start | bytes 12582920 | tf_op jit(solution)/shard_map/ppermute | solution.py:67
  136.8 48.5 %collective-permute-start.1 = (f32[2048,256]{0,1:T(8,128)S(1)}, f32[2048,256]{0,1:T(8,128)S(1)}, u32[]{:S(2)}, u32[]{:S(2)}) collective-permute-start(f32[2048,256]{0,1:T(8,128)S(1)} %slice_add_fusion), channel_id=1, source_target_pairs={{0,2},{1,3},{2,0},{3,1},{4,6},{5,7},{6,4},{7,5},{8,10},{9,11},{10,... | collective-permute-start | bytes 6291464 | tf_op jit(solution)/shard_map/ppermute | solution.py:67
  139.5 45.8 %copy-start.2 = (bf16[2048,256]{0,1:T(8,128)(2,1)S(1)}, bf16[2048,256]{0,1:T(8,128)(2,1)}, u32[]{:S(2)}) copy-start(bf16[2048,256]{0,1:T(8,128)(2,1)} %fusion.6) | copy-start | bytes 3145732
  190.3 19.7 %copy-start.7 = (bf16[1024,128]{1,0:T(8,128)(2,1)S(1)}, bf16[1024,128]{1,0:T(8,128)(2,1)}, u32[]{:S(2)}) copy-start(bf16[1024,128]{1,0:T(8,128)(2,1)} %get-tuple-element.52) | copy-start | bytes 786436
Sparse Core Ops, SparseCore 0:
  12.8 54.0 all-gather.4
  68.5 33.1 all-gather.2
  121.4 88.6 reduce-scatter.1

commit v5 on v4

--- a/solution.py
+++ b/solution.py
@@ -35,6 +35,22 @@
     return grid.reshape(UB, IB, BLK, BLK)
 
 
+def doubling_gather(part, axis_name, width, index):
+    rows, block = part.shape
+    held = part.reshape(rows, 1, block)
+    bit = width.bit_length() - 2
+    while bit >= 0:
+        partner = 1 << bit
+        perm = [(i, i ^ partner) for i in range(width)]
+        other = lax.ppermute(held, axis_name, perm)
+        upper = ((index >> bit) & 1) == 1
+        low = jnp.where(upper, other, held)
+        high = jnp.where(upper, held, other)
+        held = jnp.stack([low, high], axis=2).reshape(rows, 2 * held.shape[1], block)
+        bit -= 1
+    return held.reshape(rows, width * block)
+
+
 def halving_order(width):
     order = [0]
     step = width
@@ -44,7 +60,7 @@
     return order
 
 
-def halving_user_sums(ratio, beta_full, width, index, axis_name):
+def halving_user_sums(ratio, beta_full, width, index, axis_name, extra):
     items, factors = beta_full.shape
     block = factors // width
     order = jnp.asarray(halving_order(width), jnp.int32) ^ index
@@ -64,13 +80,15 @@
     for step_index in range(len(sizes) - 1):
         partner = 1 << step_index
         perm = [(i, i ^ partner) for i in range(width)]
+        if step_index == len(sizes) - 2:
+            terms[step_index], extra = lax.optimization_barrier((terms[step_index], extra))
         received = lax.ppermute(terms[step_index], axis_name, perm)
         offset = 0
         for later in range(step_index + 1, len(sizes)):
             span = terms[later].shape[1]
             terms[later] = terms[later] + received[:, offset : offset + span]
             offset += span
-    return terms[-1]
+    return terms[-1], extra
 
 
 def on_device(
@@ -101,15 +119,8 @@
     theta_placed = lax.dynamic_update_slice_in_dim(
         jnp.zeros((factors,), jnp.float32), theta_local, item_index * theta_columns, 0
     )
-    theta_full = lax.all_gather(theta_part, "item", axis=1, tiled=True)
+    theta_full = doubling_gather(theta_part, "item", item_width, item_index)
     beta_full = lax.all_gather(beta_part, "user", axis=1, tiled=True)
-    theta_part, beta_placed, theta_placed = lax.optimization_barrier(
-        (theta_part, beta_placed, theta_placed)
-    )
-    beta_total, theta_total = lax.psum((beta_placed, theta_placed), ("user", "item"))
-    tile_counts, beta_total, theta_total = lax.optimization_barrier(
-        (tile_counts, beta_total, theta_total)
-    )
     user_rows = theta_full.shape[0]
     item_rows = beta_full.shape[0]
     grid = dense_counts(tile_slots, tile_counts, live_tiles)
@@ -122,7 +133,10 @@
         ratio, theta_full, (((0,), (0,)), ((), ())), preferred_element_type=jnp.float32
     )
     xi_mean = (prior_a2 + factors * prior_a) / xi_rate
-    user_share = halving_user_sums(ratio, beta_full, item_width, item_index, "item")
+    user_share, placed = halving_user_sums(
+        ratio, beta_full, item_width, item_index, "item", (beta_placed, theta_placed)
+    )
+    beta_total, theta_total = lax.psum(placed, ("user", "item"))
     theta_shape_new = prior_a + theta_part.astype(jnp.float32) * user_share
     beta_slice = lax.dynamic_slice_in_dim(beta_total, item_index * theta_columns, theta_columns, 0)
     theta_rate_new = xi_mean[:, None] + beta_slice[None, :]

time: 240 us -> 259 us (1.079)
  blocking collectives: 69.7 us -> 102 us
  waiting for transfers between devices: 62.2 us -> 30.7 us
  other arithmetic: 36.5 us -> 44.4 us
  matrix products: 23.8 us -> 29.3 us
    ppermute x2, waiting for transfers between devices: 51.6 us -> 5.07 us  [halving_user_sums(): received = lax.ppermute(terms[step_index], axis_name, perm)]
    psum x1, blocking collectives: 42.9 us -> 75.8 us  [on_device(): beta_total, theta_total = lax.psum(placed, ('user', 'item'))]
    ppermute x0 -> x2, waiting for transfers between devices: none -> 17.3 us  [doubling_gather(): other = lax.ppermute(held, axis_name, perm)]
    reduce_scatter x1, waiting for transfers between devices: 10.6 us -> 0.01 us  [on_device(): lax.psum_scatter(item_acc, 'user', scatter_dimension=1, tiled=True)]
    all_gather x1, waiting for transfers between devices: 0.02 us -> 8.38 us  [on_device(): beta_full = lax.all_gather(beta_part, 'user', axis=1, tiled=True)]
    dot_general x3, matrix products: 7.35 us -> 15.1 us  [halving_user_sums(): terms.append(jnp.dot(ratio, piece, preferred_element_type=jnp.float32))]
    convert_element_type x2 -> x1, other arithmetic: 22.3 us -> 16.1 us  [exp_mean_log(): jnp.exp(lax.digamma(shape_param) - jnp.log(rate_param)).astype(jnp.bfloat16)]
    reduce_sum x0 -> x1, other arithmetic: none -> 4.44 us  [on_device(): beta_local = jnp.sum(beta_shape / beta_rate, axis=0)]
  transfers between devices with their start and end apart: 5 -> 6, of which waited for: 3 -> 3; matrix products, arithmetic and copies ran while one was open for 26% -> 24% of each run, Pallas kernels for 0% -> 0%
where the time goes in v5:
time: 259 us
  blocking collectives  102 us (39%)
  other arithmetic  44.4 us (17%)
  local copies, waits for them, and re-layouts  32.3 us (12%)
  waiting for transfers between devices  30.7 us (12%)
  matrix products  29.3 us (11%)
  between operations  14.9 us (6%)
  starting transfers between devices  4.82 us (2%)
    psum x1, blocking collectives, on_device(): beta_total, theta_total = lax.psum(placed, ('user', 'item'))  75.8 us
    psum x1, blocking collectives, on_device(): eta_rate_new = prior_c2 / prior_d2 + lax.psum(item_part, 'user')  20.7 us
    unnamed x31, local copies, waits for them, and re-layouts  19.1 us
    ppermute x2, waiting for transfers between devices, doubling_gather(): other = lax.ppermute(held, axis_name, perm)  17.3 us
    convert_element_type x1, other arithmetic, exp_mean_log(): jnp.exp(lax.digamma(shape_param) - jnp.log(rate_param)).astype(jnp.bfloat16)  16.1 us
    dot_general x3, matrix products, halving_user_sums(): terms.append(jnp.dot(ratio, piece, preferred_element_type=jnp.float32))  15.1 us
    all_gather x1, waiting for transfers between devices, on_device(): beta_full = lax.all_gather(beta_part, 'user', axis=1, tiled=True)  8.38 us
    dot_general x1, matrix products, on_device(): lax.dot_general(theta_full, beta_full, (((1,), (1,)), ((), ())), preferre...  8.07 us
  transfers between devices with their start and end apart: 6, of which 3 were waited for; matrix products, arithmetic and copies ran while one was open for 24% of the time, Pallas kernels for 0%

profile of v5, /device:TPU:0, one launch (start us, length us, event | category | flops | bytes accessed | tf_op | source)
XLA Modules:
  0.0 258.8 jit_solution(4387799369550567213)
XLA Ops:
  7.2 0.0 copy-start.2
  7.2 0.0 all-gather.2.cloned.1.call-start
  7.2 3.0 %copy.75 = f32[2048,256]{0,1:T(8,128)} copy(f32[2048,256]{1,0:T(8,128)} %param.11) | data formatting | bytes 4194304 | tf_op args[1]
  10.2 0.0 copy-done.2
  10.3 1.8 copy.66
  12.1 16.1 %fusion.6 = bf16[2048,256]{0,1:T(8,128)(2,1)S(1)} fusion(f32[2048,256]{0,1:T(8,128)} %copy.75, f32[2048,256]{0,1:T(8,128)} %copy.66), kind=kLoop, calls=%fused_computation.15 | loop fusion | flops 40370176 | bytes 5242880 | tf_op jit(solution)/shard_map/convert_element_type | solution.py:21
  28.2 3.0 %collective-permute-start = (bf16[2048,1,256]{0,2,1:T(8,128)(2,1)S(1)}, bf16[2048,1,256]{0,2,1:T(8,128)(2,1)}, u32[]{:S(2)}, u32[]{:S(2)}) collective-permute-start(bf16[2048,1,256]{0,2,1:T(8,128)(2,1)S(1)} %bitcast.52), channel_id=1, source_target_pairs={{0,2},{1,3},{2,0},{3,1},{4,6},{5,7},{6,4},{7,5},{8,10},{9,11},{10,... | collective-permute-start | bytes 3145736 | tf_op jit(solution)/shard_map/ppermute | solution.py:45
  31.2 0.0 copy-done.7
  31.2 0.0 copy-done.8
  31.2 4.4 %divide_reduce_fusion.1 = (f32[128]{0:T(128)S(1)}, bf16[1024,128]{1,0:T(8,128)(2,1)}) fusion(f32[1024,128]{1,0:T(8,128)S(1)} %copy-done.7, f32[1024,128]{1,0:T(8,128)S(1)} %copy-done.8), kind=kLoop, calls=%fused_computation.45 | loop fusion | flops 10354560 | bytes 1311232 | tf_op jit(solution)/shard_map/reduce_sum | solution.py:114
  35.7 0.0 all-gather.2.cloned.1.call-update
  35.7 0.2 reduce-scatter.2.cloned.1.call-start
  36.6 0.6 iota_reduce_fusion
  37.2 17.3 %collective-permute-done = bf16[2048,1,256]{0,2,1:T(8,128)(2,1)} collective-permute-done((bf16[2048,1,256]{0,2,1:T(8,128)(2,1)S(1)}, bf16[2048,1,256]{0,2,1:T(8,128)(2,1)}, u32[]{:S(2)}, u32[]{:S(2)}) %collective-permute-start) | collective-permute-done | bytes 1048608 | tf_op jit(solution)/shard_map/ppermute | solution.py:45
  54.5 1.4 select_bitcast_fusion.4
  55.8 1.5 maximum_bitcast_fusion
  57.3 0.0 collective-permute-start.1
  57.4 0.1 broadcast_in_dim.48
  57.4 0.1 fusion.22
  57.6 0.1 broadcast_in_dim.46
  57.7 4.9 %gather_fusion = bf16[32,256,256]{2,1,0:T(8,128)(2,1)} fusion(bf16[32,256,256]{2,1,0:T(8,128)(2,1)} %bitcast.55, s32[1024]{0:T(1024)S(1)} %pad_clamp_fusion.1), kind=kCustom, calls=%fused_computation | custom fusion | bytes 8388736 | tf_op jit(solution)/shard_map/jit(_take)/gather | solution.py:33
  62.6 5.5 %fusion.1 = f32[8,4,256,256]{3,1,2,0:T(4,128)S(1)} fusion(bf16[8,4,256,256]{3,2,1,0:T(8,128)(2,1)} %bitcast.51, pred[8,4]{1,0:T(8,128)(4,1)S(1)} %broadcast_in_dim.48, pred[8,4]{1,0:T(8,128)(4,1)S(1)} %broadcast_in_dim.46), kind=kLoop, calls=%fused_computation.6 | loop fusion | flops 6291456 | bytes 12582976 | tf_op jit(solution)/shard_map/convert_element_type | solution.py:127
  68.1 0.0 copy-start.12
  68.1 5.3 %copy.87 = f32[256,8,4,256]{3,1,2,0:T(8,128)} copy(f32[256,8,4,256]{3,2,1,0:T(4,128)S(1)} %bitcast.50) | data formatting | bytes 16777216
  73.4 0.0 copy-done.12
  73.4 0.0 collective-permute-done.1
  73.5 1.9 select_bitcast_fusion.2
  75.4 0.4 pad_maximum_fusion
  75.7 2.3 copy.77
  78.0 8.4 %all-gather.2.cloned.1.call-done = bf16[1024,1024]{1,0:T(8,128)(2,1)} async-done(((bf16[1024,128]{1,0:T(8,128)(2,1)}), bf16[1024,1024]{1,0:T(8,128)(2,1)}) %all-gather.2.cloned.1.call-update) | async-done | bytes 2097168 | tf_op jit(solution)/shard_map/all_gather | solution.py:123
  86.4 1.9 copy.94
  88.3 0.9 copy-done.5
  89.2 8.1 %divide_convert_fusion = bf16[2048,1024]{1,0:T(8,128)(2,1)S(1)} fusion(f32[2048,1024]{1,0:T(8,128)} %bitcast.53, bf16[2048,1024]{0,1:T(8,128)(2,1)S(1)} %bitcast.56, bf16[1024,1024]{1,0:T(8,128)(2,1)} %all-gather.2.cloned.1.call-done), kind=kOutput, calls=%fused_computation.2 | convolution fusion | flops 4299161600 | bytes 18874368 | tf_op jit(solution)/shard_map/dot_general | solution.py:128
  97.3 2.0 copy-done
  99.3 6.1 %fusion.25 = f32[1024,1024]{1,0:T(8,128)} fusion(bf16[2048,1024]{1,0:T(8,128)(2,1)S(1)} %divide_convert_fusion, bf16[2048,1024]{0,1:T(8,128)(2,1)S(1)} %bitcast.57), kind=kOutput, calls=%fused_computation.64 | convolution fusion | flops 4294967296 | bytes 12582912 | tf_op jit(solution)/shard_map/dot_general | solution.py:132
  105.4 0.0 reduce-scatter.2.cloned.1.call-update
  105.4 2.0 gather_fusion.1
  107.4 1.9 select_bitcast_fusion
  109.3 0.0 copy-start.4
  109.3 1.3 copy-done.4
  110.6 0.1 slice.25
  110.7 1.3 copy.79
  112.0 7.0 %fusion.24 = f32[2048,512]{0,1:T(8,128)} fusion(bf16[2048,1024]{1,0:T(8,128)(2,1)} %copy-done, bf16[1024,512]{0,1:T(8,128)(2,1)} %bitcast.59), kind=kOutput, calls=%fused_computation.63 | convolution fusion | flops 2147483648 | bytes 9437184 | tf_op jit(solution)/shard_map/dot_general | solution.py:78
  118.9 0.0 collective-permute-start.2
  118.9 0.2 dynamic_update_slice.6
  119.1 2.0 divide_reduce_fusion
  121.1 0.2 dynamic_update_slice.7
  121.4 5.1 %collective-permute-done.2 = f32[2048,512]{0,1:T(8,128)} collective-permute-done((f32[2048,512]{0,1:T(8,128)}, f32[2048,512]{0,1:T(8,128)}, u32[]{:S(2)}, u32[]{:S(2)}) %collective-permute-start.2) | collective-permute-done | bytes 4194336 | tf_op jit(solution)/shard_map/ppermute | solution.py:85
  126.4 4.5 %slice_add_fusion = f32[2048,256]{0,1:T(8,128)S(1)} fusion(f32[2048,512]{0,1:T(8,128)} %collective-permute-done.2, bf16[2048,1024]{1,0:T(8,128)(2,1)} %copy-done, bf16[1024,4,256]{2,0,1:T(8,128)(2,1)} %copy-done.4), kind=kOutput, calls=%fused_computation.17 | convolution fusion | flops 1074266112 | bytes 8912896 | tf_op jit(solution)/shard_map/dot_general | solution.py:78
  130.9 1.5 collective-permute-start.3
  132.5 0.0 copy-done.10
  132.5 3.7 %fusion.18 = f32[2048,256]{0,1:T(8,128)} fusion(bf16[2048,1024]{1,0:T(8,128)(2,1)S(1)} %copy-done.1, bf16[1024,4,256]{2,0,1:T(8,128)(2,1)} %copy-done.4), kind=kOutput, calls=%fused_computation.43 | convolution fusion | flops 1073741824 | bytes 6815744 | tf_op jit(solution)/shard_map/dot_general | solution.py:78
  136.1 75.8 %all-reduce = (f32[1024]{0:T(1024)S(1)}, f32[1024]{0:T(1024)S(1)}) all-reduce(f32[1024]{0:T(1024)S(1)} %dynamic_update_slice.6, f32[1024]{0:T(1024)S(1)} %dynamic_update_slice.7), channel_id=1, replica_groups=mesh['user'=8,'item'=4] {'user','item'}, use_global_device_ids=true, to_apply=%region_4.5 | all-reduce | flops 2048 | bytes 16384 | tf_op jit(solution)/shard_map/psum | solution.py:139
  211.9 0.1 dynamic_slice.6
  212.0 0.1 dynamic_slice.7
  212.1 0.0 collective-permute-done.3
  212.1 5.2 %fusion.10 = (f32[2048]{0:T(1024)S(1)}, f32[2048,256]{0,1:T(8,128)}, f32[2048,256]{0,1:T(8,128)S(1)}) fusion(f32[256]{0:T(256)S(1)} %dynamic_slice.6, f32[2048]{0:T(1024)S(1)} %broadcast_divide_fusion, f32[2048,256]{0,1:T(8,128)} %collective-permute-done.3, f32[2048,256]{0,1:T(8,128)} %fusion.18, f32[2048,512]{0,1:T(8,128)} %collective-permute-done.2, ...), kind=kLoop, calls=%fused_computation.27 | loop fusion | flops 4192256 | bytes 11551744 | tf_op jit(solution)/shard_map/reduce_sum | solution.py:143
  217.3 2.9 %copy.82 = f32[2048,256]{1,0:T(8,128)} copy(f32[2048,256]{0,1:T(8,128)} %get-tuple-element.43) | data formatting | bytes 4194304
  220.2 1.8 copy.83
  222.0 5.9 %psum.29 = f32[2048]{0:T(1024)S(1)} all-reduce(f32[2048]{0:T(1024)S(1)} %get-tuple-element.42), channel_id=1, replica_groups=mesh['user'=8,'item'=4] {'item'}, use_global_device_ids=true, to_apply=%region_6.7 | all-reduce | flops 2048 | bytes 16384 | tf_op jit(solution)/shard_map/psum | solution.py:144
  227.9 0.6 broadcast_add_fusion
  228.5 2.2 fusion.19
  230.6 20.7 %psum.31 = f32[1024]{0:T(1024)S(1)} all-reduce(f32[1024]{0:T(1024)S(1)} %get-tuple-element.40), channel_id=1, replica_groups=mesh['user'=8,'item'=4] {'user'}, use_global_device_ids=true, to_apply=%region_10.11 | all-reduce | flops 1024 | bytes 8192 | tf_op jit(solution)/shard_map/psum | solution.py:151
  251.4 0.6 broadcast_add_fusion.1
  (26 shorter events, 0.1 us)
Async XLA Ops:
  7.2 3.1 %copy-start.2 = (f32[2048,256]{1,0:T(8,128)S(1)}, f32[2048,256]{1,0:T(8,128)}, u32[]{:S(2)}) copy-start(f32[2048,256]{1,0:T(8,128)} %param.10) | copy-start | bytes 6291460
  7.2 79.2 %all-gather.2.cloned.1.call-start = ((), (), s32[]{:S(2)}) async-start(), calls=%async_computation.1 | async-start | bytes 2359296 | tf_op jit(solution)/shard_map/all_gather | solution.py:123
  12.1 19.2 %copy-start.7 = (f32[1024,128]{1,0:T(8,128)S(1)}, f32[1024,128]{1,0:T(8,128)}, u32[]{:S(2)}) copy-start(f32[1024,128]{1,0:T(8,128)} %param.13) | copy-start | bytes 1572868
  12.1 19.2 %copy-start.8 = (f32[1024,128]{1,0:T(8,128)S(1)}, f32[1024,128]{1,0:T(8,128)}, u32[]{:S(2)}) copy-start(f32[1024,128]{1,0:T(8,128)} %param.14) | copy-start | bytes 1572868
  12.1 24.5 %copy-start.11 = (s32[1,1,32]{2,1,0:T(1,128)S(1)}, s32[1,1,32]{2,1,0:T(1,128)}, u32[]{:S(2)}) copy-start(s32[1,1,32]{2,1,0:T(1,128)} %param.16) | copy-start | bytes 388
  28.2 26.3 %collective-permute-start = (bf16[2048,1,256]{0,2,1:T(8,128)(2,1)S(1)}, bf16[2048,1,256]{0,2,1:T(8,128)(2,1)}, u32[]{:S(2)}, u32[]{:S(2)}) collective-permute-start(bf16[2048,1,256]{0,2,1:T(8,128)(2,1)S(1)} %bitcast.52), channel_id=1, source_target_pairs={{0,2},{1,3},{2,0},{3,1},{4,6},{5,7},{6,4},{7,5},{8,10},{9,11},{10,... | collective-permute-start | bytes 3145736 | tf_op jit(solution)/shard_map/ppermute | solution.py:45
  35.7 192.8 %reduce-scatter.2.cloned.1.call-start = ((), (), s32[]{:S(2)}) async-start(), calls=%async_computation.2 | async-start | bytes 4718592 | tf_op jit(solution)/shard_map/reduce_scatter | solution.py:145
  57.3 16.1 %collective-permute-start.1 = (bf16[2048,2,256]{0,2,1:T(8,128)(2,1)}, bf16[2048,2,256]{0,2,1:T(8,128)(2,1)}, u32[]{:S(2)}, u32[]{:S(2)}) collective-permute-start(bf16[2048,2,256]{0,2,1:T(8,128)(2,1)} %maximum_bitcast_fusion), channel_id=1, source_target_pairs={{0,1},{1,0},{2,3},{3,2},{4,5},{5,4},{6,7},{7,6},{8,9},{9,8},{10,11... | collective-permute-start | bytes 6291464 | tf_op jit(solution)/shard_map/ppermute | solution.py:45
  68.1 5.3 %copy-start.12 = (s32[4]{0:T(128)S(1)}, s32[4]{0:T(128)}, u32[]{:S(2)}) copy-start(s32[4]{0:T(128)} %constant.85.clone) | copy-start | bytes 52
  86.4 2.8 %copy-start.5 = (bf16[2048,2,2,256]{0,3,2,1:T(8,128)(2,1)S(1)}, bf16[2048,2,2,256]{0,3,2,1:T(8,128)(2,1)}, u32[]{:S(2)}) copy-start(bf16[2048,2,2,256]{0,3,2,1:T(8,128)(2,1)} %copy.77) | copy-start | bytes 12582916
  97.3 2.0 copy-start
  109.3 1.3 copy-start.4
  112.0 7.2 %copy-start.3 = (f32[2048,256]{1,0:T(8,128)S(1)}, f32[2048,256]{1,0:T(8,128)}, u32[]{:S(2)}) copy-start(f32[2048,256]{1,0:T(8,128)} %param.10) | copy-start | bytes 6291460
  118.9 7.5 %collective-permute-start.2 = (f32[2048,512]{0,1:T(8,128)}, f32[2048,512]{0,1:T(8,128)}, u32[]{:S(2)}, u32[]{:S(2)}) collective-permute-start(f32[2048,512]{0,1:T(8,128)} %fusion.24), channel_id=1, source_target_pairs={{0,1},{1,0},{2,3},{3,2},{4,5},{5,4},{6,7},{7,6},{8,9},{9,8},{10,11... | collective-permute-start | bytes 12582920 | tf_op jit(solution)/shard_map/ppermute | solution.py:85
  121.4 11.1 %copy-start.10 = (f32[1024]{0:T(1024)S(1)}, f32[1024]{0:T(1024)}, u32[]{:S(2)}) copy-start(f32[1024]{0:T(1024)} %param.15) | copy-start | bytes 12292
  121.4 11.1 %copy-start.9 = (f32[2048]{0:T(1024)S(1)}, f32[2048]{0:T(1024)}, u32[]{:S(2)}) copy-start(f32[2048]{0:T(1024)} %param.12) | copy-start | bytes 24580
  121.4 11.1 %copy-start.1 = (bf16[2048,1024]{1,0:T(8,128)(2,1)S(1)}, bf16[2048,1024]{1,0:T(8,128)(2,1)}, u32[]{:S(2)}) copy-start(bf16[2048,1024]{1,0:T(8,128)(2,1)} %copy-done) | copy-start | bytes 12582916
  130.9 81.1 %collective-permute-start.3 = (f32[2048,256]{0,1:T(8,128)S(1)}, f32[2048,256]{0,1:T(8,128)}, u32[]{:S(2)}, u32[]{:S(2)}) collective-permute-start(f32[2048,256]{0,1:T(8,128)S(1)} %slice_add_fusion), channel_id=1, source_target_pairs={{0,2},{1,3},{2,0},{3,1},{4,6},{5,7},{6,4},{7,5},{8,10},{9,11},{10,... | collective-permute-start | bytes 6291464 | tf_op jit(solution)/shard_map/ppermute | solution.py:85
  220.2 8.3 %copy-start.6 = (bf16[1024,128]{1,0:T(8,128)(2,1)S(1)}, bf16[1024,128]{1,0:T(8,128)(2,1)}, u32[]{:S(2)}) copy-start(bf16[1024,128]{1,0:T(8,128)(2,1)} %get-tuple-element.51) | copy-start | bytes 786436
Sparse Core Ops, SparseCore 0:
  35.8 50.5 all-gather.1
  105.5 87.0 reduce-scatter.1

commit v6 on v5

--- a/solution.py
+++ b/solution.py
@@ -35,6 +35,15 @@
     return grid.reshape(UB, IB, BLK, BLK)
 
 
+def doubling_sum(value, axis_name, width):
+    bit = 1
+    while bit < width:
+        perm = [(i, i ^ bit) for i in range(width)]
+        value = value + lax.ppermute(value, axis_name, perm)
+        bit *= 2
+    return value
+
+
 def doubling_gather(part, axis_name, width, index):
     rows, block = part.shape
     held = part.reshape(rows, 1, block)
@@ -60,7 +69,7 @@
     return order
 
 
-def halving_user_sums(ratio, beta_full, width, index, axis_name, extra):
+def halving_user_sums(ratio, beta_full, width, index, axis_name):
     items, factors = beta_full.shape
     block = factors // width
     order = jnp.asarray(halving_order(width), jnp.int32) ^ index
@@ -80,15 +89,13 @@
     for step_index in range(len(sizes) - 1):
         partner = 1 << step_index
         perm = [(i, i ^ partner) for i in range(width)]
-        if step_index == len(sizes) - 2:
-            terms[step_index], extra = lax.optimization_barrier((terms[step_index], extra))
         received = lax.ppermute(terms[step_index], axis_name, perm)
         offset = 0
         for later in range(step_index + 1, len(sizes)):
             span = terms[later].shape[1]
             terms[later] = terms[later] + received[:, offset : offset + span]
             offset += span
-    return terms[-1], extra
+    return terms[-1]
 
 
 def on_device(
@@ -119,6 +126,10 @@
     theta_placed = lax.dynamic_update_slice_in_dim(
         jnp.zeros((factors,), jnp.float32), theta_local, item_index * theta_columns, 0
     )
+    placed = jnp.stack([beta_placed, theta_placed])
+    placed = doubling_sum(doubling_sum(placed, "item", item_width), "user", user_width)
+    beta_total = placed[0]
+    theta_total = placed[1]
     theta_full = doubling_gather(theta_part, "item", item_width, item_index)
     beta_full = lax.all_gather(beta_part, "user", axis=1, tiled=True)
     user_rows = theta_full.shape[0]
@@ -133,22 +144,19 @@
         ratio, theta_full, (((0,), (0,)), ((), ())), preferred_element_type=jnp.float32
     )
     xi_mean = (prior_a2 + factors * prior_a) / xi_rate
-    user_share, placed = halving_user_sums(
-        ratio, beta_full, item_width, item_index, "item", (beta_placed, theta_placed)
-    )
-    beta_total, theta_total = lax.psum(placed, ("user", "item"))
+    user_share = halving_user_sums(ratio, beta_full, item_width, item_index, "item")
     theta_shape_new = prior_a + theta_part.astype(jnp.float32) * user_share
     beta_slice = lax.dynamic_slice_in_dim(beta_total, item_index * theta_columns, theta_columns, 0)
     theta_rate_new = xi_mean[:, None] + beta_slice[None, :]
     user_part = jnp.sum(theta_shape_new / theta_rate_new, axis=1)
-    xi_rate_new = prior_a2 / prior_b2 + lax.psum(user_part, "item")
+    xi_rate_new = prior_a2 / prior_b2 + doubling_sum(user_part, "item", item_width)
     item_share = lax.psum_scatter(item_acc, "user", scatter_dimension=1, tiled=True)
     beta_shape_new = prior_c + beta_part.astype(jnp.float32) * item_share
     eta_mean = (prior_c2 + factors * prior_c) / eta_rate
     theta_slice = lax.dynamic_slice_in_dim(theta_total, user_index * beta_columns, beta_columns, 0)
     beta_rate_new = eta_mean[:, None] + theta_slice[None, :]
     item_part = jnp.sum(beta_shape_new / beta_rate_new, axis=1)
-    eta_rate_new = prior_c2 / prior_d2 + lax.psum(item_part, "user")
+    eta_rate_new = prior_c2 / prior_d2 + doubling_sum(item_part, "user", user_width)
     return (
         theta_shape_new,
         jnp.log(theta_rate_new),

time: 259 us -> 221 us (0.85)
  blocking collectives: 102 us -> 0 us
  waiting for transfers between devices: 30.7 us -> 89 us
  starting transfers between devices: 4.82 us -> 13.1 us
    psum x3 -> x0, blocking collectives: 102 us -> none  [the longest x1 75.8 us: on_device(): beta_total, theta_total = lax.psum(placed, ('user', 'item'))]
    ppermute x0 -> x10, waiting for transfers between devices: none -> 58 us  [doubling_sum(): value = value + lax.ppermute(value, axis_name, perm)]
    ppermute x0 -> x10, starting transfers between devices: none -> 8.45 us  [doubling_sum(): value = value + lax.ppermute(value, axis_name, perm)]
    reduce_sum x1 -> x0, other arithmetic: 4.44 us -> none  [on_device(): beta_local = jnp.sum(beta_shape / beta_rate, axis=0)]
    convert_element_type x1 -> x2, other arithmetic: 16.1 us -> 20.5 us  [exp_mean_log(): jnp.exp(lax.digamma(shape_param) - jnp.log(rate_param)).astype(jnp.bfloat16)]
    dot_general x3, matrix products: 15.1 us -> 12.4 us  [halving_user_sums(): terms.append(jnp.dot(ratio, piece, preferred_element_type=jnp.float32))]
    unnamed x31 -> x33, local copies, waits for them, and re-layouts: 19.1 us -> 19.7 us
  transfers between devices with their start and end apart: 6 -> 16, of which waited for: 3 -> 10; matrix products, arithmetic and copies ran while one was open for 24% -> 27% of each run, Pallas kernels for 0% -> 0%
where the time goes in v6:
time: 221 us; the launch traced here: 220 us
  waiting for transfers between devices  89 us (40%)
  other arithmetic  42 us (19%)
  local copies, waits for them, and re-layouts  32.2 us (15%)
  matrix products  28.9 us (13%)
  between operations  15 us (7%)
  starting transfers between devices  13.1 us (6%)
    ppermute x10, waiting for transfers between devices, doubling_sum(): value = value + lax.ppermute(value, axis_name, perm)  58 us
    convert_element_type x2, other arithmetic, exp_mean_log(): jnp.exp(lax.digamma(shape_param) - jnp.log(rate_param)).astype(jnp.bfloat16)  20.5 us
    unnamed x33, local copies, waits for them, and re-layouts  19.7 us
    ppermute x2, waiting for transfers between devices, doubling_gather(): other = lax.ppermute(held, axis_name, perm)  18.1 us
    dot_general x3, matrix products, halving_user_sums(): terms.append(jnp.dot(ratio, piece, preferred_element_type=jnp.float32))  12.4 us
    dot_general x1, matrix products, on_device(): lax.dot_general(theta_full, beta_full, (((1,), (1,)), ((), ())), preferre...  10.3 us
    ppermute x10, starting transfers between devices, doubling_sum(): value = value + lax.ppermute(value, axis_name, perm)  8.45 us
    all_gather x1, waiting for transfers between devices, on_device(): beta_full = lax.all_gather(beta_part, 'user', axis=1, tiled=True)  7.55 us
  transfers between devices with their start and end apart: 16, of which 10 were waited for; matrix products, arithmetic and copies ran while one was open for 27% of the time, Pallas kernels for 0%

profile of v6, /device:TPU:0, one launch (start us, length us, event | category | flops | bytes accessed | tf_op | source)
XLA Modules:
  0.0 220.2 jit_solution(10220769934753521721)
XLA Ops:
  7.2 0.0 copy-start.2
  7.2 0.0 all-gather.2.cloned.1.call-start
  7.2 3.0 %copy.75 = f32[2048,256]{0,1:T(8,128)} copy(f32[2048,256]{1,0:T(8,128)} %param.11) | data formatting | bytes 4194304 | tf_op args[1]
  10.3 1.8 copy.66
  12.1 16.1 %fusion.6 = bf16[2048,256]{0,1:T(8,128)(2,1)S(1)} fusion(f32[2048,256]{0,1:T(8,128)} %copy.75, f32[2048,256]{0,1:T(8,128)} %copy.66), kind=kLoop, calls=%fused_computation.15 | loop fusion | flops 40370176 | bytes 5242880 | tf_op jit(solution)/shard_map/convert_element_type | solution.py:21
  28.2 3.0 %collective-permute-start = (bf16[2048,1,256]{0,2,1:T(8,128)(2,1)S(1)}, bf16[2048,1,256]{0,2,1:T(8,128)(2,1)}, u32[]{:S(2)}, u32[]{:S(2)}) collective-permute-start(bf16[2048,1,256]{0,2,1:T(8,128)(2,1)S(1)} %bitcast.58), channel_id=1, source_target_pairs={{0,2},{1,3},{2,0},{3,1},{4,6},{5,7},{6,4},{7,5},{8,10},{9,11},{10,... | collective-permute-start | bytes 3145736 | tf_op jit(solution)/shard_map/ppermute | solution.py:54
  31.2 4.4 %fusion.16 = (bf16[1024,128]{1,0:T(8,128)(2,1)}, f32[128]{0:T(128)S(1)}) fusion(f32[1024,128]{1,0:T(8,128)S(1)} %copy-done.8, f32[1024,128]{1,0:T(8,128)S(1)} %copy-done.9), kind=kLoop, calls=%fused_computation.39 | loop fusion | flops 10354560 | bytes 1311232 | tf_op jit(solution)/shard_map/convert_element_type | solution.py:21
  35.6 0.0 all-gather.2.cloned.1.call-update
  35.7 0.0 reduce-scatter.2.cloned.1.call-start
  36.4 18.1 %collective-permute-done = bf16[2048,1,256]{0,2,1:T(8,128)(2,1)} collective-permute-done((bf16[2048,1,256]{0,2,1:T(8,128)(2,1)S(1)}, bf16[2048,1,256]{0,2,1:T(8,128)(2,1)}, u32[]{:S(2)}, u32[]{:S(2)}) %collective-permute-start) | collective-permute-done | bytes 1048608 | tf_op jit(solution)/shard_map/ppermute | solution.py:54
  54.5 1.4 select_bitcast_fusion.4
  55.8 0.0 copy-start.12
  55.9 1.5 maximum_bitcast_fusion
  57.4 0.8 iota_reduce_fusion
  58.2 0.1 broadcast_in_dim.48
  58.3 0.1 fusion.22
  58.4 0.1 broadcast_in_dim.46
  58.5 5.0 %gather_fusion = bf16[32,256,256]{2,1,0:T(8,128)(2,1)} fusion(bf16[32,256,256]{2,1,0:T(8,128)(2,1)} %bitcast.61, s32[1024]{0:T(1024)S(1)} %pad_clamp_fusion.1), kind=kCustom, calls=%fused_computation | custom fusion | bytes 8388736 | tf_op jit(solution)/shard_map/jit(_take)/gather | solution.py:33
  63.5 5.5 %fusion.1 = f32[8,4,256,256]{3,1,2,0:T(4,128)S(1)} fusion(bf16[8,4,256,256]{3,2,1,0:T(8,128)(2,1)} %bitcast.57, pred[8,4]{1,0:T(8,128)(4,1)S(1)} %broadcast_in_dim.48, pred[8,4]{1,0:T(8,128)(4,1)S(1)} %broadcast_in_dim.46), kind=kLoop, calls=%fused_computation.6 | loop fusion | flops 6291456 | bytes 12582976 | tf_op jit(solution)/shard_map/convert_element_type | solution.py:138
  69.0 0.0 copy-start.13
  69.0 5.3 %copy.87 = f32[256,8,4,256]{3,1,2,0:T(8,128)} copy(f32[256,8,4,256]{3,2,1,0:T(4,128)S(1)} %bitcast.56) | data formatting | bytes 16777216
  74.3 1.9 select_bitcast_fusion.2
  76.2 0.4 pad_maximum_fusion
  76.6 2.3 %copy.77 = bf16[2048,2,2,256]{0,3,2,1:T(8,128)(2,1)} copy(bf16[2048,2,2,256]{0,3,1,2:T(8,128)(2,1)S(1)} %pad_maximum_fusion) | data formatting | bytes 8388608 | tf_op jit(solution)/shard_map/stack | solution.py:58
  78.8 7.6 %all-gather.2.cloned.1.call-done = bf16[1024,1024]{1,0:T(8,128)(2,1)} async-done(((bf16[1024,128]{1,0:T(8,128)(2,1)}), bf16[1024,1024]{1,0:T(8,128)(2,1)}) %all-gather.2.cloned.1.call-update) | async-done | bytes 2097168 | tf_op jit(solution)/shard_map/all_gather | solution.py:134
  86.4 10.3 %divide_convert_fusion = bf16[2048,1024]{1,0:T(8,128)(2,1)S(1)} fusion(f32[2048,1024]{1,0:T(8,128)} %bitcast.59, bf16[2048,1024]{0,1:T(8,128)(2,1)} %bitcast.62, bf16[1024,1024]{1,0:T(8,128)(2,1)} %all-gather.2.cloned.1.call-done), kind=kOutput, calls=%fused_computation.2 | convolution fusion | flops 4299161600 | bytes 18874368 | tf_op jit(solution)/shard_map/dot_general | solution.py:139
  96.7 1.9 copy-done
  98.7 6.1 %fusion.28 = f32[1024,1024]{1,0:T(8,128)} fusion(bf16[2048,1024]{1,0:T(8,128)(2,1)S(1)} %divide_convert_fusion, bf16[2048,1024]{0,1:T(8,128)(2,1)S(1)} %bitcast.63), kind=kOutput, calls=%fused_computation.72 | convolution fusion | flops 4294967296 | bytes 12582912 | tf_op jit(solution)/shard_map/dot_general | solution.py:143
  104.8 0.0 reduce-scatter.2.cloned.1.call-update
  104.8 1.6 copy-done.7
  106.4 1.5 copy.94
  107.9 2.3 %gather_fusion.1 = bf16[4,1024,256]{2,1,0:T(8,128)(2,1)S(1)} fusion(bf16[1024,4,256]{2,0,1:T(8,128)(2,1)} %bitcast.60, s32[1024]{0:T(1024)S(1)} %pad_clamp_fusion), kind=kCustom, calls=%fused_computation.1 | custom fusion | bytes 4194320 | tf_op jit(solution)/shard_map/jit(_take)/gather | solution.py:76
  110.1 0.3 select_bitcast_fusion
  110.4 0.0 copy-start.4
  110.4 1.3 copy-done.4
  111.7 0.1 slice.33
  111.8 1.3 copy.79
  113.1 6.9 %fusion.27 = f32[2048,512]{0,1:T(8,128)} fusion(bf16[2048,1024]{1,0:T(8,128)(2,1)} %copy-done, bf16[1024,512]{0,1:T(8,128)(2,1)} %bitcast.65), kind=kOutput, calls=%fused_computation.71 | convolution fusion | flops 2147483648 | bytes 9437184 | tf_op jit(solution)/shard_map/dot_general | solution.py:87
  120.0 2.1 divide_reduce_fusion
  122.2 5.3 %collective-permute-done.2 = f32[2048,512]{0,1:T(8,128)} collective-permute-done((f32[2048,512]{0,1:T(8,128)}, f32[2048,512]{0,1:T(8,128)}, u32[]{:S(2)}, u32[]{:S(2)}) %collective-permute-start.2) | collective-permute-done | bytes 4194336 | tf_op jit(solution)/shard_map/ppermute | solution.py:92
  127.5 3.2 %slice_add_fusion = f32[2048,256]{0,1:T(8,128)S(1)} fusion(f32[2048,512]{0,1:T(8,128)} %collective-permute-done.2, bf16[2048,1024]{1,0:T(8,128)(2,1)S(1)} %copy-done.1, bf16[1024,4,256]{2,0,1:T(8,128)(2,1)} %copy-done.4), kind=kOutput, calls=%fused_computation.17 | convolution fusion | flops 1074266112 | bytes 8912896 | tf_op jit(solution)/shard_map/dot_general | solution.py:87
  130.7 1.5 collective-permute-start.3
  132.3 0.1 collective-permute-start.4
  132.3 1.2 collective-permute-done.4
  133.5 0.6 collective-permute-start.5
  134.1 44.5 %collective-permute-done.5 = f32[2,1024]{1,0:T(2,128)S(1)} collective-permute-done((f32[2,1024]{1,0:T(2,128)S(1)}, f32[2,1024]{1,0:T(2,128)S(1)}, u32[]{:S(2)}, u32[]{:S(2)}) %collective-permute-start.5) | collective-permute-done | bytes 8224 | tf_op jit(solution)/shard_map/ppermute | solution.py:42
  178.6 1.5 collective-permute-start.6
  180.2 2.2 collective-permute-done.6
  182.4 4.3 %collective-permute-done.7 = f32[2,1024]{1,0:T(2,128)S(1)} collective-permute-done((f32[2,1024]{1,0:T(2,128)S(1)}, f32[2,1024]{1,0:T(2,128)S(1)}, u32[]{:S(2)}, u32[]{:S(2)}) %collective-permute-start.7) | collective-permute-done | bytes 8224 | tf_op jit(solution)/shard_map/ppermute | solution.py:42
  186.7 1.1 collective-permute-start.8
  187.8 3.5 %collective-permute-done.8 = f32[2,1024]{1,0:T(2,128)S(1)} collective-permute-done((f32[2,1024]{1,0:T(2,128)S(1)}, f32[2,1024]{1,0:T(2,128)S(1)}, u32[]{:S(2)}, u32[]{:S(2)}) %collective-permute-start.8) | collective-permute-done | bytes 8224 | tf_op jit(solution)/shard_map/ppermute | solution.py:42
  191.4 2.3 %fusion.18 = f32[2048,256]{0,1:T(8,128)S(1)} fusion(bf16[2048,1024]{1,0:T(8,128)(2,1)S(1)} %copy-done.1, bf16[1024,4,256]{2,0,1:T(8,128)(2,1)} %copy-done.4), kind=kOutput, calls=%fused_computation.43 | convolution fusion | flops 1073741824 | bytes 6815744 | tf_op jit(solution)/shard_map/dot_general | solution.py:87
  193.7 0.0 copy-start.6
  193.8 4.0 %fusion.10 = (f32[2048]{0:T(1024)S(1)}, f32[2048,256]{0,1:T(8,128)}, f32[2048,256]{0,1:T(8,128)S(1)}) fusion(f32[256]{0:T(256)S(1)} %bitcast.66, f32[2048]{0:T(1024)S(1)} %broadcast_divide_fusion, f32[2048,256]{0,1:T(8,128)S(1)} %collective-permute-done.3, f32[2048,256]{0,1:T(8,128)S(1)} %fusion.18, f32[2048,512]{0,1:T(8,128)} %collective-permute-done.2, ...), kind=kLoop, calls=%fused_computation.27 | loop fusion | flops 4192256 | bytes 11551744 | tf_op jit(solution)/shard_map/reduce_sum | solution.py:151
  197.8 2.2 fusion.19
  200.0 1.6 collective-permute-start.11
  201.5 1.5 collective-permute-start.10
  203.0 0.6 collective-permute-done.11
  203.6 2.9 %copy.82 = f32[2048,256]{1,0:T(8,128)} copy(f32[2048,256]{0,1:T(8,128)} %get-tuple-element.35) | data formatting | bytes 4194304
  206.4 1.8 copy.83
  208.3 2.1 collective-permute-start.13
  210.3 0.6 add_add_fusion
  210.9 1.8 collective-permute-done.13
  212.8 0.6 add_add_fusion.1
  (55 shorter events, 0.2 us)
Async XLA Ops:
  7.2 3.1 %copy-start.2 = (f32[2048,256]{1,0:T(8,128)S(1)}, f32[2048,256]{1,0:T(8,128)}, u32[]{:S(2)}) copy-start(f32[2048,256]{1,0:T(8,128)} %param.10) | copy-start | bytes 6291460
  7.2 79.2 %all-gather.2.cloned.1.call-start = ((), (), s32[]{:S(2)}) async-start(), calls=%async_computation.1 | async-start | bytes 2359296 | tf_op jit(solution)/shard_map/all_gather | solution.py:134
  12.1 19.2 %copy-start.8 = (f32[1024,128]{1,0:T(8,128)S(1)}, f32[1024,128]{1,0:T(8,128)}, u32[]{:S(2)}) copy-start(f32[1024,128]{1,0:T(8,128)} %param.14) | copy-start | bytes 1572868
  12.1 19.2 %copy-start.9 = (f32[1024,128]{1,0:T(8,128)S(1)}, f32[1024,128]{1,0:T(8,128)}, u32[]{:S(2)}) copy-start(f32[1024,128]{1,0:T(8,128)} %param.13) | copy-start | bytes 1572868
  28.2 26.3 %collective-permute-start = (bf16[2048,1,256]{0,2,1:T(8,128)(2,1)S(1)}, bf16[2048,1,256]{0,2,1:T(8,128)(2,1)}, u32[]{:S(2)}, u32[]{:S(2)}) collective-permute-start(bf16[2048,1,256]{0,2,1:T(8,128)(2,1)S(1)} %bitcast.58), channel_id=1, source_target_pairs={{0,2},{1,3},{2,0},{3,1},{4,6},{5,7},{6,4},{7,5},{8,10},{9,11},{10,... | collective-permute-start | bytes 3145736 | tf_op jit(solution)/shard_map/ppermute | solution.py:54
  35.7 162.1 %reduce-scatter.2.cloned.1.call-start = ((), (), s32[]{:S(2)}) async-start(), calls=%async_computation.2 | async-start | bytes 4718592 | tf_op jit(solution)/shard_map/reduce_scatter | solution.py:153
  55.8 1.5 copy-start.12
  57.4 17.0 %collective-permute-start.1 = (bf16[2048,2,256]{0,2,1:T(8,128)(2,1)}, bf16[2048,2,256]{0,2,1:T(8,128)(2,1)}, u32[]{:S(2)}, u32[]{:S(2)}) collective-permute-start(bf16[2048,2,256]{0,2,1:T(8,128)(2,1)} %maximum_bitcast_fusion), channel_id=1, source_target_pairs={{0,1},{1,0},{2,3},{3,2},{4,5},{5,4},{6,7},{7,6},{8,9},{9,8},{10,11... | collective-permute-start | bytes 6291464 | tf_op jit(solution)/shard_map/ppermute | solution.py:54
  69.0 5.3 %copy-start.13 = (s32[4]{0:T(128)S(1)}, s32[4]{0:T(128)}, u32[]{:S(2)}) copy-start(s32[4]{0:T(128)} %constant.85.clone) | copy-start | bytes 52
  86.4 12.3 %copy-start.5 = (bf16[2048,2,2,256]{0,3,2,1:T(8,128)(2,1)S(1)}, bf16[2048,2,2,256]{0,3,2,1:T(8,128)(2,1)}, u32[]{:S(2)}) copy-start(bf16[2048,2,2,256]{0,3,2,1:T(8,128)(2,1)} %copy.77) | copy-start | bytes 12582916
  96.7 2.0 copy-start
  104.8 1.6 copy-start.7
  110.4 1.3 copy-start.4
  113.1 6.9 %copy-start.3 = (f32[2048,256]{1,0:T(8,128)S(1)}, f32[2048,256]{1,0:T(8,128)}, u32[]{:S(2)}) copy-start(f32[2048,256]{1,0:T(8,128)} %param.10) | copy-start | bytes 6291460
  120.0 7.5 %collective-permute-start.2 = (f32[2048,512]{0,1:T(8,128)}, f32[2048,512]{0,1:T(8,128)}, u32[]{:S(2)}, u32[]{:S(2)}) collective-permute-start(f32[2048,512]{0,1:T(8,128)} %fusion.27), channel_id=1, source_target_pairs={{0,1},{1,0},{2,3},{3,2},{4,5},{5,4},{6,7},{7,6},{8,9},{9,8},{10,11... | collective-permute-start | bytes 12582920 | tf_op jit(solution)/shard_map/ppermute | solution.py:92
  120.0 7.5 %copy-start.1 = (bf16[2048,1024]{1,0:T(8,128)(2,1)S(1)}, bf16[2048,1024]{1,0:T(8,128)(2,1)}, u32[]{:S(2)}) copy-start(bf16[2048,1024]{1,0:T(8,128)(2,1)} %copy-done) | copy-start | bytes 12582916
  122.2 60.2 %copy-start.10 = (f32[2048]{0:T(1024)S(1)}, f32[2048]{0:T(1024)}, u32[]{:S(2)}) copy-start(f32[2048]{0:T(1024)} %param.12) | copy-start | bytes 24580
  122.2 65.6 %copy-start.11 = (f32[1024]{0:T(1024)S(1)}, f32[1024]{0:T(1024)}, u32[]{:S(2)}) copy-start(f32[1024]{0:T(1024)} %param.15) | copy-start | bytes 12292
  130.7 63.0 %collective-permute-start.3 = (f32[2048,256]{0,1:T(8,128)S(1)}, f32[2048,256]{0,1:T(8,128)S(1)}, u32[]{:S(2)}, u32[]{:S(2)}) collective-permute-start(f32[2048,256]{0,1:T(8,128)S(1)} %slice_add_fusion), channel_id=1, source_target_pairs={{0,2},{1,3},{2,0},{3,1},{4,6},{5,7},{6,4},{7,5},{8,10},{9,11},{10,... | collective-permute-start | bytes 6291464 | tf_op jit(solution)/shard_map/ppermute | solution.py:92
  132.3 1.2 collective-permute-start.4
  133.5 45.1 %collective-permute-start.5 = (f32[2,1024]{1,0:T(2,128)S(1)}, f32[2,1024]{1,0:T(2,128)S(1)}, u32[]{:S(2)}, u32[]{:S(2)}) collective-permute-start(f32[2,1024]{1,0:T(2,128)S(1)} %fusion.24), channel_id=1, source_target_pairs={{0,2},{1,3},{2,0},{3,1},{4,6},{5,7},{6,4},{7,5},{8,10},{9,11},{10,... | collective-permute-start | bytes 24584 | tf_op jit(solution)/shard_map/ppermute | solution.py:42
  178.6 3.7 %collective-permute-start.6 = (f32[2,1024]{1,0:T(2,128)S(1)}, f32[2,1024]{1,0:T(2,128)S(1)}, u32[]{:S(2)}, u32[]{:S(2)}) collective-permute-start(f32[2,1024]{1,0:T(2,128)S(1)} %fusion.37), channel_id=1, source_target_pairs={{0,4},{4,0},{8,12},{12,8},{16,20},{20,16},{24,28},{28,24},{1,5},{5... | collective-permute-start | bytes 24584 | tf_op jit(solution)/shard_map/ppermute | solution.py:42
  182.3 4.4 %collective-permute-start.7 = (f32[2,1024]{1,0:T(2,128)S(1)}, f32[2,1024]{1,0:T(2,128)S(1)}, u32[]{:S(2)}, u32[]{:S(2)}) collective-permute-start(f32[2,1024]{1,0:T(2,128)S(1)} %add.130), channel_id=1, source_target_pairs={{0,8},{4,12},{8,0},{12,4},{16,24},{20,28},{24,16},{28,20},{1,9},{5... | collective-permute-start | bytes 24584 | tf_op jit(solution)/shard_map/ppermute | solution.py:42
  186.7 4.6 %collective-permute-start.8 = (f32[2,1024]{1,0:T(2,128)S(1)}, f32[2,1024]{1,0:T(2,128)S(1)}, u32[]{:S(2)}, u32[]{:S(2)}) collective-permute-start(f32[2,1024]{1,0:T(2,128)S(1)} %add.131), channel_id=1, source_target_pairs={{0,16},{4,20},{8,24},{12,28},{16,0},{20,4},{24,8},{28,12},{1,17},{... | collective-permute-start | bytes 24584 | tf_op jit(solution)/shard_map/ppermute | solution.py:42
  193.7 4.0 %copy-start.6 = (bf16[1024,128]{1,0:T(8,128)(2,1)S(1)}, bf16[1024,128]{1,0:T(8,128)(2,1)}, u32[]{:S(2)}) copy-start(bf16[1024,128]{1,0:T(8,128)(2,1)} %get-tuple-element.42) | copy-start | bytes 786436
  197.8 3.7 %collective-permute-start.9 = (f32[2048]{0:T(1024)S(1)}, f32[2048]{0:T(1024)S(1)}, u32[]{:S(2)}, u32[]{:S(2)}) collective-permute-start(f32[2048]{0:T(1024)S(1)} %get-tuple-element.34), channel_id=1, source_target_pairs={{0,1},{1,0},{2,3},{3,2},{4,5},{5,4},{6,7},{7,6},{8,9},{9,8},{10,11... | collective-permute-start | bytes 24584 | tf_op jit(solution)/shard_map/ppermute | solution.py:42
  200.0 3.6 %collective-permute-start.11 = (f32[1024]{0:T(1024)S(1)}, f32[1024]{0:T(1024)S(1)}, u32[]{:S(2)}, u32[]{:S(2)}) collective-permute-start(f32[1024]{0:T(1024)S(1)} %get-tuple-element.32), channel_id=1, source_target_pairs={{0,4},{4,0},{8,12},{12,8},{16,20},{20,16},{24,28},{28,24},{1,5},{5... | collective-permute-start | bytes 12296 | tf_op jit(solution)/shard_map/ppermute | solution.py:42
  201.5 8.8 %collective-permute-start.10 = (f32[2048]{0:T(1024)S(1)}, f32[2048]{0:T(1024)S(1)}, u32[]{:S(2)}, u32[]{:S(2)}) collective-permute-start(f32[2048]{0:T(1024)S(1)} %add.136), channel_id=1, source_target_pairs={{0,2},{1,3},{2,0},{3,1},{4,6},{5,7},{6,4},{7,5},{8,10},{9,11},{10,... | collective-permute-start | bytes 24584 | tf_op jit(solution)/shard_map/ppermute | solution.py:42
  203.6 4.7 %collective-permute-start.12 = (f32[1024]{0:T(1024)S(1)}, f32[1024]{0:T(1024)S(1)}, u32[]{:S(2)}, u32[]{:S(2)}) collective-permute-start(f32[1024]{0:T(1024)S(1)} %add.146), channel_id=1, source_target_pairs={{0,8},{4,12},{8,0},{12,4},{16,24},{20,28},{24,16},{28,20},{1,9},{5... | collective-permute-start | bytes 12296 | tf_op jit(solution)/shard_map/ppermute | solution.py:42
  208.3 4.5 %collective-permute-start.13 = (f32[1024]{0:T(1024)S(1)}, f32[1024]{0:T(1024)S(1)}, u32[]{:S(2)}, u32[]{:S(2)}) collective-permute-start(f32[1024]{0:T(1024)S(1)} %add.147), channel_id=1, source_target_pairs={{0,16},{4,20},{8,24},{12,28},{16,0},{20,4},{24,8},{28,12},{1,17},{... | collective-permute-start | bytes 12296 | tf_op jit(solution)/shard_map/ppermute | solution.py:42
Sparse Core Ops, SparseCore 0:
  35.8 50.5 all-gather.1
  105.0 87.0 reduce-scatter.1

commit v7 on v6

--- a/solution.py
+++ b/solution.py
@@ -2,6 +2,7 @@
 import jax.numpy as jnp
 from jax import lax
 from jax.sharding import PartitionSpec as P
+
 
 BLK = 256
 UB = 8
@@ -116,8 +117,8 @@
     factors = theta_shape.shape[1] * item_width
     beta_columns = factors // user_width
     theta_columns = factors // item_width
+    beta_part = exp_mean_log(beta_shape, beta_rate)
     theta_part = exp_mean_log(theta_shape, theta_rate)
-    beta_part = exp_mean_log(beta_shape, beta_rate)
     beta_local = jnp.sum(beta_shape / beta_rate, axis=0)
     theta_local = jnp.sum(theta_shape / theta_rate, axis=0)
     beta_placed = lax.dynamic_update_slice_in_dim(
@@ -127,13 +128,14 @@
         jnp.zeros((factors,), jnp.float32), theta_local, item_index * theta_columns, 0
     )
     placed = jnp.stack([beta_placed, theta_placed])
-    placed = doubling_sum(doubling_sum(placed, "item", item_width), "user", user_width)
-    beta_total = placed[0]
-    theta_total = placed[1]
     theta_full = doubling_gather(theta_part, "item", item_width, item_index)
     beta_full = lax.all_gather(beta_part, "user", axis=1, tiled=True)
     user_rows = theta_full.shape[0]
     item_rows = beta_full.shape[0]
+    placed, beta_full = lax.optimization_barrier((placed, beta_full))
+    placed = doubling_sum(doubling_sum(placed, "item", item_width), "user", user_width)
+    beta_total = placed[0]
+    theta_total = placed[1]
     grid = dense_counts(tile_slots, tile_counts, live_tiles)
     counts = grid.transpose(0, 2, 1, 3).reshape(user_rows, item_rows).astype(jnp.float32)
     denominator = lax.dot_general(
@@ -155,8 +157,10 @@
     eta_mean = (prior_c2 + factors * prior_c) / eta_rate
     theta_slice = lax.dynamic_slice_in_dim(theta_total, user_index * beta_columns, beta_columns, 0)
     beta_rate_new = eta_mean[:, None] + theta_slice[None, :]
-    item_part = jnp.sum(beta_shape_new / beta_rate_new, axis=1)
-    eta_rate_new = prior_c2 / prior_d2 + doubling_sum(item_part, "user", user_width)
+    rate_every = eta_mean[:, None] + theta_total[None, :]
+    prior_part = jnp.sum(prior_c / rate_every, axis=1)
+    device_part = jnp.sum(beta_full.astype(jnp.float32) / rate_every * item_acc, axis=1)
+    eta_rate_new = prior_c2 / prior_d2 + (prior_part + doubling_sum(device_part, "user", user_width))
     return (
         theta_shape_new,
         jnp.log(theta_rate_new),

time: 221 us -> 212 us (0.959)
  waiting for transfers between devices: 89 us -> 79.7 us
  matrix products: 28.9 us -> 22.1 us
  local copies, waits for them, and re-layouts: 32.2 us -> 36.1 us
  starting transfers between devices: 13.1 us -> 16.9 us
    ppermute x10, waiting for transfers between devices: 58 us -> 7.35 us  [doubling_sum(): value = value + lax.ppermute(value, axis_name, perm)]
    ppermute x2, waiting for transfers between devices: 5.33 us -> 43.7 us  [halving_user_sums(): received = lax.ppermute(terms[step_index], axis_name, perm)]
    reduce_scatter x1, waiting for transfers between devices: 0.01 us -> 15.2 us  [on_device(): lax.psum_scatter(item_acc, 'user', scatter_dimension=1, tiled=True)]
    unnamed x33 -> x40, local copies, waits for them, and re-layouts: 19.7 us -> 28.2 us
    all_gather x1, waiting for transfers between devices: 7.55 us -> 0.01 us  [on_device(): beta_full = lax.all_gather(beta_part, 'user', axis=1, tiled=True)]
    dot_general x3, matrix products: 12.4 us -> 7.29 us  [halving_user_sums(): terms.append(jnp.dot(ratio, piece, preferred_element_type=jnp.float32))]
    ppermute x2, waiting for transfers between devices: 18.1 us -> 13.4 us  [doubling_gather(): other = lax.ppermute(held, axis_name, perm)]
    dot_general x1, matrix products: 10.3 us -> 6.15 us  [on_device(): lax.dot_general(theta_full, beta_full, (((1,), (1,)), ((), ())), preferre...]
  transfers between devices with their start and end apart: 16 -> 16, of which waited for: 10 -> 9; matrix products, arithmetic and copies ran while one was open for 27% -> 36% of each run, Pallas kernels for 0% -> 0%
where the time goes in v7:
time: 212 us
  waiting for transfers between devices  79.7 us (38%)
  other arithmetic  42 us (20%)
  local copies, waits for them, and re-layouts  36.1 us (17%)
  matrix products  22.1 us (10%)
  starting transfers between devices  16.9 us (8%)
  between operations  15 us (7%)
    ppermute x2, waiting for transfers between devices, halving_user_sums(): received = lax.ppermute(terms[step_index], axis_name, perm)  43.7 us
    unnamed x40, local copies, waits for them, and re-layouts  28.2 us
    convert_element_type x2, other arithmetic, exp_mean_log(): jnp.exp(lax.digamma(shape_param) - jnp.log(rate_param)).astype(jnp.bfloat16)  20.4 us
    reduce_scatter x1, waiting for transfers between devices, on_device(): lax.psum_scatter(item_acc, 'user', scatter_dimension=1, tiled=True)  15.2 us
    ppermute x2, waiting for transfers between devices, doubling_gather(): other = lax.ppermute(held, axis_name, perm)  13.4 us
    ppermute x10, starting transfers between devices, doubling_sum(): value = value + lax.ppermute(value, axis_name, perm)  12.1 us
    dot_general x1, matrix products, on_device(): lax.dot_general(ratio, theta_full, (((0,), (0,)), ((), ())), preferred_el...  8.63 us
    ppermute x10, waiting for transfers between devices, doubling_sum(): value = value + lax.ppermute(value, axis_name, perm)  7.35 us
  transfers between devices with their start and end apart: 16, of which 9 were waited for; matrix products, arithmetic and copies ran while one was open for 36% of the time, Pallas kernels for 0%

profile of v7, /device:TPU:0, one launch (start us, length us, event | category | flops | bytes accessed | tf_op | source)
XLA Modules:
  0.0 211.7 jit_solution(10529148941933653213)
XLA Ops:
  7.2 1.2 copy.90
  8.5 1.2 copy.81
  9.7 4.4 %fusion.19 = bf16[1024,128]{0,1:T(8,128)(2,1)} fusion(f32[1024,128]{0,1:T(8,128)S(1)} %copy.90, f32[1024,128]{0,1:T(8,128)S(1)} %copy.81), kind=kLoop, calls=%fused_computation.41 | loop fusion | flops 10092544 | bytes 1310720 | tf_op jit(solution)/shard_map/convert_element_type | solution.py:22
  14.1 0.0 reduce-scatter.2.cloned.1.call-start
  14.2 3.0 %copy.78 = f32[2048,256]{0,1:T(8,128)} copy(f32[2048,256]{1,0:T(8,128)} %param.11) | data formatting | bytes 4194304 | tf_op args[1]
  17.2 1.8 copy.69
  19.0 16.0 %fusion.9 = bf16[2048,256]{0,1:T(8,128)(2,1)S(1)} fusion(f32[2048,256]{0,1:T(8,128)} %copy.78, f32[2048,256]{0,1:T(8,128)} %copy.69), kind=kLoop, calls=%fused_computation.20 | loop fusion | flops 40370176 | bytes 5242880 | tf_op jit(solution)/shard_map/convert_element_type | solution.py:22
  35.1 3.0 %collective-permute-start = (bf16[2048,1,256]{0,2,1:T(8,128)(2,1)S(1)}, bf16[2048,1,256]{0,2,1:T(8,128)(2,1)}, u32[]{:S(2)}, u32[]{:S(2)}) collective-permute-start(bf16[2048,1,256]{0,2,1:T(8,128)(2,1)S(1)} %bitcast.56), channel_id=1, source_target_pairs={{0,2},{1,3},{2,0},{3,1},{4,6},{5,7},{6,4},{7,5},{8,10},{9,11},{10,... | collective-permute-start | bytes 3145736 | tf_op jit(solution)/shard_map/ppermute | solution.py:55
  38.8 0.6 iota_reduce_fusion
  39.4 0.1 broadcast_in_dim.49
  39.5 0.1 fusion.24
  39.6 0.1 broadcast_in_dim.47
  39.7 5.0 %gather_fusion = bf16[32,256,256]{2,1,0:T(8,128)(2,1)} fusion(bf16[32,256,256]{2,1,0:T(8,128)(2,1)} %bitcast.60, s32[1024]{0:T(1024)S(1)} %pad_clamp_fusion.1), kind=kCustom, calls=%fused_computation | custom fusion | bytes 8388736 | tf_op jit(solution)/shard_map/jit(_take)/gather | solution.py:34
  44.7 1.4 divide_reduce_fusion.1
  46.0 1.9 divide_reduce_fusion
  48.0 13.4 %collective-permute-done = bf16[2048,1,256]{0,2,1:T(8,128)(2,1)} collective-permute-done((bf16[2048,1,256]{0,2,1:T(8,128)(2,1)S(1)}, bf16[2048,1,256]{0,2,1:T(8,128)(2,1)}, u32[]{:S(2)}, u32[]{:S(2)}) %collective-permute-start) | collective-permute-done | bytes 1048608 | tf_op jit(solution)/shard_map/ppermute | solution.py:55
  61.4 1.4 select_bitcast_fusion.4
  62.8 1.5 maximum_bitcast_fusion
  64.4 1.3 copy-done
  65.7 6.4 %fusion.3 = f32[8,4,256,256]{3,1,2,0:T(4,128)} fusion(bf16[8,4,256,256]{3,2,1,0:T(8,128)(2,1)S(1)} %bitcast.55, pred[8,4]{1,0:T(8,128)(4,1)S(1)} %broadcast_in_dim.49, pred[8,4]{1,0:T(8,128)(4,1)S(1)} %broadcast_in_dim.47), kind=kLoop, calls=%fused_computation.10 | loop fusion | flops 6291456 | bytes 12582976 | tf_op jit(solution)/shard_map/convert_element_type | solution.py:140
  72.1 8.7 %copy.98 = f32[256,8,4,256]{3,1,2,0:T(8,128)} copy(f32[256,8,4,256]{3,2,1,0:T(4,128)} %bitcast.54) | data formatting | bytes 16777216
  80.8 1.8 collective-permute-start.5
  82.6 1.9 select_bitcast_fusion.2
  84.5 0.0 collective-permute-done.5
  84.6 1.8 collective-permute-start.6
  86.3 0.4 pad_maximum_fusion
  86.7 0.3 copy.80
  87.1 1.2 collective-permute-done.6
  88.3 1.8 collective-permute-start.7
  90.0 1.4 slice-done.1
  91.4 0.6 copy-done.8
  92.0 6.1 %divide_convert_fusion = bf16[2048,1024]{1,0:T(8,128)(2,1)} fusion(f32[2048,1024]{1,0:T(8,128)S(1)} %bitcast.59, bf16[2048,1024]{0,1:T(8,128)(2,1)S(1)} %bitcast.61, bf16[1024,1024]{0,1:T(8,128)(2,1)S(1)} %copy-done.8), kind=kOutput, calls=%fused_computation.2 | convolution fusion | flops 4299161600 | bytes 18874368 | tf_op jit(solution)/shard_map/dot_general | solution.py:141
  98.2 2.3 %gather_fusion.1 = bf16[4,1024,256]{1,2,0:T(8,128)(2,1)S(1)} fusion(bf16[1024,4,256]{0,2,1:T(8,128)(2,1)} %bitcast.63, s32[1024]{0:T(1024)S(1)} %pad_clamp_fusion), kind=kCustom, calls=%fused_computation.1 | custom fusion | bytes 4194320 | tf_op jit(solution)/shard_map/jit(_take)/gather | solution.py:77
  100.5 2.7 %collective-permute-start.8 = (f32[2,1024]{1,0:T(2,128)S(1)}, f32[2,1024]{1,0:T(2,128)S(1)}, u32[]{:S(2)}, u32[]{:S(2)}) collective-permute-start(f32[2,1024]{1,0:T(2,128)S(1)} %add.149), channel_id=1, source_target_pairs={{0,16},{4,20},{8,24},{12,28},{16,0},{20,4},{24,8},{28,12},{1,17},{... | collective-permute-start | bytes 24584 | tf_op jit(solution)/shard_map/ppermute | solution.py:43
  103.1 0.3 select_bitcast_fusion
  103.4 1.3 copy-done.4
  104.7 0.1 slice.33
  104.8 0.3 collective-permute-done.8
  105.1 1.0 copy-done.2
  106.1 0.9 copy-done.9
  106.9 8.6 %fusion.4 = (f32[1024]{0:T(1024)S(1)}, f32[1024]{0:T(1024)S(1)}, f32[1024,1024]{0,1:T(8,128)}) fusion(bf16[1024,1024]{0,1:T(8,128)(2,1)S(1)} %copy-done.9, f32[1024]{0:T(1024)S(1)} %bitcast.67, f32[1024]{0:T(1024)S(1)} %broadcast_divide_fusion.1, bf16[2048,1024]{0,1:T(8,128)(2,1)} %bitcast.62, bf16[2048,1024]{1,0:T(8,128)(2,1)S(1)} %copy-done.2), kind=kOutput, calls=%fused_computation.11 | convolution fusion | flops 4302305280 | bytes 14696448 | tf_op jit(solution)/shard_map/dot_general | solution.py:145
  115.6 4.7 %fusion.28 = f32[2048,512]{0,1:T(8,128)S(1)} fusion(bf16[2048,1024]{1,0:T(8,128)(2,1)} %divide_convert_fusion, bf16[1024,512]{0,1:T(8,128)(2,1)S(1)} %bitcast.64), kind=kOutput, calls=%fused_computation.72 | convolution fusion | flops 2147483648 | bytes 9437184 | tf_op jit(solution)/shard_map/dot_general | solution.py:88
  120.3 0.1 collective-permute-start.2
  120.4 7.1 %collective-permute-done.2 = f32[2048,512]{0,1:T(8,128)S(1)} collective-permute-done((f32[2048,512]{0,1:T(8,128)S(1)}, f32[2048,512]{0,1:T(8,128)S(1)}, u32[]{:S(2)}, u32[]{:S(2)}) %collective-permute-start.2) | collective-permute-done | bytes 4194336 | tf_op jit(solution)/shard_map/ppermute | solution.py:93
  127.6 1.3 slice_add_fusion
  128.9 1.6 collective-permute-start.3
  130.4 1.3 fusion.21
  131.7 0.6 collective-permute-start.11
  132.3 3.1 %collective-permute-done.11 = f32[1024]{0:T(1024)S(1)} collective-permute-done((f32[1024]{0:T(1024)S(1)}, f32[1024]{0:T(1024)S(1)}, u32[]{:S(2)}, u32[]{:S(2)}) %collective-permute-start.11) | collective-permute-done | bytes 4128 | tf_op jit(solution)/shard_map/ppermute | solution.py:43
  135.4 1.6 collective-permute-start.12
  137.0 2.5 %collective-permute-done.12 = f32[1024]{0:T(1024)S(1)} collective-permute-done((f32[1024]{0:T(1024)S(1)}, f32[1024]{0:T(1024)S(1)}, u32[]{:S(2)}, u32[]{:S(2)}) %collective-permute-start.12) | collective-permute-done | bytes 4128 | tf_op jit(solution)/shard_map/ppermute | solution.py:43
  139.5 0.5 collective-permute-start.13
  140.0 36.6 %collective-permute-done.3 = f32[2048,256]{0,1:T(8,128)S(1)} collective-permute-done((f32[2048,256]{0,1:T(8,128)S(1)}, f32[2048,256]{0,1:T(8,128)S(1)}, u32[]{:S(2)}, u32[]{:S(2)}) %collective-permute-start.3) | collective-permute-done | bytes 2097184 | tf_op jit(solution)/shard_map/ppermute | solution.py:93
  176.6 2.3 %fusion.13 = (f32[2048]{0:T(1024)S(1)}, f32[2048,256]{0,1:T(8,128)}, f32[2048,256]{0,1:T(8,128)S(1)}) fusion(f32[256]{0:T(256)S(1)} %bitcast.65, f32[2048]{0:T(1024)S(1)} %broadcast_divide_fusion, f32[2048,256]{0,1:T(8,128)S(1)} %collective-permute-done.3, f32[2048,256]{0,1:T(8,128)S(1)} %fusion.21, f32[2048,512]{0,1:T(8,128)S(1)} %collective-permute-done.2, ...), kind=kLoop, calls=%fused_computation.31 | loop fusion | flops 4192256 | bytes 11551744 | tf_op jit(solution)/shard_map/reduce_sum | solution.py:153
  178.9 1.0 add_log_fusion.1
  179.9 0.2 collective-permute-done.9
  180.1 1.5 collective-permute-start.10
  181.6 0.6 add_add_fusion.1
  182.2 2.9 %copy.93 = f32[2048,256]{1,0:T(8,128)} copy(f32[2048,256]{0,1:T(8,128)} %get-tuple-element.33) | data formatting | bytes 4194304
  185.1 1.8 copy.94
  186.9 0.6 add_add_fusion
  187.5 15.2 %reduce-scatter.2.cloned.1.call-done = f32[1024,128]{0,1:T(8,128)} async-done(((f32[1024,1024]{0,1:T(8,128)}), f32[1024,128]{0,1:T(8,128)}) %reduce-scatter.2.cloned.1.call-update) | async-done | bytes 524304 | tf_op jit(solution)/shard_map/reduce_scatter | solution.py:155
  202.7 1.1 multiply_add_fusion
  203.8 1.0 copy.95
  (63 shorter events, 0.3 us)
Async XLA Ops:
  7.2 65.0 %all-gather.2.cloned.1.call-start = ((), (), s32[]{:S(2)}) async-start(), calls=%async_computation.1 | async-start | bytes 2359296 | tf_op jit(solution)/shard_map/all_gather | solution.py:132
  14.1 3.1 %copy-start.1 = (f32[2048,256]{1,0:T(8,128)S(1)}, f32[2048,256]{1,0:T(8,128)}, u32[]{:S(2)}) copy-start(f32[2048,256]{1,0:T(8,128)} %param.10) | copy-start | bytes 6291460
  14.1 188.6 %reduce-scatter.2.cloned.1.call-start = ((), (), s32[]{:S(2)}) async-start(), calls=%async_computation.2 | async-start | bytes 4718592 | tf_op jit(solution)/shard_map/reduce_scatter | solution.py:155
  19.0 19.7 %copy-start.12 = (s32[1,1,32]{2,1,0:T(1,128)S(1)}, s32[1,1,32]{2,1,0:T(1,128)}, u32[]{:S(2)}) copy-start(s32[1,1,32]{2,1,0:T(1,128)} %param.16) | copy-start | bytes 388
  35.1 26.3 %collective-permute-start = (bf16[2048,1,256]{0,2,1:T(8,128)(2,1)S(1)}, bf16[2048,1,256]{0,2,1:T(8,128)(2,1)}, u32[]{:S(2)}, u32[]{:S(2)}) collective-permute-start(bf16[2048,1,256]{0,2,1:T(8,128)(2,1)S(1)} %bitcast.56), channel_id=1, source_target_pairs={{0,2},{1,3},{2,0},{3,1},{4,6},{5,7},{6,4},{7,5},{8,10},{9,11},{10,... | collective-permute-start | bytes 3145736 | tf_op jit(solution)/shard_map/ppermute | solution.py:55
  62.7 1.6 copy-start.13
  62.7 1.6 copy-start.11
  62.7 3.0 %copy-start = (bf16[32,256,256]{2,1,0:T(8,128)(2,1)S(1)}, bf16[32,256,256]{2,1,0:T(8,128)(2,1)}, u32[]{:S(2)}) copy-start(bf16[32,256,256]{2,1,0:T(8,128)(2,1)} %gather_fusion) | copy-start | bytes 12582916
  64.3 18.4 %collective-permute-start.1 = (bf16[2048,2,256]{0,2,1:T(8,128)(2,1)}, bf16[2048,2,256]{0,2,1:T(8,128)(2,1)}, u32[]{:S(2)}, u32[]{:S(2)}) collective-permute-start(bf16[2048,2,256]{0,2,1:T(8,128)(2,1)} %maximum_bitcast_fusion), channel_id=1, source_target_pairs={{0,1},{1,0},{2,3},{3,2},{4,5},{5,4},{6,7},{7,6},{8,9},{9,8},{10,11... | collective-permute-start | bytes 6291464 | tf_op jit(solution)/shard_map/ppermute | solution.py:55
  72.1 8.7 %collective-permute-start.4 = (f32[2,1024]{1,0:T(2,128)S(1)}, f32[2,1024]{1,0:T(2,128)S(1)}, u32[]{:S(2)}, u32[]{:S(2)}) collective-permute-start(f32[2,1024]{1,0:T(2,128)S(1)} %pad_maximum_fusion.1), channel_id=1, source_target_pairs={{0,1},{1,0},{2,3},{3,2},{4,5},{5,4},{6,7},{7,6},{8,9},{9,8},{10,11... | collective-permute-start | bytes 24584 | tf_op jit(solution)/shard_map/ppermute | solution.py:43
  80.8 3.7 %collective-permute-start.5 = (f32[2,1024]{1,0:T(2,128)S(1)}, f32[2,1024]{1,0:T(2,128)S(1)}, u32[]{:S(2)}, u32[]{:S(2)}) collective-permute-start(f32[2,1024]{1,0:T(2,128)S(1)} %add.146), channel_id=1, source_target_pairs={{0,2},{1,3},{2,0},{3,1},{4,6},{5,7},{6,4},{7,5},{8,10},{9,11},{10,... | collective-permute-start | bytes 24584 | tf_op jit(solution)/shard_map/ppermute | solution.py:43
  84.6 3.7 %collective-permute-start.6 = (f32[2,1024]{1,0:T(2,128)S(1)}, f32[2,1024]{1,0:T(2,128)S(1)}, u32[]{:S(2)}, u32[]{:S(2)}) collective-permute-start(f32[2,1024]{1,0:T(2,128)S(1)} %add.147), channel_id=1, source_target_pairs={{0,4},{4,0},{8,12},{12,8},{16,20},{20,16},{24,28},{28,24},{1,5},{5... | collective-permute-start | bytes 24584 | tf_op jit(solution)/shard_map/ppermute | solution.py:43
  86.3 3.7 %slice-start = ((s8[8388608]{0:T(1024)(128)(4,1)}), s8[4194304]{0:T(1024)(128)(4,1)S(1)}, s32[]{:S(2)}) async-start(s8[8388608]{0:T(1024)(128)(4,1)} %bitcast.57), calls=%async_computation.3 | async-start | bytes 8388608
  86.7 4.7 %slice-start.1 = ((s8[8388608]{0:T(1024)(128)(4,1)}), s8[4194304]{0:T(1024)(128)(4,1)S(1)}, s32[]{:S(2)}) async-start(s8[8388608]{0:T(1024)(128)(4,1)} %bitcast.57), calls=%async_computation.4 | async-start | bytes 8388608
  86.7 5.3 %copy-start.8 = (bf16[1024,1024]{0,1:T(8,128)(2,1)S(1)}, bf16[1024,1024]{0,1:T(8,128)(2,1)}, u32[]{:S(2)}) copy-start(bf16[1024,1024]{0,1:T(8,128)(2,1)} %all-gather.2.cloned.1.call-done) | copy-start | bytes 6291460
  87.1 11.1 %copy-start.6 = (bf16[2048,2,2,256]{0,3,2,1:T(8,128)(2,1)}, bf16[2048,2,2,256]{0,3,2,1:T(8,128)(2,1)S(1)}, u32[]{:S(2)}) copy-start(bf16[2048,2,2,256]{0,3,2,1:T(8,128)(2,1)S(1)} %copy.80) | copy-start | bytes 12582916
  88.3 12.2 %collective-permute-start.7 = (f32[2,1024]{1,0:T(2,128)S(1)}, f32[2,1024]{1,0:T(2,128)S(1)}, u32[]{:S(2)}, u32[]{:S(2)}) collective-permute-start(f32[2,1024]{1,0:T(2,128)S(1)} %add.148), channel_id=1, source_target_pairs={{0,8},{4,12},{8,0},{12,4},{16,24},{20,28},{24,16},{28,20},{1,9},{5... | collective-permute-start | bytes 24584 | tf_op jit(solution)/shard_map/ppermute | solution.py:43
  100.5 4.6 %collective-permute-start.8 = (f32[2,1024]{1,0:T(2,128)S(1)}, f32[2,1024]{1,0:T(2,128)S(1)}, u32[]{:S(2)}, u32[]{:S(2)}) collective-permute-start(f32[2,1024]{1,0:T(2,128)S(1)} %add.149), channel_id=1, source_target_pairs={{0,16},{4,20},{8,24},{12,28},{16,0},{20,4},{24,8},{28,12},{1,17},{... | collective-permute-start | bytes 24584 | tf_op jit(solution)/shard_map/ppermute | solution.py:43
  103.1 2.9 %copy-start.2 = (bf16[2048,1024]{1,0:T(8,128)(2,1)S(1)}, bf16[2048,1024]{1,0:T(8,128)(2,1)}, u32[]{:S(2)}) copy-start(bf16[2048,1024]{1,0:T(8,128)(2,1)} %divide_convert_fusion) | copy-start | bytes 12582916
  103.4 1.3 copy-start.4
  104.7 2.2 %copy-start.9 = (bf16[1024,1024]{0,1:T(8,128)(2,1)S(1)}, bf16[1024,1024]{0,1:T(8,128)(2,1)}, u32[]{:S(2)}) copy-start(bf16[1024,1024]{0,1:T(8,128)(2,1)} %all-gather.2.cloned.1.call-done) | copy-start | bytes 6291460
  115.6 12.0 %copy-start.3 = (bf16[2048,1024]{1,0:T(8,128)(2,1)S(1)}, bf16[2048,1024]{1,0:T(8,128)(2,1)}, u32[]{:S(2)}) copy-start(bf16[2048,1024]{1,0:T(8,128)(2,1)} %divide_convert_fusion) | copy-start | bytes 12582916
  115.6 12.0 %copy-start.5 = (bf16[1024,4,256]{0,2,1:T(8,128)(2,1)S(1)}, bf16[1024,4,256]{0,2,1:T(8,128)(2,1)}, u32[]{:S(2)}) copy-start(bf16[1024,4,256]{0,2,1:T(8,128)(2,1)} %copy-done.4) | copy-start | bytes 6291460
  120.3 10.1 %copy-start.10 = (f32[2048]{0:T(1024)S(1)}, f32[2048]{0:T(1024)}, u32[]{:S(2)}) copy-start(f32[2048]{0:T(1024)} %param.12) | copy-start | bytes 24580
  120.3 7.2 %collective-permute-start.2 = (f32[2048,512]{0,1:T(8,128)S(1)}, f32[2048,512]{0,1:T(8,128)S(1)}, u32[]{:S(2)}, u32[]{:S(2)}) collective-permute-start(f32[2048,512]{0,1:T(8,128)S(1)} %fusion.28), channel_id=1, source_target_pairs={{0,1},{1,0},{2,3},{3,2},{4,5},{5,4},{6,7},{7,6},{8,9},{9,8},{10,11... | collective-permute-start | bytes 12582920 | tf_op jit(solution)/shard_map/ppermute | solution.py:93
  128.9 47.7 %collective-permute-start.3 = (f32[2048,256]{0,1:T(8,128)S(1)}, f32[2048,256]{0,1:T(8,128)S(1)}, u32[]{:S(2)}, u32[]{:S(2)}) collective-permute-start(f32[2048,256]{0,1:T(8,128)S(1)} %slice_add_fusion), channel_id=1, source_target_pairs={{0,2},{1,3},{2,0},{3,1},{4,6},{5,7},{6,4},{7,5},{8,10},{9,11},{10,... | collective-permute-start | bytes 6291464 | tf_op jit(solution)/shard_map/ppermute | solution.py:93
  131.7 3.7 %collective-permute-start.11 = (f32[1024]{0:T(1024)S(1)}, f32[1024]{0:T(1024)S(1)}, u32[]{:S(2)}, u32[]{:S(2)}) collective-permute-start(f32[1024]{0:T(1024)S(1)} %get-tuple-element.30), channel_id=1, source_target_pairs={{0,4},{4,0},{8,12},{12,8},{16,20},{20,16},{24,28},{28,24},{1,5},{5... | collective-permute-start | bytes 12296 | tf_op jit(solution)/shard_map/ppermute | solution.py:43
  135.4 4.1 %collective-permute-start.12 = (f32[1024]{0:T(1024)S(1)}, f32[1024]{0:T(1024)S(1)}, u32[]{:S(2)}, u32[]{:S(2)}) collective-permute-start(f32[1024]{0:T(1024)S(1)} %add.168), channel_id=1, source_target_pairs={{0,8},{4,12},{8,0},{12,4},{16,24},{20,28},{24,16},{28,20},{1,9},{5... | collective-permute-start | bytes 12296 | tf_op jit(solution)/shard_map/ppermute | solution.py:43
  139.5 42.0 %collective-permute-start.13 = (f32[1024]{0:T(1024)S(1)}, f32[1024]{0:T(1024)S(1)}, u32[]{:S(2)}, u32[]{:S(2)}) collective-permute-start(f32[1024]{0:T(1024)S(1)} %add.169), channel_id=1, source_target_pairs={{0,16},{4,20},{8,24},{12,28},{16,0},{20,4},{24,8},{28,12},{1,17},{... | collective-permute-start | bytes 12296 | tf_op jit(solution)/shard_map/ppermute | solution.py:43
  178.9 1.2 collective-permute-start.9
  180.1 6.8 %collective-permute-start.10 = (f32[2048]{0:T(1024)S(1)}, f32[2048]{0:T(1024)S(1)}, u32[]{:S(2)}, u32[]{:S(2)}) collective-permute-start(f32[2048]{0:T(1024)S(1)} %add.154), channel_id=1, source_target_pairs={{0,2},{1,3},{2,0},{3,1},{4,6},{5,7},{6,4},{7,5},{8,10},{9,11},{10,... | collective-permute-start | bytes 24584 | tf_op jit(solution)/shard_map/ppermute | solution.py:43
  185.1 17.6 %copy-start.7 = (bf16[1024,128]{0,1:T(8,128)(2,1)S(1)}, bf16[1024,128]{0,1:T(8,128)(2,1)}, u32[]{:S(2)}) copy-start(bf16[1024,128]{0,1:T(8,128)(2,1)} %fusion.19) | copy-start | bytes 786436
Sparse Core Ops, SparseCore 0:
  14.2 51.8 all-gather.1
  115.7 86.9 reduce-scatter.1

commit v8 on v7

--- a/solution.py
+++ b/solution.py
@@ -132,12 +132,13 @@
     beta_full = lax.all_gather(beta_part, "user", axis=1, tiled=True)
     user_rows = theta_full.shape[0]
     item_rows = beta_full.shape[0]
-    placed, beta_full = lax.optimization_barrier((placed, beta_full))
+    grid = dense_counts(tile_slots, tile_counts, live_tiles)
+    grid = grid.transpose(0, 2, 1, 3).reshape(user_rows, item_rows)
+    placed, beta_full, grid = lax.optimization_barrier((placed, beta_full, grid))
     placed = doubling_sum(doubling_sum(placed, "item", item_width), "user", user_width)
     beta_total = placed[0]
     theta_total = placed[1]
-    grid = dense_counts(tile_slots, tile_counts, live_tiles)
-    counts = grid.transpose(0, 2, 1, 3).reshape(user_rows, item_rows).astype(jnp.float32)
+    counts = grid.astype(jnp.float32)
     denominator = lax.dot_general(
         theta_full, beta_full, (((1,), (1,)), ((), ())), preferred_element_type=jnp.float32
     )
@@ -159,7 +160,9 @@
     beta_rate_new = eta_mean[:, None] + theta_slice[None, :]
     rate_every = eta_mean[:, None] + theta_total[None, :]
     prior_part = jnp.sum(prior_c / rate_every, axis=1)
-    device_part = jnp.sum(beta_full.astype(jnp.float32) / rate_every * item_acc, axis=1)
+    device_part = jnp.sum(
+        beta_full.astype(jnp.float32) / rate_every * lax.optimization_barrier(item_acc), axis=1
+    )
     eta_rate_new = prior_c2 / prior_d2 + (prior_part + doubling_sum(device_part, "user", user_width))
     return (
         theta_shape_new,

time: 212 us -> 204 us (0.962)
  waiting for transfers between devices: 79.7 us -> 73.5 us
  starting transfers between devices: 16.9 us -> 14.5 us
    ppermute x2, waiting for transfers between devices: 43.7 us -> 28.3 us  [halving_user_sums(): received = lax.ppermute(terms[step_index], axis_name, perm)]
    reduce_scatter x1, waiting for transfers between devices: 15.2 us -> 0.01 us  [on_device(): lax.psum_scatter(item_acc, 'user', scatter_dimension=1, tiled=True)]
    all_gather x1, waiting for transfers between devices: 0.01 us -> 13.6 us  [on_device(): beta_full = lax.all_gather(beta_part, 'user', axis=1, tiled=True)]
    ppermute x10, waiting for transfers between devices: 7.35 us -> 19.5 us  [doubling_sum(): value = value + lax.ppermute(value, axis_name, perm)]
    unnamed x40 -> x37, local copies, waits for them, and re-layouts: 28.2 us -> 18.8 us
    convert_element_type x1 -> x0, other arithmetic: 6.42 us -> none  [on_device(): grid.transpose(0, 2, 1, 3).reshape(user_rows, item_rows).astype(jnp.float32)]
    select_n x0 -> x1, other arithmetic: none -> 3.7 us  [dense_counts(): grid = jnp.where(present[:, None, None], grid, jnp.zeros_like(grid))]
    slice x1 -> x2, local copies, waits for them, and re-layouts: 0.07 us -> 3.35 us  [halving_user_sums(): piece = beta_ordered[:, first:first + size].reshape(items, size * block)]
  transfers between devices with their start and end apart: 16 -> 16, of which waited for: 9 -> 11; matrix products, arithmetic and copies ran while one was open for 36% -> 28% of each run, Pallas kernels for 0% -> 0%
where the time goes in v8:
time: 204 us
  waiting for transfers between devices  73.5 us (36%)
  other arithmetic  43.1 us (21%)
  local copies, waits for them, and re-layouts  34.7 us (17%)
  matrix products  23.2 us (11%)
  between operations  15 us (7%)
  starting transfers between devices  14.5 us (7%)
    ppermute x2, waiting for transfers between devices, halving_user_sums(): received = lax.ppermute(terms[step_index], axis_name, perm)  28.3 us
    convert_element_type x2, other arithmetic, exp_mean_log(): jnp.exp(lax.digamma(shape_param) - jnp.log(rate_param)).astype(jnp.bfloat16)  20.5 us
    ppermute x10, waiting for transfers between devices, doubling_sum(): value = value + lax.ppermute(value, axis_name, perm)  19.5 us
    unnamed x37, local copies, waits for them, and re-layouts  18.8 us
    all_gather x1, waiting for transfers between devices, on_device(): beta_full = lax.all_gather(beta_part, 'user', axis=1, tiled=True)  13.6 us
    ppermute x2, waiting for transfers between devices, doubling_gather(): other = lax.ppermute(held, axis_name, perm)  12 us
    ppermute x10, starting transfers between devices, doubling_sum(): value = value + lax.ppermute(value, axis_name, perm)  9.81 us
    dot_general x1, matrix products, on_device(): lax.dot_general(theta_full, beta_full, (((1,), (1,)), ((), ())), preferre...  9.37 us
  transfers between devices with their start and end apart: 16, of which 11 were waited for; matrix products, arithmetic and copies ran while one was open for 28% of the time, Pallas kernels for 0%

profile of v8, /device:TPU:0, one launch (start us, length us, event | category | flops | bytes accessed | tf_op | source)
XLA Modules:
  0.0 203.9 jit_solution(2723609775081605897)
XLA Ops:
  7.2 0.0 all-gather.2.cloned.1.call-start
  7.2 3.0 %copy.66 = f32[2048,256]{0,1:T(8,128)} copy(f32[2048,256]{1,0:T(8,128)} %param.10) | data formatting | bytes 4194304 | tf_op args[0]
  10.3 1.8 copy.75
  12.1 16.1 %fusion.8 = bf16[2048,256]{0,1:T(8,128)(2,1)S(1)} fusion(f32[2048,256]{0,1:T(8,128)} %copy.75, f32[2048,256]{0,1:T(8,128)} %copy.66), kind=kLoop, calls=%fused_computation.19 | loop fusion | flops 40370176 | bytes 5242880 | tf_op jit(solution)/shard_map/convert_element_type | solution.py:22
  28.2 3.0 %collective-permute-start = (bf16[2048,1,256]{0,2,1:T(8,128)(2,1)S(1)}, bf16[2048,1,256]{0,2,1:T(8,128)(2,1)}, u32[]{:S(2)}, u32[]{:S(2)}) collective-permute-start(bf16[2048,1,256]{0,2,1:T(8,128)(2,1)S(1)} %bitcast.59), channel_id=1, source_target_pairs={{0,2},{1,3},{2,0},{3,1},{4,6},{5,7},{6,4},{7,5},{8,10},{9,11},{10,... | collective-permute-start | bytes 3145736 | tf_op jit(solution)/shard_map/ppermute | solution.py:55
  31.2 4.4 %fusion.18 = (bf16[1024,128]{1,0:T(8,128)(2,1)}, f32[128]{0:T(128)S(1)}) fusion(f32[1024,128]{1,0:T(8,128)S(1)} %copy-done.10, f32[1024,128]{1,0:T(8,128)S(1)} %copy-done.11), kind=kLoop, calls=%fused_computation.41 | loop fusion | flops 10354560 | bytes 1311232 | tf_op jit(solution)/shard_map/convert_element_type | solution.py:22
  35.7 0.0 reduce-scatter.2.cloned.1.call-start
  36.4 0.8 iota_reduce_fusion
  37.2 0.1 broadcast_in_dim.49
  37.3 0.1 fusion.23
  37.4 0.1 broadcast_in_dim.47
  37.5 5.0 %gather_fusion = bf16[32,256,256]{2,1,0:T(8,128)(2,1)} fusion(bf16[32,256,256]{2,1,0:T(8,128)(2,1)} %bitcast.62, s32[1024]{0:T(1024)S(1)} %pad_clamp_fusion.1), kind=kCustom, calls=%fused_computation | custom fusion | bytes 8388736 | tf_op jit(solution)/shard_map/jit(_take)/gather | solution.py:34
  42.5 12.0 %collective-permute-done = bf16[2048,1,256]{0,2,1:T(8,128)(2,1)} collective-permute-done((bf16[2048,1,256]{0,2,1:T(8,128)(2,1)S(1)}, bf16[2048,1,256]{0,2,1:T(8,128)(2,1)}, u32[]{:S(2)}, u32[]{:S(2)}) %collective-permute-start) | collective-permute-done | bytes 1048608 | tf_op jit(solution)/shard_map/ppermute | solution.py:55
  54.5 1.4 select_bitcast_fusion.4
  55.9 1.5 maximum_bitcast_fusion
  57.4 1.4 copy-done
  58.8 3.7 %fusion.2 = bf16[8,4,256,256]{3,1,2,0:T(4,128)(2,1)S(1)} fusion(bf16[8,4,256,256]{3,2,1,0:T(8,128)(2,1)S(1)} %bitcast.57, pred[8,4]{1,0:T(8,128)(4,1)S(1)} %broadcast_in_dim.49, pred[8,4]{1,0:T(8,128)(4,1)S(1)} %broadcast_in_dim.47), kind=kLoop, calls=%fused_computation.9 | loop fusion | flops 4194304 | bytes 8388672 | tf_op jit(solution)/shard_map/jit(_where)/select_n | solution.py:35
  62.5 3.0 %copy.87 = bf16[256,8,4,256]{3,1,2,0:T(8,128)(2,1)} copy(bf16[256,8,4,256]{3,2,1,0:T(4,128)(2,1)S(1)} %bitcast.58) | data formatting | bytes 8388608
  65.5 2.6 %divide_reduce_fusion = f32[256]{0:T(256)S(1)} fusion(f32[2048,256]{1,0:T(8,128)} %param.10, f32[2048,256]{1,0:T(8,128)} %param.11), kind=kLoop, calls=%fused_computation.30 | loop fusion | flops 1048320 | bytes 4195328 | tf_op jit(solution)/shard_map/reduce_sum | solution.py:123
  68.2 1.9 select_bitcast_fusion.2
  70.1 0.4 pad_maximum_fusion
  70.5 2.3 %copy.77 = bf16[2048,2,2,256]{0,3,2,1:T(8,128)(2,1)} copy(bf16[2048,2,2,256]{0,3,1,2:T(8,128)(2,1)S(1)} %pad_maximum_fusion) | data formatting | bytes 8388608 | tf_op jit(solution)/shard_map/stack | solution.py:59
  72.8 13.6 %all-gather.2.cloned.1.call-done = bf16[1024,1024]{1,0:T(8,128)(2,1)} async-done(((bf16[1024,128]{1,0:T(8,128)(2,1)}), bf16[1024,1024]{1,0:T(8,128)(2,1)}) %all-gather.2.cloned.1.call-update) | async-done | bytes 2097168 | tf_op jit(solution)/shard_map/all_gather | solution.py:132
  86.4 9.4 %divide_convert_fusion = bf16[2048,1024]{1,0:T(8,128)(2,1)S(1)} fusion(bf16[2048,1024]{1,0:T(8,128)(2,1)} %bitcast.63, bf16[2048,1024]{0,1:T(8,128)(2,1)} %bitcast.64, bf16[1024,1024]{1,0:T(8,128)(2,1)} %all-gather.2.cloned.1.call-done), kind=kOutput, calls=%fused_computation.2 | convolution fusion | flops 4301258752 | bytes 14680064 | tf_op jit(solution)/shard_map/dot_general | solution.py:142
  95.8 1.9 copy-done.2
  97.7 6.1 %fusion.28 = f32[1024,1024]{1,0:T(8,128)} fusion(bf16[2048,1024]{1,0:T(8,128)(2,1)S(1)} %divide_convert_fusion, bf16[2048,1024]{0,1:T(8,128)(2,1)S(1)} %bitcast.65), kind=kOutput, calls=%fused_computation.73 | convolution fusion | flops 4294967296 | bytes 12582912 | tf_op jit(solution)/shard_map/dot_general | solution.py:146
  103.9 1.6 copy-done.4
  105.5 1.5 copy.92
  106.9 3.6 %gather_fusion.1 = bf16[4,1024,256]{2,1,0:T(8,128)(2,1)} fusion(bf16[1024,4,256]{2,0,1:T(8,128)(2,1)} %bitcast.61, s32[1024]{0:T(1024)S(1)} %pad_clamp_fusion), kind=kCustom, calls=%fused_computation.1 | custom fusion | bytes 4194320 | tf_op jit(solution)/shard_map/jit(_take)/gather | solution.py:77
  110.5 1.9 select_bitcast_fusion
  112.4 1.3 copy-done.6
  113.7 1.0 slice.33
  114.7 2.3 %copy.79 = bf16[1024,2,256]{0,2,1:T(8,128)(2,1)} copy(bf16[1024,2,256]{2,0,1:T(8,128)(2,1)} %slice.33) | data formatting | bytes 2097152 | tf_op jit(solution)/shard_map/slice | solution.py:87
  117.0 5.0 %fusion.27 = f32[2048,512]{0,1:T(8,128)S(1)} fusion(bf16[2048,1024]{1,0:T(8,128)(2,1)} %copy-done.2, bf16[1024,512]{0,1:T(8,128)(2,1)} %bitcast.66), kind=kOutput, calls=%fused_computation.72 | convolution fusion | flops 2147483648 | bytes 9437184 | tf_op jit(solution)/shard_map/dot_general | solution.py:88
  122.1 0.1 collective-permute-start.2
  122.2 0.5 collective-permute-start.4
  122.6 6.7 %collective-permute-done.4 = f32[2,1024]{1,0:T(2,128)S(1)} collective-permute-done((f32[2,1024]{1,0:T(2,128)S(1)}, f32[2,1024]{1,0:T(2,128)S(1)}, u32[]{:S(2)}, u32[]{:S(2)}) %collective-permute-start.4) | collective-permute-done | bytes 8224 | tf_op jit(solution)/shard_map/ppermute | solution.py:43
  129.3 1.5 collective-permute-start.5
  130.8 2.2 %collective-permute-done.5 = f32[2,1024]{1,0:T(2,128)S(1)} collective-permute-done((f32[2,1024]{1,0:T(2,128)S(1)}, f32[2,1024]{1,0:T(2,128)S(1)}, u32[]{:S(2)}, u32[]{:S(2)}) %collective-permute-start.5) | collective-permute-done | bytes 8224 | tf_op jit(solution)/shard_map/ppermute | solution.py:43
  133.0 1.5 collective-permute-start.6
  134.4 2.2 %collective-permute-done.6 = f32[2,1024]{1,0:T(2,128)S(1)} collective-permute-done((f32[2,1024]{1,0:T(2,128)S(1)}, f32[2,1024]{1,0:T(2,128)S(1)}, u32[]{:S(2)}, u32[]{:S(2)}) %collective-permute-start.6) | collective-permute-done | bytes 8224 | tf_op jit(solution)/shard_map/ppermute | solution.py:43
  136.6 0.1 collective-permute-start.7
  136.7 1.3 slice_add_fusion
  138.1 1.5 collective-permute-start.3
  139.6 1.4 collective-permute-done.7
  141.0 1.2 collective-permute-start.8
  142.2 1.3 fusion.20
  143.5 2.2 %collective-permute-done.8 = f32[2,1024]{1,0:T(2,128)S(1)} collective-permute-done((f32[2,1024]{1,0:T(2,128)S(1)}, f32[2,1024]{1,0:T(2,128)S(1)}, u32[]{:S(2)}, u32[]{:S(2)}) %collective-permute-start.8) | collective-permute-done | bytes 8224 | tf_op jit(solution)/shard_map/ppermute | solution.py:43
  145.7 1.9 fusion.3
  147.6 1.6 collective-permute-start.11
  149.2 2.1 %collective-permute-done.11 = f32[1024]{0:T(1024)S(1)} collective-permute-done((f32[1024]{0:T(1024)S(1)}, f32[1024]{0:T(1024)S(1)}, u32[]{:S(2)}, u32[]{:S(2)}) %collective-permute-start.11) | collective-permute-done | bytes 4128 | tf_op jit(solution)/shard_map/ppermute | solution.py:43
  151.3 0.9 collective-permute-start.12
  152.1 2.7 %collective-permute-done.12 = f32[1024]{0:T(1024)S(1)} collective-permute-done((f32[1024]{0:T(1024)S(1)}, f32[1024]{0:T(1024)S(1)}, u32[]{:S(2)}, u32[]{:S(2)}) %collective-permute-start.12) | collective-permute-done | bytes 4128 | tf_op jit(solution)/shard_map/ppermute | solution.py:43
  154.9 1.2 collective-permute-start.13
  156.0 28.3 %collective-permute-done.3 = f32[2048,256]{0,1:T(8,128)S(1)} collective-permute-done((f32[2048,256]{0,1:T(8,128)S(1)}, f32[2048,256]{0,1:T(8,128)S(1)}, u32[]{:S(2)}, u32[]{:S(2)}) %collective-permute-start.3) | collective-permute-done | bytes 2097184 | tf_op jit(solution)/shard_map/ppermute | solution.py:93
  184.3 2.3 %fusion.12 = (f32[2048]{0:T(1024)S(1)}, f32[2048,256]{0,1:T(8,128)}, f32[2048,256]{0,1:T(8,128)S(1)}) fusion(f32[256]{0:T(256)S(1)} %bitcast.68, f32[2048]{0:T(1024)S(1)} %broadcast_divide_fusion, f32[2048,256]{0,1:T(8,128)S(1)} %collective-permute-done.3, f32[2048,256]{0,1:T(8,128)S(1)} %fusion.20, f32[2048,512]{0,1:T(8,128)S(1)} %collective-permute-done.2, ...), kind=kLoop, calls=%fused_computation.31 | loop fusion | flops 4192256 | bytes 11551744 | tf_op jit(solution)/shard_map/reduce_sum | solution.py:154
  186.6 1.0 add_log_fusion.1
  187.6 0.2 collective-permute-done.9
  187.8 1.5 collective-permute-start.10
  189.3 0.6 add_add_fusion.1
  189.9 2.9 %copy.82 = f32[2048,256]{1,0:T(8,128)} copy(f32[2048,256]{0,1:T(8,128)} %get-tuple-element.41) | data formatting | bytes 4194304
  192.8 1.8 copy.83
  194.6 0.6 add_add_fusion
  195.2 1.9 multiply_add_fusion
  (61 shorter events, 0.3 us)
Async XLA Ops:
  7.2 3.1 %copy-start.5 = (f32[2048,256]{1,0:T(8,128)S(1)}, f32[2048,256]{1,0:T(8,128)}, u32[]{:S(2)}) copy-start(f32[2048,256]{1,0:T(8,128)} %param.11) | copy-start | bytes 6291460
  7.2 79.2 %all-gather.2.cloned.1.call-start = ((), (), s32[]{:S(2)}) async-start(), calls=%async_computation.1 | async-start | bytes 2359296 | tf_op jit(solution)/shard_map/all_gather | solution.py:132
  12.1 19.2 %copy-start.10 = (f32[1024,128]{1,0:T(8,128)S(1)}, f32[1024,128]{1,0:T(8,128)}, u32[]{:S(2)}) copy-start(f32[1024,128]{1,0:T(8,128)} %param.14) | copy-start | bytes 1572868
  12.1 19.2 %copy-start.11 = (f32[1024,128]{1,0:T(8,128)S(1)}, f32[1024,128]{1,0:T(8,128)}, u32[]{:S(2)}) copy-start(f32[1024,128]{1,0:T(8,128)} %param.13) | copy-start | bytes 1572868
  12.1 24.3 %copy-start.14 = (s32[1,1,32]{2,1,0:T(1,128)S(1)}, s32[1,1,32]{2,1,0:T(1,128)}, u32[]{:S(2)}) copy-start(s32[1,1,32]{2,1,0:T(1,128)} %param.16) | copy-start | bytes 388
  28.2 26.3 %collective-permute-start = (bf16[2048,1,256]{0,2,1:T(8,128)(2,1)S(1)}, bf16[2048,1,256]{0,2,1:T(8,128)(2,1)}, u32[]{:S(2)}, u32[]{:S(2)}) collective-permute-start(bf16[2048,1,256]{0,2,1:T(8,128)(2,1)S(1)} %bitcast.59), channel_id=1, source_target_pairs={{0,2},{1,3},{2,0},{3,1},{4,6},{5,7},{6,4},{7,5},{8,10},{9,11},{10,... | collective-permute-start | bytes 3145736 | tf_op jit(solution)/shard_map/ppermute | solution.py:55
  35.7 159.5 %reduce-scatter.2.cloned.1.call-start = ((), (), s32[]{:S(2)}) async-start(), calls=%async_computation.2 | async-start | bytes 4718592 | tf_op jit(solution)/shard_map/reduce_scatter | solution.py:156
  55.8 3.0 %copy-start = (bf16[32,256,256]{2,1,0:T(8,128)(2,1)S(1)}, bf16[32,256,256]{2,1,0:T(8,128)(2,1)}, u32[]{:S(2)}) copy-start(bf16[32,256,256]{2,1,0:T(8,128)(2,1)} %gather_fusion) | copy-start | bytes 12582916
  57.4 10.9 %collective-permute-start.1 = (bf16[2048,2,256]{0,2,1:T(8,128)(2,1)}, bf16[2048,2,256]{0,2,1:T(8,128)(2,1)}, u32[]{:S(2)}, u32[]{:S(2)}) collective-permute-start(bf16[2048,2,256]{0,2,1:T(8,128)(2,1)} %maximum_bitcast_fusion), channel_id=1, source_target_pairs={{0,1},{1,0},{2,3},{3,2},{4,5},{5,4},{6,7},{7,6},{8,9},{9,8},{10,11... | collective-permute-start | bytes 6291464 | tf_op jit(solution)/shard_map/ppermute | solution.py:55
  65.5 2.6 %copy-start.15 = (s32[4]{0:T(128)S(1)}, s32[4]{0:T(128)}, u32[]{:S(2)}) copy-start(s32[4]{0:T(128)} %constant.85.clone) | copy-start | bytes 52
  86.4 11.3 %copy-start.8 = (bf16[2048,2,2,256]{0,3,2,1:T(8,128)(2,1)S(1)}, bf16[2048,2,2,256]{0,3,2,1:T(8,128)(2,1)}, u32[]{:S(2)}) copy-start(bf16[2048,2,2,256]{0,3,2,1:T(8,128)(2,1)} %copy.77) | copy-start | bytes 12582916
  95.8 2.0 copy-start.2
  103.9 1.6 copy-start.4
  112.4 1.3 copy-start.6
  117.0 17.4 %copy-start.12 = (f32[2048]{0:T(1024)S(1)}, f32[2048]{0:T(1024)}, u32[]{:S(2)}) copy-start(f32[2048]{0:T(1024)} %param.12) | copy-start | bytes 24580
  117.0 19.7 %copy-start.3 = (bf16[2048,1024]{1,0:T(8,128)(2,1)S(1)}, bf16[2048,1024]{1,0:T(8,128)(2,1)}, u32[]{:S(2)}) copy-start(bf16[2048,1024]{1,0:T(8,128)(2,1)} %copy-done.2) | copy-start | bytes 12582916
  117.0 19.7 %copy-start.7 = (bf16[1024,4,256]{2,0,1:T(8,128)(2,1)S(1)}, bf16[1024,4,256]{2,0,1:T(8,128)(2,1)}, u32[]{:S(2)}) copy-start(bf16[1024,4,256]{2,0,1:T(8,128)(2,1)} %copy-done.6) | copy-start | bytes 6291460
  122.1 14.6 %collective-permute-start.2 = (f32[2048,512]{0,1:T(8,128)S(1)}, f32[2048,512]{0,1:T(8,128)S(1)}, u32[]{:S(2)}, u32[]{:S(2)}) collective-permute-start(f32[2048,512]{0,1:T(8,128)S(1)} %fusion.27), channel_id=1, source_target_pairs={{0,1},{1,0},{2,3},{3,2},{4,5},{5,4},{6,7},{7,6},{8,9},{9,8},{10,11... | collective-permute-start | bytes 12582920 | tf_op jit(solution)/shard_map/ppermute | solution.py:93
  122.2 7.2 %collective-permute-start.4 = (f32[2,1024]{1,0:T(2,128)S(1)}, f32[2,1024]{1,0:T(2,128)S(1)}, u32[]{:S(2)}, u32[]{:S(2)}) collective-permute-start(f32[2,1024]{1,0:T(2,128)S(1)} %pad_maximum_fusion.1), channel_id=1, source_target_pairs={{0,1},{1,0},{2,3},{3,2},{4,5},{5,4},{6,7},{7,6},{8,9},{9,8},{10,11... | collective-permute-start | bytes 24584 | tf_op jit(solution)/shard_map/ppermute | solution.py:43
  129.3 3.7 %collective-permute-start.5 = (f32[2,1024]{1,0:T(2,128)S(1)}, f32[2,1024]{1,0:T(2,128)S(1)}, u32[]{:S(2)}, u32[]{:S(2)}) collective-permute-start(f32[2,1024]{1,0:T(2,128)S(1)} %add.146), channel_id=1, source_target_pairs={{0,2},{1,3},{2,0},{3,1},{4,6},{5,7},{6,4},{7,5},{8,10},{9,11},{10,... | collective-permute-start | bytes 24584 | tf_op jit(solution)/shard_map/ppermute | solution.py:43
  133.0 3.7 %collective-permute-start.6 = (f32[2,1024]{1,0:T(2,128)S(1)}, f32[2,1024]{1,0:T(2,128)S(1)}, u32[]{:S(2)}, u32[]{:S(2)}) collective-permute-start(f32[2,1024]{1,0:T(2,128)S(1)} %add.147), channel_id=1, source_target_pairs={{0,4},{4,0},{8,12},{12,8},{16,20},{20,16},{24,28},{28,24},{1,5},{5... | collective-permute-start | bytes 24584 | tf_op jit(solution)/shard_map/ppermute | solution.py:43
  136.6 3.0 %copy-start.13 = (f32[1024]{0:T(1024)S(1)}, f32[1024]{0:T(1024)}, u32[]{:S(2)}) copy-start(f32[1024]{0:T(1024)} %param.15) | copy-start | bytes 12292
  136.6 4.4 %collective-permute-start.7 = (f32[2,1024]{1,0:T(2,128)S(1)}, f32[2,1024]{1,0:T(2,128)S(1)}, u32[]{:S(2)}, u32[]{:S(2)}) collective-permute-start(f32[2,1024]{1,0:T(2,128)S(1)} %add.148), channel_id=1, source_target_pairs={{0,8},{4,12},{8,0},{12,4},{16,24},{20,28},{24,16},{28,20},{1,9},{5... | collective-permute-start | bytes 24584 | tf_op jit(solution)/shard_map/ppermute | solution.py:43
  138.1 46.2 %collective-permute-start.3 = (f32[2048,256]{0,1:T(8,128)S(1)}, f32[2048,256]{0,1:T(8,128)S(1)}, u32[]{:S(2)}, u32[]{:S(2)}) collective-permute-start(f32[2048,256]{0,1:T(8,128)S(1)} %slice_add_fusion), channel_id=1, source_target_pairs={{0,2},{1,3},{2,0},{3,1},{4,6},{5,7},{6,4},{7,5},{8,10},{9,11},{10,... | collective-permute-start | bytes 6291464 | tf_op jit(solution)/shard_map/ppermute | solution.py:93
  141.0 4.7 %collective-permute-start.8 = (f32[2,1024]{1,0:T(2,128)S(1)}, f32[2,1024]{1,0:T(2,128)S(1)}, u32[]{:S(2)}, u32[]{:S(2)}) collective-permute-start(f32[2,1024]{1,0:T(2,128)S(1)} %add.149), channel_id=1, source_target_pairs={{0,16},{4,20},{8,24},{12,28},{16,0},{20,4},{24,8},{28,12},{1,17},{... | collective-permute-start | bytes 24584 | tf_op jit(solution)/shard_map/ppermute | solution.py:43
  142.2 3.5 %copy-start.1 = (f32[1024,1024]{1,0:T(8,128)S(1)}, f32[1024,1024]{1,0:T(8,128)}, u32[]{:S(2)}) copy-start(f32[1024,1024]{1,0:T(8,128)} %fusion.28) | copy-start | bytes 12582916
  147.6 3.7 %collective-permute-start.11 = (f32[1024]{0:T(1024)S(1)}, f32[1024]{0:T(1024)S(1)}, u32[]{:S(2)}, u32[]{:S(2)}) collective-permute-start(f32[1024]{0:T(1024)S(1)} %get-tuple-element.38), channel_id=1, source_target_pairs={{0,4},{4,0},{8,12},{12,8},{16,20},{20,16},{24,28},{28,24},{1,5},{5... | collective-permute-start | bytes 12296 | tf_op jit(solution)/shard_map/ppermute | solution.py:43
  151.3 3.6 %collective-permute-start.12 = (f32[1024]{0:T(1024)S(1)}, f32[1024]{0:T(1024)S(1)}, u32[]{:S(2)}, u32[]{:S(2)}) collective-permute-start(f32[1024]{0:T(1024)S(1)} %add.168), channel_id=1, source_target_pairs={{0,8},{4,12},{8,0},{12,4},{16,24},{20,28},{24,16},{28,20},{1,9},{5... | collective-permute-start | bytes 12296 | tf_op jit(solution)/shard_map/ppermute | solution.py:43
  154.9 34.4 %collective-permute-start.13 = (f32[1024]{0:T(1024)S(1)}, f32[1024]{0:T(1024)S(1)}, u32[]{:S(2)}, u32[]{:S(2)}) collective-permute-start(f32[1024]{0:T(1024)S(1)} %add.169), channel_id=1, source_target_pairs={{0,16},{4,20},{8,24},{12,28},{16,0},{20,4},{24,8},{28,12},{1,17},{... | collective-permute-start | bytes 12296 | tf_op jit(solution)/shard_map/ppermute | solution.py:43
  186.6 1.2 collective-permute-start.9
  187.8 6.8 %collective-permute-start.10 = (f32[2048]{0:T(1024)S(1)}, f32[2048]{0:T(1024)S(1)}, u32[]{:S(2)}, u32[]{:S(2)}) collective-permute-start(f32[2048]{0:T(1024)S(1)} %add.154), channel_id=1, source_target_pairs={{0,2},{1,3},{2,0},{3,1},{4,6},{5,7},{6,4},{7,5},{8,10},{9,11},{10,... | collective-permute-start | bytes 24584 | tf_op jit(solution)/shard_map/ppermute | solution.py:43
  192.8 2.4 %copy-start.9 = (bf16[1024,128]{1,0:T(8,128)(2,1)S(1)}, bf16[1024,128]{1,0:T(8,128)(2,1)}, u32[]{:S(2)}) copy-start(bf16[1024,128]{1,0:T(8,128)(2,1)} %get-tuple-element.48) | copy-start | bytes 786436
Sparse Core Ops, SparseCore 0:
  35.8 50.5 all-gather.1
  104.0 87.2 reduce-scatter.1
